TPU v7x, 32 devices: a whole 2x2x4 slice. The times are simulated.
32 devices in a mesh: grp: 2 (over x), seq: 16 (over z, y, core).
Axes of the slice: x: 2, y: 2, z: 4, core: 2. Of those that a mesh axis runs over, the one named last changes fastest.
Arguments:
- scalars: bfloat16 [256, 4096], P(None, ('grp', 'seq')), parts along dimension 1, may hold values from -6 to 6
- vectors: bfloat16 [3, 256, 4096], P(None, None, ('grp', 'seq')), parts along dimension 2, may hold values from -6 to 6
- w_qkw_s: bfloat16 [2, 768, 256], replicated, may hold values from -0.375 to 0.375
- w_qkw_v: bfloat16 [2, 768, 256], replicated, may hold values from -0.375 to 0.375
- w_out_s: bfloat16 [2, 256, 256], replicated, may hold values from -0.375 to 0.375
- w_out_v: bfloat16 [2, 256, 256], replicated, may hold values from -0.375 to 0.375
- w_up: bfloat16 [2, 1024, 256], replicated, may hold values from -0.375 to 0.375
- w_down: bfloat16 [2, 256, 1024], replicated, may hold values from -0.1875 to 0.1875
- w_mix: bfloat16 [2, 256, 256], replicated, may hold values from -0.375 to 0.375
- w_gate: bfloat16 [2, 256, 256], replicated, may hold values from -0.375 to 0.375
- gains: float32 [2, 4, 256], replicated, may hold values from 0.5 to 1.5
- pe_w1: float32 [2, 64, 16], replicated, may hold values from -24 to 24
- pe_w2: float32 [2, 64, 64], replicated, may hold values from -0.75 to 0.75
- pe_w3: float32 [2, 256, 64], replicated, may hold values from -1.5 to 1.5
- rates: float32 [2, 256], replicated, may hold values from 0.05 to 40
Outputs:
- scalars_out: bfloat16 [256, 4096], P(None, ('grp', 'seq')), parts along dimension 1
- vectors_out: bfloat16 [3, 256, 4096], P(None, None, ('grp', 'seq')), parts along dimension 2
There are 2 independent parts, one for each index of `grp`. A program takes and returns all parts, laid end to end along the dimension named above; an argument that names none is the same for every part. Nothing has to cross between parts.
All inputs are finite; a program needn't handle non-finite values.
Results may differ from a plain program's by a relative error of at most 0.02.
Values may be sent and summed in bfloat16 or wider, within the bound.
No kernel may reach another device: no remote copies, remote signals or barrier semaphores. Data moves between devices by JAX's collectives and lax.ppermute only.
A program may use at most 64 MiB of HBM per device.

v0:
```python
import math

import jax
import jax.numpy as jnp
import numpy as np
from jax import lax
from jax.sharding import PartitionSpec as P

HIGH = lax.Precision.HIGHEST


def filter_values(positions, length, first, second, third, decay):
    count = first.shape[1] // 2
    freqs = jnp.arange(1, count + 1, dtype=jnp.int32)
    turns = freqs[:, None] * positions[None, :] % length
    angle = turns.astype(jnp.float32) * (2.0 * math.pi / length)
    feats = jnp.concatenate([jnp.cos(angle), jnp.sin(angle)], axis=0)
    hid_one = jnp.sin(jnp.dot(first, feats, precision=HIGH))
    hid_two = jnp.sin(jnp.dot(second, hid_one, precision=HIGH))
    raw = jnp.dot(third, hid_two, precision=HIGH)
    envelope = jnp.exp(-decay[:, None] * positions[None, :].astype(jnp.float32) / length)
    return (raw * envelope / math.sqrt(length)).astype(jnp.bfloat16)


def scalar_norm(field, gain):
    return field * lax.rsqrt(jnp.mean(field * field, axis=0, keepdims=True) + 1e-05) * gain[:, None]


def vector_norm(field, gain):
    return (
        field
        * lax.rsqrt(jnp.mean(field * field, axis=(0, 1), keepdims=True) + 1e-05)
        * gain[None, :, None]
    )


def make_tables(shards, local):
    length = shards * local
    a = np.arange(shards)
    ang_s = 2.0 * np.pi * np.outer(a, a) / shards
    lead_fwd = np.concatenate([np.cos(ang_s), -np.sin(ang_s)], axis=0)
    lead_inv = np.concatenate([np.cos(ang_s), -np.sin(ang_s)], axis=1)
    b = np.arange(local)
    ang_t = 2.0 * np.pi * np.outer(a, b) / length
    tw_c = np.cos(ang_t)[:, None, None, :]
    tw_s = np.sin(ang_t)[:, None, None, :]
    ang_l = 2.0 * np.pi * np.outer(b, b) / local
    cos_l, sin_l = np.cos(ang_l), np.sin(ang_l)
    lane_fwd = np.block([[cos_l, -sin_l], [sin_l, cos_l]])
    lane_inv = np.block([[cos_l, sin_l], [-sin_l, cos_l]])
    f32 = lambda v: jnp.asarray(v, dtype=jnp.float32)
    return tuple(f32(v) for v in (lead_fwd, lead_inv, tw_c, tw_s, lane_fwd, lane_inv))


def forward_dft(field, tables):
    lead_fwd, _, tw_c, tw_s, lane_fwd, _ = tables
    shards = field.shape[0]
    stage = jnp.einsum("ka,apcb->kpcb", lead_fwd, field, precision=HIGH)
    st_r, st_i = stage[:shards], stage[shards:]
    tw_r = st_r * tw_c + st_i * tw_s
    tw_i = st_i * tw_c - st_r * tw_s
    joined = jnp.concatenate([tw_r, tw_i], axis=-1)
    return jnp.einsum("kpcb,bm->kpcm", joined, lane_fwd, precision=HIGH)


def inverse_dft(spec, tables):
    _, lead_inv, tw_c, tw_s, _, lane_inv = tables
    local = spec.shape[-1] // 2
    back = jnp.einsum("kpcm,mb->kpcb", spec, lane_inv, precision=HIGH)
    bk_r, bk_i = back[..., :local], back[..., local:]
    un_r = bk_r * tw_c - bk_i * tw_s
    un_i = bk_r * tw_s + bk_i * tw_c
    stacked = jnp.concatenate([un_r, un_i], axis=0)
    return jnp.einsum("ak,kpcb->apcb", lead_inv, stacked, precision=HIGH)


def cmul(a_r, a_i, b_r, b_i):
    return a_r * b_r - a_i * b_i, a_r * b_i + a_i * b_r


def convolve(received, filt_spec, tables):
    shards, _, chans, local = received.shape
    length = shards * local
    spec = forward_dft(received.astype(jnp.float32), tables)
    re, im = spec[..., :local], spec[..., local:]
    h_r, h_i = filt_spec[..., :local], filt_spec[..., local:]
    p_r, p_i = cmul(re[:, 0], im[:, 0], h_r, h_i)
    outs_r, outs_i = [p_r], [p_i]
    for j in range(3):
        one, two = (j + 1) % 3, (j + 2) % 3
        a_r, a_i = cmul(re[:, 1 + one], im[:, 1 + one], re[:, 4 + two], im[:, 4 + two])
        b_r, b_i = cmul(re[:, 1 + two], im[:, 1 + two], re[:, 4 + one], im[:, 4 + one])
        outs_r.append(a_r - b_r)
        outs_i.append(a_i - b_i)
    prod = jnp.concatenate([jnp.stack(outs_r, axis=1), jnp.stack(outs_i, axis=1)], axis=-1)
    result = inverse_dft(prod, tables)
    inv_root = 1.0 / math.sqrt(length)
    scale = jnp.array([1.0, inv_root, inv_root, inv_root], dtype=jnp.float32) / length
    return (result * scale[None, :, None, None]).astype(jnp.bfloat16)


def per_device(
    scalars,
    vectors,
    w_qkw_s,
    w_qkw_v,
    w_out_s,
    w_out_v,
    w_up,
    w_down,
    w_mix,
    w_gate,
    gains,
    pe_w1,
    pe_w2,
    pe_w3,
    rates,
):
    chans = scalars.shape[0]
    tok_local = scalars.shape[1]
    shards = lax.axis_size("seq")
    rank = lax.axis_index("seq")
    length = tok_local * shards
    own = chans // shards
    depth = w_qkw_s.shape[0]
    tables = make_tables(shards, tok_local)
    positions = jnp.arange(length, dtype=jnp.int32)
    filt = []
    for layer in range(depth):
        third = lax.dynamic_slice_in_dim(pe_w3[layer], rank * own, own, axis=0)
        decay = lax.dynamic_slice_in_dim(rates[layer], rank * own, own, axis=0)
        made = filter_values(positions, length, pe_w1[layer], pe_w2[layer], third, decay)
        filt.append(made.reshape(own, shards, tok_local).transpose(1, 0, 2))
    filt = jnp.stack(filt, axis=1).astype(jnp.float32)
    filt_spec = forward_dft(filt, tables)
    state_s = scalars.astype(jnp.float32)
    state_v = vectors.astype(jnp.float32)
    for layer in range(depth):
        normed_s = scalar_norm(state_s, gains[layer, 0]).astype(jnp.bfloat16)
        normed_v = vector_norm(state_v, gains[layer, 1]).astype(jnp.bfloat16)
        proj_s = jnp.dot(w_qkw_s[layer], normed_s, preferred_element_type=jnp.float32)
        query_s = proj_s[:chans].astype(jnp.bfloat16)
        signal_s = (proj_s[chans : 2 * chans] * proj_s[2 * chans :]).astype(jnp.bfloat16)
        proj_v = jnp.einsum(
            "oc,jct->jot", w_qkw_v[layer], normed_v, preferred_element_type=jnp.float32
        ).astype(jnp.bfloat16)
        query_v = proj_v[:, :chans]
        key_v = proj_v[:, chans : 2 * chans].reshape(3, shards, own, tok_local)
        val_v = proj_v[:, 2 * chans :].reshape(3, shards, own, tok_local)
        outgoing = jnp.concatenate(
            [
                signal_s.reshape(shards, 1, own, tok_local),
                key_v.transpose(1, 0, 2, 3),
                val_v.transpose(1, 0, 2, 3),
            ],
            axis=1,
        )
        regrouped = lax.all_to_all(outgoing, "seq", 0, 0, tiled=True)
        convolved = convolve(regrouped, filt_spec[:, layer], tables)
        returned = lax.all_to_all(convolved, "seq", 0, 0, tiled=True)
        conv_s = returned[:, 0].reshape(chans, tok_local).astype(jnp.float32)
        conv_v = returned[:, 1:].transpose(1, 0, 2, 3).reshape(3, chans, tok_local)
        conv_v = conv_v.astype(jnp.float32)
        qs_f = query_s.astype(jnp.float32)
        out_s = (qs_f * conv_s + jnp.sum(query_v.astype(jnp.float32) * conv_v, axis=0)).astype(
            jnp.bfloat16
        )
        out_v = (qs_f[None] * conv_v).astype(jnp.bfloat16)
        state_s = state_s + jnp.dot(w_out_s[layer], out_s, preferred_element_type=jnp.float32)
        state_v = state_v + jnp.einsum(
            "oc,jct->jot", w_out_v[layer], out_v, preferred_element_type=jnp.float32
        )
        mlp_s = scalar_norm(state_s, gains[layer, 2]).astype(jnp.bfloat16)
        mlp_v = vector_norm(state_v, gains[layer, 3]).astype(jnp.bfloat16)
        hidden = jax.nn.gelu(
            jnp.dot(w_up[layer], mlp_s, preferred_element_type=jnp.float32)
        ).astype(jnp.bfloat16)
        gate = jax.nn.sigmoid(jnp.dot(w_gate[layer], mlp_s, preferred_element_type=jnp.float32))
        state_s = state_s + jnp.dot(w_down[layer], hidden, preferred_element_type=jnp.float32)
        state_v = (
            state_v
            + jnp.einsum("oc,jct->jot", w_mix[layer], mlp_v, preferred_element_type=jnp.float32)
            * gate[None]
        )
    return (state_s.astype(jnp.bfloat16), state_v.astype(jnp.bfloat16))


def solution(mesh):
    in_specs = (
        P(None, ("grp", "seq")),
        P(None, None, ("grp", "seq")),
        P(),
        P(),
        P(),
        P(),
        P(),
        P(),
        P(),
        P(),
        P(),
        P(),
        P(),
        P(),
        P(),
    )
    out_specs = (P(None, ("grp", "seq")), P(None, None, ("grp", "seq")))
    return jax.shard_map(
        per_device, mesh=mesh, in_specs=in_specs, out_specs=out_specs, check_vma=False
    )
```

profile of v0, /device:TPU:0, one launch (start us, length us, event | category | flops | bytes accessed | tf_op | source)
XLA Modules:
  0.0 100.9 jit_solution(6750692452291250835)
XLA Ops:
  0.7 1.1 %copy.121 = bf16[3,256,128]{1,2,0:T(8,128)(2,1)S(1)} copy(bf16[3,256,128]{2,1,0:T(8,128)(2,1)} %param.24) | data formatting | bytes 393216 | tf_op args[1]
  1.8 1.5 %fusion.205 = (f32[1,1,256]{2,1,0:T(1,128)}, f32[1,1,256]{2,1,0:T(1,128)}, f32[1,1,256]{2,1,0:T(1,128)}, f32[1,1,256]{2,1,0:T(1,128)}, f32[1,1,256]{2,1,0:T(1,12...) fusion(f32[2,4,256]{2,1,0:T(4,128)} %param.33), kind=kLoop, calls=%fused_computation.305 | loop fusion | bytes 16384 | tf_op jit(solution)/shard_map/slice | solution.py:174
  3.4 1.4 %fusion.8 = bf16[3,768,128]{1,2,0:T(8,128)(2,1)S(1)} fusion(bf16[2,768,256]{2,1,0:T(8,128)(2,1)} %param.26, bf16[3,256,128]{1,2,0:T(8,128)(2,1)S(1)} %copy.121, f32[256]{0:T(256)S(1)} %bitcast.314, f32[128]{0:T(128)S(1)} %add_rsqrt_fusion.6), kind=kOutput, calls=%fused_computation.18 | convolution fusion | flops 151683072 | bytes 1181184 | tf_op jit(solution)/shard_map/oc,jct->jot/dot_general | solution.py:144
  5.4 0.3 convolution_bitcast_fusion.7
  5.9 0.8 copy.124
  6.7 7.4 %all-to-all-start = ((bf16[16,7,16,128]{3,2,1,0:T(8,128)(2,1)}), bf16[16,7,16,128]{3,2,1,0:T(8,128)(2,1)S(1)}, u32[]{:S(2)}, u32[]{:S(2)}) async-start(bf16[16,7,16,128]{3,2,1,0:T(8,128)(2,1)} %copy.124), calls=%async_computation | async-start | bytes 917504 | tf_op jit(solution)/shard_map/all_to_all | solution.py:158
  14.2 0.3 fusion.176
  14.5 2.3 %convolution_sine_fusion.1 = f32[2048,64]{0,1:T(8,128)S(1)} fusion(f32[8,2048]{1,0:T(8,128)S(1)} %get-tuple-element.53, f32[8,2048]{1,0:T(8,128)S(1)} %get-tuple-element.52, f32[2,64,16]{1,2,0:T(8,128)S(1)} %copy-done.19), kind=kOutput, calls=%fused_computation.1 | convolution fusion | flops 25198592 | bytes 663552 | tf_op jit(solution)/shard_map/dot_general | solution.py:18
  16.8 2.3 %convolution_sine_fusion.3 = f32[2048,64]{0,1:T(8,128)S(1)} fusion(f32[8,2048]{1,0:T(8,128)S(1)} %get-tuple-element.53, f32[8,2048]{1,0:T(8,128)S(1)} %get-tuple-element.52, f32[2,64,16]{1,2,0:T(8,128)S(1)} %copy-done.19), kind=kOutput, calls=%fused_computation.3 | convolution fusion | flops 25198592 | bytes 663552 | tf_op jit(solution)/shard_map/dot_general | solution.py:18
  19.1 2.3 %convolution_sine_fusion = f32[2048,64]{0,1:T(8,128)S(1)} fusion(f32[2048,64]{0,1:T(8,128)S(1)} %convolution_sine_fusion.1, f32[2,64,64]{2,1,0:T(8,128)S(1)} %copy-done.15), kind=kOutput, calls=%fused_computation | convolution fusion | flops 100663296 | bytes 1081344 | tf_op jit(solution)/shard_map/dot_general | solution.py:19
  21.5 0.5 fusion.34
  22.0 2.3 %convolution_sine_fusion.2 = f32[2048,64]{0,1:T(8,128)S(1)} fusion(f32[2048,64]{0,1:T(8,128)S(1)} %convolution_sine_fusion.3, f32[2,64,64]{2,1,0:T(8,128)S(1)} %copy-done.15), kind=kOutput, calls=%fused_computation.2 | convolution fusion | flops 100663296 | bytes 1081344 | tf_op jit(solution)/shard_map/dot_general | solution.py:19
  24.3 0.5 fusion.35
  24.8 0.4 fusion.123
  25.3 0.8 fusion.78
  26.2 1.2 %all-to-all-done = bf16[16,7,16,128]{3,2,1,0:T(8,128)(2,1)S(1)} async-done(((bf16[16,7,16,128]{3,2,1,0:T(8,128)(2,1)}), bf16[16,7,16,128]{3,2,1,0:T(8,128)(2,1)S(1)}, u32[]{:S(2)}, u32[]{:S(2)}) %all-to-all-start) | async-done | bytes 458784 | tf_op jit(solution)/shard_map/all_to_all | solution.py:158
  27.4 1.1 %fusion.88 = f32[32,7,16,128]{3,0,2,1:T(8,128)S(1)} fusion(f32[32,16,1,1]{0,1,3,2:T(8,128)S(1)} %copy-done.13, bf16[16,7,16,128]{3,2,1,0:T(8,128)(2,1)S(1)} %all-to-all-done), kind=kOutput, calls=%fused_computation.128 | convolution fusion | flops 88080384 | bytes 2295808 | tf_op jit(solution)/shard_map/ka,apcb->kpcb/dot_general | solution.py:58
  28.9 2.5 %fusion.6 = f32[16,7,16,256]{3,2,1,0:T(8,128)S(1)} fusion(f32[256,256,1,1]{1,0,3,2:T(8,128)S(1)} %copy-done, f32[16,7,16,256]{3,0,2,1:T(8,128)S(1)} %pad_maximum_fusion), kind=kOutput, calls=%fused_computation.14 | convolution fusion | flops 1409286144 | bytes 3932160 | tf_op jit(solution)/shard_map/kpcb,bm->kpcm/dot_general | solution.py:63
  31.8 0.7 copy-done.32
  32.5 1.0 fusion.36
  33.8 0.4 copy-done.17
  34.2 1.3 %fusion.20 = bf16[16,4,16,128]{3,0,2,1:T(8,128)(2,1)S(1)} fusion(f32[16,32,1,1]{1,0,3,2:T(8,128)S(1)} %copy-done.17, f32[32,4,16,128]{3,2,1,0:T(8,128)S(1)} %pad_maximum_fusion.2, f32[4]{0:T(128)S(1)} %copy-done.24), kind=kOutput, calls=%fused_computation.40 | convolution fusion | flops 50593792 | bytes 1312784 | tf_op jit(solution)/shard_map/ak,kpcb->apcb/dot_general | solution.py:74
  35.5 0.8 copy.133
  36.2 5.0 %all-to-all-start.1 = ((bf16[16,4,16,128]{3,2,1,0:T(8,128)(2,1)}), bf16[16,4,16,128]{3,2,1,0:T(8,128)(2,1)S(1)}, u32[]{:S(2)}, u32[]{:S(2)}) async-start(bf16[16,4,16,128]{3,2,1,0:T(8,128)(2,1)} %copy.133), calls=%async_computation.1 | async-start | bytes 524288 | tf_op jit(solution)/shard_map/all_to_all | solution.py:160
  41.4 9.9 %all-to-all-done.1 = bf16[16,4,16,128]{3,2,1,0:T(8,128)(2,1)S(1)} async-done(((bf16[16,4,16,128]{3,2,1,0:T(8,128)(2,1)}), bf16[16,4,16,128]{3,2,1,0:T(8,128)(2,1)S(1)}, u32[]{:S(2)}, u32[]{:S(2)}) %all-to-all-start.1) | async-done | bytes 262176 | tf_op jit(solution)/shard_map/all_to_all | solution.py:160
  51.8 0.3 multiply_reduce_fusion.7
  52.1 0.3 multiply_reduce_fusion.3
  52.8 0.4 multiply_reduce_fusion.2
  53.2 0.4 fusion.9
  54.0 1.9 %multiply_reduce_fusion.6 = (f32[128]{0:T(128)S(1)}, f32[256,128]{0,1:T(8,128)S(1)}) fusion(f32[256,128]{0,1:T(8,128)} %copy-done.11, bf16[2,256,1024]{2,1,0:T(8,128)(2,1)} %param.30, bf16[2,1024,256]{2,1,0:T(8,128)(2,1)} %param.29, f32[256]{0:T(256)S(1)} %bitcast.321, f32[128]{0:T(128)} %copy-done.34), kind=kOutput, calls=%fused_computation.220 | convolution fusion | flops 135593856 | bytes 1443840 | tf_op jit(solution)/shard_map/dot_general | solution.py:179
  55.9 0.3 convolution_bitcast_fusion.6
  56.5 16.0 %all_to_all.20 = bf16[16,7,16,128]{3,2,1,0:T(8,128)(2,1)S(1)} all-to-all(bf16[16,7,16,128]{3,2,1,0:T(8,128)(2,1)S(1)} %copy.143), channel_id=1, replica_groups=mesh['grp'=2,'seq'=16] {'seq'}, dimensions={0} | all-to-all | bytes 917504 | tf_op jit(solution)/shard_map/all_to_all | solution.py:158
  72.5 0.9 fusion.86
  73.9 0.8 copy-done.8
  74.6 2.5 %fusion.4 = f32[16,7,16,256]{3,2,0,1:T(8,128)S(1)} fusion(f32[256,256,1,1]{1,0,2,3:T(8,128)S(1)} %copy-done.8, f32[16,7,16,256]{3,0,2,1:T(8,128)S(1)} %pad_maximum_fusion.1), kind=kOutput, calls=%fused_computation.12 | convolution fusion | flops 1409286144 | bytes 3932160 | tf_op jit(solution)/shard_map/kpcb,bm->kpcm/dot_general | solution.py:63
  77.6 0.7 copy-done.33
  78.2 1.0 fusion.53
  79.5 0.4 copy-done.18
  79.9 1.3 %fusion.19 = bf16[16,4,16,128]{3,0,2,1:T(8,128)(2,1)S(1)} fusion(f32[16,32,1,1]{1,0,3,2:T(8,128)S(1)} %copy-done.18, f32[32,4,16,128]{3,2,1,0:T(8,128)S(1)} %pad_maximum_fusion.3, f32[4]{0:T(128)S(1)} %copy-done.25), kind=kOutput, calls=%fused_computation.39 | convolution fusion | flops 50593792 | bytes 1312784 | tf_op jit(solution)/shard_map/ak,kpcb->apcb/dot_general | solution.py:74
  81.2 0.8 copy.162
  82.0 3.9 %all-to-all-start.3 = ((bf16[16,4,16,128]{3,2,1,0:T(8,128)(2,1)}), bf16[16,4,16,128]{3,2,1,0:T(8,128)(2,1)S(1)}, u32[]{:S(2)}, u32[]{:S(2)}) async-start(bf16[16,4,16,128]{3,2,1,0:T(8,128)(2,1)} %copy.162), calls=%async_computation.3 | async-start | bytes 524288 | tf_op jit(solution)/shard_map/all_to_all | solution.py:160
  86.0 9.9 %all-to-all-done.3 = bf16[16,4,16,128]{3,2,1,0:T(8,128)(2,1)S(1)} async-done(((bf16[16,4,16,128]{3,2,1,0:T(8,128)(2,1)}), bf16[16,4,16,128]{3,2,1,0:T(8,128)(2,1)S(1)}, u32[]{:S(2)}, u32[]{:S(2)}) %all-to-all-start.3) | async-done | bytes 262176 | tf_op jit(solution)/shard_map/all_to_all | solution.py:160
  96.3 0.3 multiply_reduce_fusion.5
  96.6 1.8 %fusion.33 = bf16[256,128]{0,1:T(8,128)(2,1)S(1)} fusion(f32[256,128]{0,1:T(8,128)S(1)} %get-tuple-element.63, bf16[2,256,1024]{2,1,0:T(8,128)(2,1)} %param.30, bf16[2,1024,256]{2,1,0:T(8,128)(2,1)} %param.29, f32[256]{0:T(256)S(1)} %bitcast.318, f32[128]{0:T(128)S(1)} %add_rsqrt_fusion.1), kind=kOutput, calls=%fused_computation.59 | convolution fusion | flops 135561216 | bytes 1377792 | tf_op jit(solution)/shard_map/dot_general | solution.py:179
  98.7 0.7 copy.169
  99.5 0.3 multiply_reduce_fusion
  99.9 0.3 fusion.18
  100.1 0.8 copy.170
  (135 shorter events, 5.4 us)
Async XLA Ops:
  0.6 4.5 %copy-start.16 = (bf16[256,128]{1,0:T(8,128)(2,1)S(1)}, bf16[256,128]{1,0:T(8,128)(2,1)}, u32[]{:S(2)}) copy-start(bf16[256,128]{1,0:T(8,128)(2,1)} %param.23) | copy-start | bytes 196612
  0.6 4.8 %copy-start.2 = (bf16[2,768,256]{2,1,0:T(8,128)(2,1)S(1)}, bf16[2,768,256]{2,1,0:T(8,128)(2,1)}, u32[]{:S(2)}) copy-start(bf16[2,768,256]{2,1,0:T(8,128)(2,1)} %param.25) | copy-start | bytes 2359300
  5.7 8.8 %copy-start.19 = (f32[2,64,16]{1,2,0:T(8,128)S(1)}, f32[2,64,16]{1,2,0:T(8,128)}, u32[]{:S(2)}) copy-start(f32[2,64,16]{1,2,0:T(8,128)} %param.34) | copy-start | bytes 24580
  5.9 13.2 %copy-start.26 = (f32[2,256]{1,0:T(2,128)S(1)}, f32[2,256]{1,0:T(2,128)}, u32[]{:S(2)}) copy-start(f32[2,256]{1,0:T(2,128)} %param.37) | copy-start | bytes 6148
  5.9 13.2 %copy-start.12 = (f32[2,256,64]{1,2,0:T(8,128)S(1)}, f32[2,256,64]{1,2,0:T(8,128)}, u32[]{:S(2)}) copy-start(f32[2,256,64]{1,2,0:T(8,128)} %param.36) | copy-start | bytes 393220
  5.9 13.2 %copy-start.15 = (f32[2,64,64]{2,1,0:T(8,128)S(1)}, f32[2,64,64]{2,1,0:T(8,128)}, u32[]{:S(2)}) copy-start(f32[2,64,64]{2,1,0:T(8,128)} %param.35) | copy-start | bytes 98308
  6.7 20.6 %all-to-all-start = ((bf16[16,7,16,128]{3,2,1,0:T(8,128)(2,1)}), bf16[16,7,16,128]{3,2,1,0:T(8,128)(2,1)S(1)}, u32[]{:S(2)}, u32[]{:S(2)}) async-start(bf16[16,7,16,128]{3,2,1,0:T(8,128)(2,1)} %copy.124), calls=%async_computation | async-start | bytes 917504 | tf_op jit(solution)/shard_map/all_to_all | solution.py:158
  19.1 5.7 %copy-start.13 = (f32[32,16,1,1]{0,1,3,2:T(8,128)S(1)}, f32[32,16,1,1]{0,1,3,2:T(8,128)}, u32[]{:S(2)}) copy-start(f32[32,16,1,1]{0,1,3,2:T(8,128)} %constant.96) | copy-start | bytes 6148
  21.4 3.8 %copy-start.9 = (f32[16,128]{1,0:T(8,128)S(1)}, f32[16,128]{1,0:T(8,128)}, u32[]{:S(2)}) copy-start(f32[16,128]{1,0:T(8,128)} %constant.94) | copy-start | bytes 24580
  21.4 3.8 %copy-start.10 = (f32[16,128]{1,0:T(8,128)S(1)}, f32[16,128]{1,0:T(8,128)}, u32[]{:S(2)}) copy-start(f32[16,128]{1,0:T(8,128)} %constant.93) | copy-start | bytes 24580
  24.3 1.1 %copy-start = (f32[256,256,1,1]{1,0,3,2:T(8,128)S(1)}, f32[256,256,1,1]{1,0,3,2:T(8,128)}, u32[]{:S(2)}) copy-start(f32[256,256,1,1]{1,0,3,2:T(8,128)} %constant.97) | copy-start | bytes 786436
  31.5 1.0 copy-start.32
  33.5 0.7 copy-start.17
  33.5 0.7 copy-start.24
  36.2 15.5 %copy-start.4 = (bf16[2,256,256]{2,1,0:T(8,128)(2,1)S(1)}, bf16[2,256,256]{2,1,0:T(8,128)(2,1)}, u32[]{:S(2)}) copy-start(bf16[2,256,256]{2,1,0:T(8,128)(2,1)} %param.27) | copy-start | bytes 786436
  36.2 15.0 %all-to-all-start.1 = ((bf16[16,4,16,128]{3,2,1,0:T(8,128)(2,1)}), bf16[16,4,16,128]{3,2,1,0:T(8,128)(2,1)S(1)}, u32[]{:S(2)}, u32[]{:S(2)}) async-start(bf16[16,4,16,128]{3,2,1,0:T(8,128)(2,1)} %copy.133), calls=%async_computation.1 | async-start | bytes 524288 | tf_op jit(solution)/shard_map/all_to_all | solution.py:160
  41.3 10.8 %copy-start.5 = (bf16[2,256,256]{2,1,0:T(8,128)(2,1)S(1)}, bf16[2,256,256]{2,1,0:T(8,128)(2,1)}, u32[]{:S(2)}) copy-start(bf16[2,256,256]{2,1,0:T(8,128)(2,1)} %param.28) | copy-start | bytes 786436
  51.5 1.0 %copy-start.28 = (f32[1,1,256]{2,1,0:T(1,128)S(1)}, f32[1,1,256]{2,1,0:T(1,128)}, u32[]{:S(2)}) copy-start(f32[1,1,256]{2,1,0:T(1,128)} %get-tuple-element.46) | copy-start | bytes 3076
  51.5 1.0 %copy-start.30 = (bf16[2,256,256]{2,1,0:T(8,128)(2,1)S(1)}, bf16[2,256,256]{2,1,0:T(8,128)(2,1)}, u32[]{:S(2)}) copy-start(bf16[2,256,256]{2,1,0:T(8,128)(2,1)} %param.32) | copy-start | bytes 786436
  51.6 1.2 %copy-start.6 = (bf16[2,256,256]{2,1,0:T(8,128)(2,1)S(1)}, bf16[2,256,256]{2,1,0:T(8,128)(2,1)}, u32[]{:S(2)}) copy-start(bf16[2,256,256]{2,1,0:T(8,128)(2,1)} %param.31) | copy-start | bytes 786436
  51.6 1.2 %copy-start.23 = (f32[1,1,256]{2,1,0:T(1,128)S(1)}, f32[1,1,256]{2,1,0:T(1,128)}, u32[]{:S(2)}) copy-start(f32[1,1,256]{2,1,0:T(1,128)} %get-tuple-element.44) | copy-start | bytes 3076
  51.7 1.4 %copy-start.1 = (bf16[2,768,256]{2,1,0:T(8,128)(2,1)S(1)}, bf16[2,768,256]{2,1,0:T(8,128)(2,1)}, u32[]{:S(2)}) copy-start(bf16[2,768,256]{2,1,0:T(8,128)(2,1)} %param.26) | copy-start | bytes 2359300
  51.7 1.4 %copy-start.22 = (f32[1,1,256]{2,1,0:T(1,128)S(1)}, f32[1,1,256]{2,1,0:T(1,128)}, u32[]{:S(2)}) copy-start(f32[1,1,256]{2,1,0:T(1,128)} %get-tuple-element.43) | copy-start | bytes 3076
  52.0 1.5 %copy-start.11 = (f32[256,128]{0,1:T(8,128)}, f32[256,128]{0,1:T(8,128)S(1)}, u32[]{:S(2)}) copy-start(f32[256,128]{0,1:T(8,128)S(1)} %get-tuple-element.55) | copy-start | bytes 393220
  52.1 1.5 %copy-start.34 = (f32[128]{0:T(128)}, f32[128]{0:T(128)S(1)}, u32[]{:S(2)}) copy-start(f32[128]{0:T(128)S(1)} %add_rsqrt_fusion.5) | copy-start | bytes 1540
  53.1 0.8 copy-start.29
  53.6 2.3 %copy-start.3 = (bf16[2,768,256]{2,1,0:T(8,128)(2,1)S(1)}, bf16[2,768,256]{2,1,0:T(8,128)(2,1)}, u32[]{:S(2)}) copy-start(bf16[2,768,256]{2,1,0:T(8,128)(2,1)} %param.25) | copy-start | bytes 2359300
  53.6 2.3 %copy-start.21 = (f32[1,1,256]{2,1,0:T(1,128)S(1)}, f32[1,1,256]{2,1,0:T(1,128)}, u32[]{:S(2)}) copy-start(f32[1,1,256]{2,1,0:T(1,128)} %get-tuple-element.45) | copy-start | bytes 3076
  56.2 16.3 %copy-start.14 = (f32[32,16,1,1]{0,1,3,2:T(8,128)S(1)}, f32[32,16,1,1]{0,1,3,2:T(8,128)}, u32[]{:S(2)}) copy-start(f32[32,16,1,1]{0,1,3,2:T(8,128)} %constant.96) | copy-start | bytes 6148
  73.7 1.0 copy-start.8
  77.3 1.0 copy-start.33
  79.2 0.7 copy-start.18
  79.2 0.7 copy-start.25
  82.0 13.9 %all-to-all-start.3 = ((bf16[16,4,16,128]{3,2,1,0:T(8,128)(2,1)}), bf16[16,4,16,128]{3,2,1,0:T(8,128)(2,1)S(1)}, u32[]{:S(2)}, u32[]{:S(2)}) async-start(bf16[16,4,16,128]{3,2,1,0:T(8,128)(2,1)} %copy.162), calls=%async_computation.3 | async-start | bytes 524288 | tf_op jit(solution)/shard_map/all_to_all | solution.py:160
  85.9 10.7 %copy-start.27 = (f32[1,1,256]{2,1,0:T(1,128)S(1)}, f32[1,1,256]{2,1,0:T(1,128)}, u32[]{:S(2)}) copy-start(f32[1,1,256]{2,1,0:T(1,128)} %get-tuple-element.49) | copy-start | bytes 3076
  96.2 2.2 %copy-start.31 = (bf16[2,256,256]{2,1,0:T(8,128)(2,1)S(1)}, bf16[2,256,256]{2,1,0:T(8,128)(2,1)}, u32[]{:S(2)}) copy-start(bf16[2,256,256]{2,1,0:T(8,128)(2,1)} %param.32) | copy-start | bytes 786436
  98.4 1.4 %copy-start.7 = (bf16[2,256,256]{2,1,0:T(8,128)(2,1)S(1)}, bf16[2,256,256]{2,1,0:T(8,128)(2,1)}, u32[]{:S(2)}) copy-start(bf16[2,256,256]{2,1,0:T(8,128)(2,1)} %param.31) | copy-start | bytes 786436
  98.5 1.4 %copy-start.20 = (f32[1,1,256]{2,1,0:T(1,128)S(1)}, f32[1,1,256]{2,1,0:T(1,128)}, u32[]{:S(2)}) copy-start(f32[1,1,256]{2,1,0:T(1,128)} %get-tuple-element.42) | copy-start | bytes 3076
where the time goes:
time: 102 us; the launch traced here: 101 us
  matrix products  31.2 us (31%)
  waiting for transfers between devices  21 us (21%)
  starting transfers between devices  16.2 us (16%)
  blocking collectives  16 us (16%)
  local copies, waits for them, and re-layouts  11.5 us (11%)
  other arithmetic  3.19 us (3%)
  between operations  1.8 us (2%)
    all_to_all x2, waiting for transfers between devices, per_device(): returned = lax.all_to_all(convolved, 'seq', 0, 0, tiled=True)  19.8 us
    all_to_all x1, blocking collectives, per_device(): regrouped = lax.all_to_all(outgoing, 'seq', 0, 0, tiled=True)  16 us
    all_to_all x2, starting transfers between devices, per_device(): returned = lax.all_to_all(convolved, 'seq', 0, 0, tiled=True)  8.85 us
    all_to_all x1, starting transfers between devices, per_device(): regrouped = lax.all_to_all(outgoing, 'seq', 0, 0, tiled=True)  7.39 us
    unnamed x76, local copies, waits for them, and re-layouts  5.98 us
    dot_general x3, matrix products, forward_dft(): return jnp.einsum('kpcb,bm->kpcm', joined, lane_fwd, precision=HIGH)  5.88 us
    dot_general x2, matrix products, filter_values(): hid_one = jnp.sin(jnp.dot(first, feats, precision=HIGH))  4.52 us
    dot_general x2, matrix products, filter_values(): hid_two = jnp.sin(jnp.dot(second, hid_one, precision=HIGH))  4.51 us
  transfers between devices with their start and end apart: 3, of which 3 were waited for; matrix products, arithmetic and copies ran while one was open for 12% of the time, Pallas kernels for 0%

commit v1 on v0

--- a/solution.py
+++ b/solution.py
@@ -7,6 +7,7 @@
 from jax.sharding import PartitionSpec as P
 
 HIGH = lax.Precision.HIGHEST
+FAST = lax.Precision.DEFAULT
 
 
 def filter_values(positions, length, first, second, third, decay):
@@ -52,26 +53,31 @@
     return tuple(f32(v) for v in (lead_fwd, lead_inv, tw_c, tw_s, lane_fwd, lane_inv))
 
 
-def forward_dft(field, tables):
+def forward_dft(field, tables, prec):
     lead_fwd, _, tw_c, tw_s, lane_fwd, _ = tables
-    shards = field.shape[0]
-    stage = jnp.einsum("ka,apcb->kpcb", lead_fwd, field, precision=HIGH)
+    shards, planes, chans, local = field.shape
+    stage = jnp.dot(lead_fwd, field.reshape(shards, -1), precision=prec)
+    stage = stage.reshape(2 * shards, planes, chans, local)
     st_r, st_i = stage[:shards], stage[shards:]
     tw_r = st_r * tw_c + st_i * tw_s
     tw_i = st_i * tw_c - st_r * tw_s
-    joined = jnp.concatenate([tw_r, tw_i], axis=-1)
-    return jnp.einsum("kpcb,bm->kpcm", joined, lane_fwd, precision=HIGH)
-
-
-def inverse_dft(spec, tables):
+    joined = jnp.concatenate([tw_r, tw_i], axis=-1).reshape(-1, 2 * local)
+    spec = jnp.dot(joined, lane_fwd, precision=prec)
+    return spec.reshape(shards, planes, chans, 2 * local)
+
+
+def inverse_dft(spec, tables, prec):
     _, lead_inv, tw_c, tw_s, _, lane_inv = tables
-    local = spec.shape[-1] // 2
-    back = jnp.einsum("kpcm,mb->kpcb", spec, lane_inv, precision=HIGH)
+    shards, planes, chans, width = spec.shape
+    local = width // 2
+    back = jnp.dot(spec.reshape(-1, width), lane_inv, precision=prec)
+    back = back.reshape(shards, planes, chans, width)
     bk_r, bk_i = back[..., :local], back[..., local:]
     un_r = bk_r * tw_c - bk_i * tw_s
     un_i = bk_r * tw_s + bk_i * tw_c
-    stacked = jnp.concatenate([un_r, un_i], axis=0)
-    return jnp.einsum("ak,kpcb->apcb", lead_inv, stacked, precision=HIGH)
+    stacked = jnp.concatenate([un_r, un_i], axis=0).reshape(2 * shards, -1)
+    whole = jnp.dot(lead_inv, stacked, precision=prec)
+    return whole.reshape(shards, planes, chans, local)
 
 
 def cmul(a_r, a_i, b_r, b_i):
@@ -81,7 +87,7 @@
 def convolve(received, filt_spec, tables):
     shards, _, chans, local = received.shape
     length = shards * local
-    spec = forward_dft(received.astype(jnp.float32), tables)
+    spec = forward_dft(received.astype(jnp.float32), tables, FAST)
     re, im = spec[..., :local], spec[..., local:]
     h_r, h_i = filt_spec[..., :local], filt_spec[..., local:]
     p_r, p_i = cmul(re[:, 0], im[:, 0], h_r, h_i)
@@ -93,7 +99,7 @@
         outs_r.append(a_r - b_r)
         outs_i.append(a_i - b_i)
     prod = jnp.concatenate([jnp.stack(outs_r, axis=1), jnp.stack(outs_i, axis=1)], axis=-1)
-    result = inverse_dft(prod, tables)
+    result = inverse_dft(prod, tables, FAST)
     inv_root = 1.0 / math.sqrt(length)
     scale = jnp.array([1.0, inv_root, inv_root, inv_root], dtype=jnp.float32) / length
     return (result * scale[None, :, None, None]).astype(jnp.bfloat16)
@@ -132,7 +138,7 @@
         made = filter_values(positions, length, pe_w1[layer], pe_w2[layer], third, decay)
         filt.append(made.reshape(own, shards, tok_local).transpose(1, 0, 2))
     filt = jnp.stack(filt, axis=1).astype(jnp.float32)
-    filt_spec = forward_dft(filt, tables)
+    filt_spec = forward_dft(filt, tables, FAST)
     state_s = scalars.astype(jnp.float32)
     state_v = vectors.astype(jnp.float32)
     for layer in range(depth):
@@ -141,8 +147,11 @@
         proj_s = jnp.dot(w_qkw_s[layer], normed_s, preferred_element_type=jnp.float32)
         query_s = proj_s[:chans].astype(jnp.bfloat16)
         signal_s = (proj_s[chans : 2 * chans] * proj_s[2 * chans :]).astype(jnp.bfloat16)
-        proj_v = jnp.einsum(
-            "oc,jct->jot", w_qkw_v[layer], normed_v, preferred_element_type=jnp.float32
+        proj_v = jnp.stack(
+            [
+                jnp.dot(w_qkw_v[layer], normed_v[j], preferred_element_type=jnp.float32)
+                for j in range(3)
+            ]
         ).astype(jnp.bfloat16)
         query_v = proj_v[:, :chans]
         key_v = proj_v[:, chans : 2 * chans].reshape(3, shards, own, tok_local)

time: 102 us -> 103 us (level)
  local copies, waits for them, and re-layouts: 11.5 us -> 15.5 us
  matrix products: 31.2 us -> 27.6 us
  waiting for transfers between devices: 21 us -> 19.2 us
  other arithmetic: 3.19 us -> 4.82 us
  starting transfers between devices: 16.2 us -> 17.4 us
    dot_general x12 -> x16, matrix products: 14.5 us -> 7.24 us  [the longest x6 3.72 us: per_device(): jnp.dot(w_qkw_v[layer], normed_v[j], preferred_element_type=jnp.float32)]
    convert_element_type x0 -> x4, other arithmetic: none -> 1.86 us  [the longest x2 1.64 us: convolve(): return (result * scale[None, :, None, None]).astype(jnp.bfloat16)]
    unnamed x76 -> x87, local copies, waits for them, and re-layouts: 5.98 us -> 7.67 us
    convert_element_type x2 -> x0, local copies, waits for them, and re-layouts: 1.54 us -> none  [convolve(): return (result * scale[None, :, None, None]).astype(jnp.bfloat16)]
    slice x1, local copies, waits for them, and re-layouts: 0.01 us -> 1.53 us  [per_device(): third = lax.dynamic_slice_in_dim(pe_w3[layer], rank * own, own, axis=0)]
    dot_general x2, matrix products: 0.93 us -> 2.39 us  [filter_values(): raw = jnp.dot(third, hid_two, precision=HIGH)]
    all_to_all x2, starting transfers between devices: 8.85 us -> 10 us  [per_device(): returned = lax.all_to_all(convolved, 'seq', 0, 0, tiled=True)]
    all_to_all x1, waiting for transfers between devices: 1.17 us -> 0.01 us  [per_device(): regrouped = lax.all_to_all(outgoing, 'seq', 0, 0, tiled=True)]
  transfers between devices with their start and end apart: 3 -> 3, of which waited for: 3 -> 2; matrix products, arithmetic and copies ran while one was open for 12% -> 18% of each run, Pallas kernels for 0% -> 0%
where the time goes in v1:
time: 103 us; the launch traced here: 102 us
  matrix products  27.6 us (27%)
  waiting for transfers between devices  19.2 us (19%)
  starting transfers between devices  17.4 us (17%)
  blocking collectives  16 us (16%)
  local copies, waits for them, and re-layouts  15.5 us (15%)
  other arithmetic  4.82 us (5%)
  between operations  1.77 us (2%)
    all_to_all x2, waiting for transfers between devices, per_device(): returned = lax.all_to_all(convolved, 'seq', 0, 0, tiled=True)  19.2 us
    all_to_all x1, blocking collectives, per_device(): regrouped = lax.all_to_all(outgoing, 'seq', 0, 0, tiled=True)  16 us
    all_to_all x2, starting transfers between devices, per_device(): returned = lax.all_to_all(convolved, 'seq', 0, 0, tiled=True)  10 us
    unnamed x87, local copies, waits for them, and re-layouts  7.67 us
    all_to_all x1, starting transfers between devices, per_device(): regrouped = lax.all_to_all(outgoing, 'seq', 0, 0, tiled=True)  7.38 us
    dot_general x2, matrix products, filter_values(): hid_two = jnp.sin(jnp.dot(second, hid_one, precision=HIGH))  5.34 us
    dot_general x2, matrix products, filter_values(): hid_one = jnp.sin(jnp.dot(first, feats, precision=HIGH))  5.22 us
    dot_general x6, matrix products, per_device(): jnp.dot(w_qkw_v[layer], normed_v[j], preferred_element_type=jnp.float32)  3.72 us
  transfers between devices with their start and end apart: 3, of which 2 were waited for; matrix products, arithmetic and copies ran while one was open for 18% of the time, Pallas kernels for 0%

profile of v1, /device:TPU:0, one launch (start us, length us, event | category | flops | bytes accessed | tf_op | source)
XLA Modules:
  0.0 102.3 jit_solution(2183296809642990214)
XLA Ops:
  0.6 1.5 %fusion.216 = (f32[1,1,256]{2,1,0:T(1,128)}, f32[1,1,256]{2,1,0:T(1,128)}, f32[1,1,256]{2,1,0:T(1,128)}, f32[1,1,256]{2,1,0:T(1,128)}, f32[1,1,256]{2,1,0:T(1,12...) fusion(f32[2,4,256]{2,1,0:T(4,128)} %param.33), kind=kLoop, calls=%fused_computation.338 | loop fusion | bytes 16384 | tf_op jit(solution)/shard_map/slice | solution.py:183
  2.1 1.1 %copy.95 = bf16[3,256,128]{1,2,0:T(8,128)(2,1)S(1)} copy(bf16[3,256,128]{2,1,0:T(8,128)(2,1)} %param.24) | data formatting | bytes 393216 | tf_op args[1]
  3.5 1.3 %fusion.17 = bf16[1,768,128]{1,2,0:T(8,128)(2,1)S(1)} fusion(bf16[2,768,256]{2,1,0:T(8,128)(2,1)} %param.26, bf16[3,256,128]{1,2,0:T(8,128)(2,1)S(1)} %fusion.100), kind=kOutput, calls=%fused_computation.40 | convolution fusion | flops 50429952 | bytes 655360 | tf_op jit(solution)/shard_map/dot_general | solution.py:152
  4.8 1.3 %fusion.18 = bf16[1,768,128]{1,2,0:T(8,128)(2,1)S(1)} fusion(bf16[2,768,256]{2,1,0:T(8,128)(2,1)} %param.26, bf16[3,256,128]{1,2,0:T(8,128)(2,1)S(1)} %fusion.100), kind=kOutput, calls=%fused_computation.41 | convolution fusion | flops 50429952 | bytes 655360 | tf_op jit(solution)/shard_map/dot_general | solution.py:152
  7.7 0.8 copy.98
  8.5 7.4 %all-to-all-start = ((bf16[16,7,16,128]{3,2,1,0:T(8,128)(2,1)}), bf16[16,7,16,128]{3,2,1,0:T(8,128)(2,1)S(1)}, u32[]{:S(2)}, u32[]{:S(2)}) async-start(bf16[16,7,16,128]{3,2,1,0:T(8,128)(2,1)} %copy.98), calls=%async_computation | async-start | bytes 917504 | tf_op jit(solution)/shard_map/all_to_all | solution.py:167
  15.9 0.3 fusion.186
  16.3 2.3 %convolution_sine_fusion.1 = f32[2048,64]{0,1:T(8,128)S(1)} fusion(f32[8,2048]{1,0:T(8,128)S(1)} %get-tuple-element.59, f32[8,2048]{1,0:T(8,128)S(1)} %get-tuple-element.58, f32[2,64,16]{1,2,0:T(8,128)S(1)} %copy-done.24), kind=kOutput, calls=%fused_computation.1 | convolution fusion | flops 25198592 | bytes 663552 | tf_op jit(solution)/shard_map/dot_general | solution.py:19
  18.6 3.0 %convolution_sine_fusion.3 = f32[2048,64]{0,1:T(8,128)S(1)} fusion(f32[8,2048]{1,0:T(8,128)S(1)} %get-tuple-element.59, f32[8,2048]{1,0:T(8,128)S(1)} %get-tuple-element.58, f32[2,64,16]{1,2,0:T(8,128)} %param.34), kind=kOutput, calls=%fused_computation.3 | convolution fusion | flops 25198592 | bytes 663552 | tf_op jit(solution)/shard_map/dot_general | solution.py:19
  21.5 0.8 fusion.217
  22.3 1.5 %fusion.215 = (f32[1,256,64]{1,2,0:T(8,128)}, f32[1,256,64]{1,2,0:T(8,128)}) fusion(f32[2,256,64]{1,2,0:T(8,128)} %param.36), kind=kLoop, calls=%fused_computation.337 | loop fusion | bytes 262144 | tf_op jit(solution)/shard_map/slice | solution.py:136
  23.8 3.1 %convolution_sine_fusion = f32[2048,64]{0,1:T(8,128)S(1)} fusion(f32[2048,64]{0,1:T(8,128)S(1)} %convolution_sine_fusion.1, f32[2,64,64]{2,1,0:T(8,128)} %param.35), kind=kOutput, calls=%fused_computation | convolution fusion | flops 100663296 | bytes 1081344 | tf_op jit(solution)/shard_map/dot_general | solution.py:20
  27.0 1.2 %fusion.36 = bf16[2,16,8,128]{3,2,1,0:T(8,128)(2,1)S(1)} fusion(f32[2048,64]{0,1:T(8,128)S(1)} %convolution_sine_fusion, f32[16]{0:T(128)S(1)} %get-tuple-element.73, f32[2048]{0:T(1024)S(1)} %iota_convert_fusion, f32[1,256,64]{1,2,0:T(8,128)} %get-tuple-element.47, s32[]{:T(128)S(6)} %select_n.17), kind=kOutput, calls=%fused_computation.65 | convolution fusion | flops 25329664 | bytes 630852 | tf_op jit(solution)/shard_map/dot_general | solution.py:21
  28.3 2.3 %convolution_sine_fusion.2 = f32[2048,64]{0,1:T(8,128)S(1)} fusion(f32[2048,64]{0,1:T(8,128)S(1)} %convolution_sine_fusion.3, f32[2,64,64]{2,1,0:T(8,128)S(1)} %copy-done.21), kind=kOutput, calls=%fused_computation.2 | convolution fusion | flops 100663296 | bytes 1081344 | tf_op jit(solution)/shard_map/dot_general | solution.py:20
  30.6 1.2 %fusion.37 = bf16[2,16,8,128]{3,2,1,0:T(8,128)(2,1)S(1)} fusion(f32[2048,64]{0,1:T(8,128)S(1)} %convolution_sine_fusion.2, f32[2048]{0:T(1024)} %copy-done.18, f32[16]{0:T(128)S(1)} %get-tuple-element.72, f32[1,256,64]{1,2,0:T(8,128)S(1)} %copy-done.14, s32[]{:T(128)S(6)} %select_n.17), kind=kOutput, calls=%fused_computation.66 | convolution fusion | flops 25329664 | bytes 631300 | tf_op jit(solution)/shard_map/dot_general | solution.py:21
  32.3 0.4 copy-done.5
  32.9 0.8 slice_bitcast_fusion.4
  33.8 0.4 fusion.95
  34.9 0.6 fusion.4
  35.8 0.7 copy-done.2
  36.6 0.3 fusion.42
  37.1 0.5 copy-done.23
  37.6 0.4 convolution_bitcast_fusion.3
  38.1 0.8 multiply_convert_fusion.1
  38.9 6.1 %all-to-all-start.1 = ((bf16[16,4,16,128]{3,2,1,0:T(8,128)(2,1)}), bf16[16,4,16,128]{3,2,1,0:T(8,128)(2,1)S(1)}, u32[]{:S(2)}, u32[]{:S(2)}) async-start(bf16[16,4,16,128]{3,2,1,0:T(8,128)(2,1)} %multiply_convert_fusion.1), calls=%async_computation.1 | async-start | bytes 524288 | tf_op jit(solution)/shard_map/all_to_all | solution.py:169
  45.1 0.8 copy.110
  45.9 9.3 %all-to-all-done.1 = bf16[16,4,16,128]{3,2,1,0:T(8,128)(2,1)S(1)} async-done(((bf16[16,4,16,128]{3,2,1,0:T(8,128)(2,1)}), bf16[16,4,16,128]{3,2,1,0:T(8,128)(2,1)S(1)}, u32[]{:S(2)}, u32[]{:S(2)}) %all-to-all-start.1) | async-done | bytes 262176 | tf_op jit(solution)/shard_map/all_to_all | solution.py:169
  55.6 0.3 multiply_reduce_fusion.7
  55.9 0.3 copy-done.6
  56.3 0.3 multiply_reduce_fusion.3
  57.0 0.4 multiply_reduce_fusion.2
  57.8 0.3 fusion.21
  58.4 1.9 %multiply_reduce_fusion.6 = (f32[128]{0:T(128)S(1)}, f32[256,128]{0,1:T(8,128)S(1)}) fusion(f32[256,128]{0,1:T(8,128)S(1)} %copy-done.17, bf16[2,256,1024]{2,1,0:T(8,128)(2,1)} %param.30, bf16[2,1024,256]{2,1,0:T(8,128)(2,1)} %param.29, f32[256]{0:T(256)S(1)} %bitcast.431, f32[128]{0:T(128)S(1)} %add_rsqrt_fusion.5), kind=kOutput, calls=%fused_computation.244 | convolution fusion | flops 135593856 | bytes 1443840 | tf_op jit(solution)/shard_map/dot_general | solution.py:188
  61.3 16.0 %all_to_all.20 = bf16[16,7,16,128]{3,2,1,0:T(8,128)(2,1)S(1)} all-to-all(bf16[16,7,16,128]{3,2,1,0:T(8,128)(2,1)S(1)} %copy.114), channel_id=1, replica_groups=mesh['grp'=2,'seq'=16] {'seq'}, dimensions={0} | all-to-all | bytes 917504 | tf_op jit(solution)/shard_map/all_to_all | solution.py:167
  77.3 0.4 fusion.92
  78.5 0.6 copy-done.15
  79.1 0.4 fusion.8
  79.8 0.7 copy-done.1
  81.1 0.4 convolution_bitcast_fusion.2
  81.6 0.8 multiply_convert_fusion
  82.4 3.9 %all-to-all-start.3 = ((bf16[16,4,16,128]{3,2,1,0:T(8,128)(2,1)}), bf16[16,4,16,128]{3,2,1,0:T(8,128)(2,1)S(1)}, u32[]{:S(2)}, u32[]{:S(2)}) async-start(bf16[16,4,16,128]{3,2,1,0:T(8,128)(2,1)} %multiply_convert_fusion), calls=%async_computation.3 | async-start | bytes 524288 | tf_op jit(solution)/shard_map/all_to_all | solution.py:169
  86.5 9.9 %all-to-all-done.3 = bf16[16,4,16,128]{3,2,1,0:T(8,128)(2,1)S(1)} async-done(((bf16[16,4,16,128]{3,2,1,0:T(8,128)(2,1)}), bf16[16,4,16,128]{3,2,1,0:T(8,128)(2,1)S(1)}, u32[]{:S(2)}, u32[]{:S(2)}) %all-to-all-start.3) | async-done | bytes 262176 | tf_op jit(solution)/shard_map/all_to_all | solution.py:169
  96.8 0.3 multiply_reduce_fusion.5
  97.1 1.2 %fusion.28 = f32[256,128]{0,1:T(8,128)S(1)} fusion(bf16[2,256,256]{2,1,0:T(8,128)(2,1)} %param.32, f32[256,128]{0,1:T(8,128)S(1)} %get-tuple-element.69, f32[256]{0:T(256)S(1)} %bitcast.428, f32[128]{0:T(128)S(1)} %add_rsqrt_fusion.1), kind=kOutput, calls=%fused_computation.54 | convolution fusion | flops 16973824 | bytes 394752 | tf_op jit(solution)/shard_map/dot_general | solution.py:187
  98.4 1.7 %fusion.35 = bf16[256,128]{0,1:T(8,128)(2,1)S(1)} fusion(f32[256,128]{0,1:T(8,128)S(1)} %get-tuple-element.69, bf16[2,256,1024]{2,1,0:T(8,128)(2,1)S(1)} %copy-done.32, bf16[2,1024,256]{2,1,0:T(8,128)(2,1)} %param.29, f32[256]{0:T(256)S(1)} %bitcast.429, f32[128]{0:T(128)S(1)} %add_rsqrt_fusion.1), kind=kOutput, calls=%fused_computation.64 | convolution fusion | flops 135561216 | bytes 1377792 | tf_op jit(solution)/shard_map/dot_general | solution.py:188
  100.1 0.3 multiply_reduce_fusion
  100.7 0.8 copy.137
  101.6 0.7 copy.136
  (154 shorter events, 8.9 us)
Async XLA Ops:
  0.6 5.4 %copy-start = (bf16[2,768,256]{2,1,0:T(8,128)(2,1)S(1)}, bf16[2,768,256]{2,1,0:T(8,128)(2,1)}, u32[]{:S(2)}) copy-start(bf16[2,768,256]{2,1,0:T(8,128)(2,1)} %param.26) | copy-start | bytes 2359300
  6.1 0.8 copy-start.22
  6.1 1.2 %copy-start.3 = (bf16[2,768,256]{2,1,0:T(8,128)(2,1)S(1)}, bf16[2,768,256]{2,1,0:T(8,128)(2,1)}, u32[]{:S(2)}) copy-start(bf16[2,768,256]{2,1,0:T(8,128)(2,1)} %param.25) | copy-start | bytes 2359300
  7.5 8.8 %copy-start.24 = (f32[2,64,16]{1,2,0:T(8,128)S(1)}, f32[2,64,16]{1,2,0:T(8,128)}, u32[]{:S(2)}) copy-start(f32[2,64,16]{1,2,0:T(8,128)} %param.34) | copy-start | bytes 24580
  8.5 25.2 %all-to-all-start = ((bf16[16,7,16,128]{3,2,1,0:T(8,128)(2,1)}), bf16[16,7,16,128]{3,2,1,0:T(8,128)(2,1)S(1)}, u32[]{:S(2)}, u32[]{:S(2)}) async-start(bf16[16,7,16,128]{3,2,1,0:T(8,128)(2,1)} %copy.98), calls=%async_computation | async-start | bytes 917504 | tf_op jit(solution)/shard_map/all_to_all | solution.py:167
  15.9 14.6 %copy-start.18 = (f32[2048]{0:T(1024)}, f32[2048]{0:T(1024)S(1)}, u32[]{:S(2)}) copy-start(f32[2048]{0:T(1024)S(1)} %iota_convert_fusion) | copy-start | bytes 24580
  23.8 4.4 %copy-start.21 = (f32[2,64,64]{2,1,0:T(8,128)S(1)}, f32[2,64,64]{2,1,0:T(8,128)}, u32[]{:S(2)}) copy-start(f32[2,64,64]{2,1,0:T(8,128)} %param.35) | copy-start | bytes 98308
  23.8 6.7 %copy-start.14 = (f32[1,256,64]{1,2,0:T(8,128)S(1)}, f32[1,256,64]{1,2,0:T(8,128)}, u32[]{:S(2)}) copy-start(f32[1,256,64]{1,2,0:T(8,128)} %get-tuple-element.46) | copy-start | bytes 196612
  23.8 8.0 %copy-start.19 = (bf16[32,16]{1,0:T(8,128)(2,1)S(1)}, bf16[32,16]{1,0:T(8,128)(2,1)}, u32[]{:S(2)}) copy-start(bf16[32,16]{1,0:T(8,128)(2,1)} %constant.320) | copy-start | bytes 3076
  30.5 1.7 %copy-start.12 = (f32[16,128]{1,0:T(8,128)S(1)}, f32[16,128]{1,0:T(8,128)}, u32[]{:S(2)}) copy-start(f32[16,128]{1,0:T(8,128)} %constant.93) | copy-start | bytes 24580
  30.6 1.7 %copy-start.13 = (f32[16,128]{1,0:T(8,128)S(1)}, f32[16,128]{1,0:T(8,128)}, u32[]{:S(2)}) copy-start(f32[16,128]{1,0:T(8,128)} %constant.94) | copy-start | bytes 24580
  31.8 0.9 copy-start.5
  32.1 1.7 %copy-start.20 = (bf16[32,16]{1,0:T(8,128)(2,1)S(1)}, bf16[32,16]{1,0:T(8,128)(2,1)}, u32[]{:S(2)}) copy-start(bf16[32,16]{1,0:T(8,128)(2,1)} %constant.320) | copy-start | bytes 3076
  35.6 1.0 copy-start.2
  35.6 1.0 copy-start.34
  36.9 0.7 copy-start.23
  37.1 1.0 %copy-start.29 = (f32[4]{0:T(128)S(1)}, f32[4]{0:T(128)}, u32[]{:S(2)}) copy-start(f32[4]{0:T(128)} %constant.95) | copy-start | bytes 52
  38.9 16.7 %copy-start.7 = (bf16[2,256,256]{2,1,0:T(8,128)(2,1)S(1)}, bf16[2,256,256]{2,1,0:T(8,128)(2,1)}, u32[]{:S(2)}) copy-start(bf16[2,256,256]{2,1,0:T(8,128)(2,1)} %param.27) | copy-start | bytes 786436
  38.9 16.2 %all-to-all-start.1 = ((bf16[16,4,16,128]{3,2,1,0:T(8,128)(2,1)}), bf16[16,4,16,128]{3,2,1,0:T(8,128)(2,1)S(1)}, u32[]{:S(2)}, u32[]{:S(2)}) async-start(bf16[16,4,16,128]{3,2,1,0:T(8,128)(2,1)} %multiply_convert_fusion.1), calls=%async_computation.1 | async-start | bytes 524288 | tf_op jit(solution)/shard_map/all_to_all | solution.py:169
  55.3 0.9 copy-start.6
  55.3 1.4 %copy-start.31 = (f32[1,1,256]{2,1,0:T(1,128)S(1)}, f32[1,1,256]{2,1,0:T(1,128)}, u32[]{:S(2)}) copy-start(f32[1,1,256]{2,1,0:T(1,128)} %get-tuple-element.52) | copy-start | bytes 3076
  55.4 1.0 copy-start.8
  55.4 1.3 %copy-start.33 = (bf16[2,256,256]{2,1,0:T(8,128)(2,1)S(1)}, bf16[2,256,256]{2,1,0:T(8,128)(2,1)}, u32[]{:S(2)}) copy-start(bf16[2,256,256]{2,1,0:T(8,128)(2,1)} %param.32) | copy-start | bytes 786436
  55.4 1.6 %copy-start.10 = (bf16[2,256,256]{2,1,0:T(8,128)(2,1)S(1)}, bf16[2,256,256]{2,1,0:T(8,128)(2,1)}, u32[]{:S(2)}) copy-start(bf16[2,256,256]{2,1,0:T(8,128)(2,1)} %param.31) | copy-start | bytes 786436
  55.4 1.6 %copy-start.28 = (f32[1,1,256]{2,1,0:T(1,128)S(1)}, f32[1,1,256]{2,1,0:T(1,128)}, u32[]{:S(2)}) copy-start(f32[1,1,256]{2,1,0:T(1,128)} %get-tuple-element.50) | copy-start | bytes 3076
  55.6 1.8 %copy-start.26 = (f32[1,1,256]{2,1,0:T(1,128)S(1)}, f32[1,1,256]{2,1,0:T(1,128)}, u32[]{:S(2)}) copy-start(f32[1,1,256]{2,1,0:T(1,128)} %get-tuple-element.49) | copy-start | bytes 3076
  55.9 1.1 %copy-start.16 = (f32[256,128]{0,1:T(8,128)}, f32[256,128]{0,1:T(8,128)S(1)}, u32[]{:S(2)}) copy-start(f32[256,128]{0,1:T(8,128)S(1)} %get-tuple-element.61) | copy-start | bytes 393220
  57.3 1.0 %copy-start.17 = (f32[256,128]{0,1:T(8,128)S(1)}, f32[256,128]{0,1:T(8,128)}, u32[]{:S(2)}) copy-start(f32[256,128]{0,1:T(8,128)} %copy-done.16) | copy-start | bytes 393220
  58.1 2.2 %copy-start.4 = (bf16[2,768,256]{2,1,0:T(8,128)(2,1)S(1)}, bf16[2,768,256]{2,1,0:T(8,128)(2,1)}, u32[]{:S(2)}) copy-start(bf16[2,768,256]{2,1,0:T(8,128)(2,1)} %param.25) | copy-start | bytes 2359300
  58.1 2.2 %copy-start.27 = (f32[1,1,256]{2,1,0:T(1,128)S(1)}, f32[1,1,256]{2,1,0:T(1,128)}, u32[]{:S(2)}) copy-start(f32[1,1,256]{2,1,0:T(1,128)} %get-tuple-element.51) | copy-start | bytes 3076
  78.2 0.9 copy-start.15
  79.6 1.0 copy-start.1
  79.6 1.0 copy-start.35
  82.4 13.9 %all-to-all-start.3 = ((bf16[16,4,16,128]{3,2,1,0:T(8,128)(2,1)}), bf16[16,4,16,128]{3,2,1,0:T(8,128)(2,1)S(1)}, u32[]{:S(2)}, u32[]{:S(2)}) async-start(bf16[16,4,16,128]{3,2,1,0:T(8,128)(2,1)} %multiply_convert_fusion), calls=%async_computation.3 | async-start | bytes 524288 | tf_op jit(solution)/shard_map/all_to_all | solution.py:169
  86.4 10.7 %copy-start.30 = (f32[1,1,256]{2,1,0:T(1,128)S(1)}, f32[1,1,256]{2,1,0:T(1,128)}, u32[]{:S(2)}) copy-start(f32[1,1,256]{2,1,0:T(1,128)} %get-tuple-element.55) | copy-start | bytes 3076
  96.6 1.7 %copy-start.32 = (bf16[2,256,1024]{2,1,0:T(8,128)(2,1)S(1)}, bf16[2,256,1024]{2,1,0:T(8,128)(2,1)}, u32[]{:S(2)}) copy-start(bf16[2,256,1024]{2,1,0:T(8,128)(2,1)} %param.30) | copy-start | bytes 3145732
  97.1 3.0 %copy-start.9 = (bf16[2,256,256]{2,1,0:T(8,128)(2,1)S(1)}, bf16[2,256,256]{2,1,0:T(8,128)(2,1)}, u32[]{:S(2)}) copy-start(bf16[2,256,256]{2,1,0:T(8,128)(2,1)} %param.28) | copy-start | bytes 786436
  98.3 2.1 %copy-start.11 = (bf16[2,256,256]{2,1,0:T(8,128)(2,1)S(1)}, bf16[2,256,256]{2,1,0:T(8,128)(2,1)}, u32[]{:S(2)}) copy-start(bf16[2,256,256]{2,1,0:T(8,128)(2,1)} %param.31) | copy-start | bytes 786436
  98.3 2.1 %copy-start.25 = (f32[1,1,256]{2,1,0:T(1,128)S(1)}, f32[1,1,256]{2,1,0:T(1,128)}, u32[]{:S(2)}) copy-start(f32[1,1,256]{2,1,0:T(1,128)} %get-tuple-element.48) | copy-start | bytes 3076

commit v2 on v1

--- a/solution.py
+++ b/solution.py
@@ -131,14 +131,15 @@
     depth = w_qkw_s.shape[0]
     tables = make_tables(shards, tok_local)
     positions = jnp.arange(length, dtype=jnp.int32)
-    filt = []
-    for layer in range(depth):
-        third = lax.dynamic_slice_in_dim(pe_w3[layer], rank * own, own, axis=0)
-        decay = lax.dynamic_slice_in_dim(rates[layer], rank * own, own, axis=0)
-        made = filter_values(positions, length, pe_w1[layer], pe_w2[layer], third, decay)
-        filt.append(made.reshape(own, shards, tok_local).transpose(1, 0, 2))
-    filt = jnp.stack(filt, axis=1).astype(jnp.float32)
-    filt_spec = forward_dft(filt, tables, FAST)
+
+    def filter_spec(first, second, third, decay):
+        third = lax.dynamic_slice_in_dim(third, rank * own, own, axis=0)
+        decay = lax.dynamic_slice_in_dim(decay, rank * own, own, axis=0)
+        made = filter_values(positions, length, first, second, third, decay)
+        made = made.reshape(own, shards, tok_local).transpose(1, 0, 2)
+        return forward_dft(made[:, None].astype(jnp.float32), tables, FAST)[:, 0]
+
+    spec_next = filter_spec(pe_w1[0], pe_w2[0], pe_w3[0], rates[0])
     state_s = scalars.astype(jnp.float32)
     state_v = vectors.astype(jnp.float32)
     for layer in range(depth):
@@ -165,7 +166,12 @@
             axis=1,
         )
         regrouped = lax.all_to_all(outgoing, "seq", 0, 0, tiled=True)
-        convolved = convolve(regrouped, filt_spec[:, layer], tables)
+        convolved = convolve(regrouped, spec_next, tables)
+        if layer + 1 < depth:
+            tied = lax.optimization_barrier(
+                (pe_w1[layer + 1], pe_w2[layer + 1], pe_w3[layer + 1], rates[layer + 1], convolved)
+            )
+            spec_next = filter_spec(*tied[:4])
         returned = lax.all_to_all(convolved, "seq", 0, 0, tiled=True)
         conv_s = returned[:, 0].reshape(chans, tok_local).astype(jnp.float32)
         conv_v = returned[:, 1:].transpose(1, 0, 2, 3).reshape(3, chans, tok_local)

time: 103 us -> 98.9 us (0.960)
  blocking collectives: 16 us -> 0 us
  waiting for transfers between devices: 19.2 us -> 32.6 us
  local copies, waits for them, and re-layouts: 15.5 us -> 13.8 us
  matrix products: 27.6 us -> 26 us
  starting transfers between devices: 17.4 us -> 18.9 us
    all_to_all x1 -> x2, waiting for transfers between devices: 0.01 us -> 18.5 us  [per_device(): regrouped = lax.all_to_all(outgoing, 'seq', 0, 0, tiled=True)]
    all_to_all x1 -> x0, blocking collectives: 16 us -> none  [per_device(): regrouped = lax.all_to_all(outgoing, 'seq', 0, 0, tiled=True)]
    all_to_all x2, waiting for transfers between devices: 19.2 us -> 14.1 us  [per_device(): returned = lax.all_to_all(convolved, 'seq', 0, 0, tiled=True)]
    all_to_all x1 -> x2, starting transfers between devices: 7.38 us -> 11.1 us  [per_device(): regrouped = lax.all_to_all(outgoing, 'seq', 0, 0, tiled=True)]
    all_to_all x2, starting transfers between devices: 10 us -> 7.84 us  [per_device(): returned = lax.all_to_all(convolved, 'seq', 0, 0, tiled=True)]
    slice x2 -> x1, local copies, waits for them, and re-layouts: 2.29 us -> 0.57 us  [per_device(): rates[layer + 1]]
    dot_general x2, matrix products: 2.39 us -> 0.94 us  [filter_values(): raw = jnp.dot(third, hid_two, precision=HIGH)]
    unnamed x87 -> x92, local copies, waits for them, and re-layouts: 7.67 us -> 7.24 us
  transfers between devices with their start and end apart: 3 -> 4, of which waited for: 2 -> 4; matrix products, arithmetic and copies ran while one was open for 18% -> 14% of each run, Pallas kernels for 0% -> 0%
where the time goes in v2:
time: 98.9 us; the launch traced here: 98 us
  waiting for transfers between devices  32.6 us (33%)
  matrix products  26 us (26%)
  starting transfers between devices  18.9 us (19%)
  local copies, waits for them, and re-layouts  13.8 us (14%)
  other arithmetic  4.88 us (5%)
  between operations  1.85 us (2%)
    all_to_all x2, waiting for transfers between devices, per_device(): regrouped = lax.all_to_all(outgoing, 'seq', 0, 0, tiled=True)  18.5 us
    all_to_all x2, waiting for transfers between devices, per_device(): returned = lax.all_to_all(convolved, 'seq', 0, 0, tiled=True)  14.1 us
    all_to_all x2, starting transfers between devices, per_device(): regrouped = lax.all_to_all(outgoing, 'seq', 0, 0, tiled=True)  11.1 us
    all_to_all x2, starting transfers between devices, per_device(): returned = lax.all_to_all(convolved, 'seq', 0, 0, tiled=True)  7.84 us
    unnamed x92, local copies, waits for them, and re-layouts  7.24 us
    dot_general x2, matrix products, filter_values(): hid_two = jnp.sin(jnp.dot(second, hid_one, precision=HIGH))  4.67 us
    dot_general x2, matrix products, filter_values(): hid_one = jnp.sin(jnp.dot(first, feats, precision=HIGH))  4.52 us
    dot_general x2, matrix products, per_device(): jnp.dot(w_down[layer], hidden, preferred_element_type=jnp.float32)  3.78 us
  transfers between devices with their start and end apart: 4, of which 4 were waited for; matrix products, arithmetic and copies ran while one was open for 14% of the time, Pallas kernels for 0%

profile of v2, /device:TPU:0, one launch (start us, length us, event | category | flops | bytes accessed | tf_op | source)
XLA Modules:
  0.0 98.0 jit_solution(11973246474551721925)
XLA Ops:
  0.6 1.5 %fusion.238 = (f32[1,1,256]{2,1,0:T(1,128)}, f32[1,1,256]{2,1,0:T(1,128)}, f32[1,1,256]{2,1,0:T(1,128)}, f32[1,1,256]{2,1,0:T(1,128)}, f32[1,1,256]{2,1,0:T(1,12...) fusion(f32[2,4,256]{2,1,0:T(4,128)} %param.33), kind=kLoop, calls=%fused_computation.366 | loop fusion | bytes 16384 | tf_op jit(solution)/shard_map/slice | solution.py:189
  2.1 1.1 %copy.69 = bf16[3,256,128]{1,2,0:T(8,128)(2,1)S(1)} copy(bf16[3,256,128]{2,1,0:T(8,128)(2,1)} %param.24) | data formatting | bytes 393216 | tf_op args[1]
  3.5 1.3 %fusion.19 = bf16[1,768,128]{1,2,0:T(8,128)(2,1)S(1)} fusion(bf16[2,768,256]{2,1,0:T(8,128)(2,1)} %param.26, bf16[3,256,128]{1,2,0:T(8,128)(2,1)S(1)} %fusion.112), kind=kOutput, calls=%fused_computation.41 | convolution fusion | flops 50429952 | bytes 655360 | tf_op jit(solution)/shard_map/dot_general | solution.py:153
  4.7 1.3 %fusion.20 = bf16[1,768,128]{1,2,0:T(8,128)(2,1)S(1)} fusion(bf16[2,768,256]{2,1,0:T(8,128)(2,1)} %param.26, bf16[3,256,128]{1,2,0:T(8,128)(2,1)S(1)} %fusion.112), kind=kOutput, calls=%fused_computation.42 | convolution fusion | flops 50429952 | bytes 655360 | tf_op jit(solution)/shard_map/dot_general | solution.py:153
  7.8 0.8 copy.72
  8.5 7.5 %all-to-all-start = ((bf16[16,7,16,128]{3,2,1,0:T(8,128)(2,1)}), bf16[16,7,16,128]{3,2,1,0:T(8,128)(2,1)S(1)}, u32[]{:S(2)}, u32[]{:S(2)}) async-start(bf16[16,7,16,128]{3,2,1,0:T(8,128)(2,1)} %copy.72), calls=%async_computation | async-start | bytes 917504 | tf_op jit(solution)/shard_map/all_to_all | solution.py:168
  16.1 0.6 fusion.239
  16.7 0.3 fusion.210
  17.1 2.3 %convolution_sine_fusion.3 = f32[2048,64]{0,1:T(8,128)S(1)} fusion(f32[8,2048]{1,0:T(8,128)S(1)} %get-tuple-element.69, f32[8,2048]{1,0:T(8,128)S(1)} %get-tuple-element.68, f32[2,64,16]{1,2,0:T(8,128)S(1)} %copy-done.22), kind=kOutput, calls=%fused_computation.3 | convolution fusion | flops 25198592 | bytes 663552 | tf_op jit(solution)/shard_map/dot_general | solution.py:19
  19.4 2.3 %convolution_sine_fusion.2 = f32[2048,64]{0,1:T(8,128)S(1)} fusion(f32[2048,64]{0,1:T(8,128)S(1)} %convolution_sine_fusion.3, f32[2,64,64]{2,1,0:T(8,128)S(1)} %copy-done.17), kind=kOutput, calls=%fused_computation.2 | convolution fusion | flops 100663296 | bytes 1081344 | tf_op jit(solution)/shard_map/dot_general | solution.py:20
  21.7 0.5 fusion.39
  22.6 0.6 slice_bitcast_fusion.26
  23.4 5.9 %all-to-all-done = bf16[16,7,16,128]{3,2,1,0:T(8,128)(2,1)S(1)} async-done(((bf16[16,7,16,128]{3,2,1,0:T(8,128)(2,1)}), bf16[16,7,16,128]{3,2,1,0:T(8,128)(2,1)S(1)}, u32[]{:S(2)}, u32[]{:S(2)}) %all-to-all-start) | async-done | bytes 458784 | tf_op jit(solution)/shard_map/all_to_all | solution.py:168
  29.3 0.4 fusion.107
  30.5 0.6 copy-done.3
  31.1 0.4 fusion.4
  31.9 0.7 copy-done.35
  33.1 0.4 copy-done.20
  33.5 0.4 convolution_bitcast_fusion.3
  34.0 0.8 multiply_convert_fusion.1
  34.9 3.9 %all-to-all-start.1 = ((bf16[16,4,16,128]{3,2,1,0:T(8,128)(2,1)}), bf16[16,4,16,128]{3,2,1,0:T(8,128)(2,1)S(1)}, u32[]{:S(2)}, u32[]{:S(2)}) async-start(bf16[16,4,16,128]{3,2,1,0:T(8,128)(2,1)} %multiply_convert_fusion.1), calls=%async_computation.1 | async-start | bytes 524288 | tf_op jit(solution)/shard_map/all_to_all | solution.py:175
  38.8 2.3 %convolution_sine_fusion.1 = f32[64,2048]{1,0:T(8,128)S(1)} fusion(f32[64,16]{0,1:T(8,128)S(1)} %copy-done.19, f32[8,2048]{1,0:T(8,128)S(1)} %get-tuple-element.69, f32[8,2048]{1,0:T(8,128)S(1)} %get-tuple-element.68), kind=kOutput, calls=%fused_computation.1 | convolution fusion | flops 25198592 | bytes 659456 | tf_op jit(solution)/shard_map/dot_general | solution.py:19
  41.1 2.4 %convolution_sine_fusion = f32[64,2048]{1,0:T(8,128)S(1)} fusion(f32[64,64]{1,0:T(8,128)S(1)} %slice_bitcast_fusion.25, f32[64,2048]{1,0:T(8,128)S(1)} %convolution_sine_fusion.1), kind=kOutput, calls=%fused_computation | convolution fusion | flops 100663296 | bytes 1064960 | tf_op jit(solution)/shard_map/dot_general | solution.py:20
  43.6 0.5 fusion.38
  44.0 0.6 copy.161
  44.7 4.1 %all-to-all-done.1 = bf16[16,4,16,128]{3,2,1,0:T(8,128)(2,1)S(1)} async-done(((bf16[16,4,16,128]{3,2,1,0:T(8,128)(2,1)}), bf16[16,4,16,128]{3,2,1,0:T(8,128)(2,1)S(1)}, u32[]{:S(2)}, u32[]{:S(2)}) %all-to-all-start.1) | async-done | bytes 262176 | tf_op jit(solution)/shard_map/all_to_all | solution.py:175
  49.3 1.2 %multiply_reduce_fusion.7 = (f32[128]{0:T(128)S(1)}, f32[256,128]{0,1:T(8,128)S(1)}) fusion(bf16[2,256,256]{2,1,0:T(8,128)(2,1)} %param.27, f32[256,128]{0,1:T(8,128)S(1)} %multiply_reduce_fusion.4, f32[256,128]{0,1:T(8,128)S(1)} %copy.78, f32[768,128]{0,1:T(8,128)S(1)} %convolution_bitcast_fusion.9, bf16[256,128]{0,1:T(8,128)(2,1)S(1)} %copy.67), kind=kOutput, calls=%fused_computation.270 | convolution fusion | flops 17039232 | bytes 655872 | tf_op jit(solution)/shard_map/dot_general | solution.py:184
  50.5 0.3 multiply_reduce_fusion.3
  51.2 0.4 multiply_reduce_fusion.2
  52.6 1.9 %multiply_reduce_fusion.6 = (f32[128]{0:T(128)S(1)}, f32[256,128]{0,1:T(8,128)S(1)}) fusion(f32[256,128]{0,1:T(8,128)} %copy-done.13, bf16[2,256,1024]{2,1,0:T(8,128)(2,1)} %param.30, bf16[2,1024,256]{2,1,0:T(8,128)(2,1)} %param.29, f32[256]{0:T(256)S(1)} %bitcast.452, f32[128]{0:T(128)S(1)} %add_rsqrt_fusion.5), kind=kOutput, calls=%fused_computation.268 | convolution fusion | flops 135593856 | bytes 1443840 | tf_op jit(solution)/shard_map/dot_general | solution.py:194
  55.5 0.8 copy.86
  56.3 3.6 %all-to-all-start.2 = ((bf16[16,7,16,128]{3,2,1,0:T(8,128)(2,1)}), bf16[16,7,16,128]{3,2,1,0:T(8,128)(2,1)S(1)}, u32[]{:S(2)}, u32[]{:S(2)}) async-start(bf16[16,7,16,128]{3,2,1,0:T(8,128)(2,1)} %copy.86), calls=%async_computation.2 | async-start | bytes 917504 | tf_op jit(solution)/shard_map/all_to_all | solution.py:168
  60.4 12.7 %all-to-all-done.2 = bf16[16,7,16,128]{3,2,1,0:T(8,128)(2,1)S(1)} async-done(((bf16[16,7,16,128]{3,2,1,0:T(8,128)(2,1)}), bf16[16,7,16,128]{3,2,1,0:T(8,128)(2,1)S(1)}, u32[]{:S(2)}, u32[]{:S(2)}) %all-to-all-start.2) | async-done | bytes 458784 | tf_op jit(solution)/shard_map/all_to_all | solution.py:168
  73.1 0.4 fusion.104
  74.2 0.4 fusion.8
  75.0 0.7 copy-done.36
  75.7 0.3 fusion.60
  76.2 0.5 copy-done.21
  76.6 0.4 convolution_bitcast_fusion.2
  77.2 0.8 multiply_convert_fusion
  78.0 3.9 %all-to-all-start.3 = ((bf16[16,4,16,128]{3,2,1,0:T(8,128)(2,1)}), bf16[16,4,16,128]{3,2,1,0:T(8,128)(2,1)S(1)}, u32[]{:S(2)}, u32[]{:S(2)}) async-start(bf16[16,4,16,128]{3,2,1,0:T(8,128)(2,1)} %multiply_convert_fusion), calls=%async_computation.3 | async-start | bytes 524288 | tf_op jit(solution)/shard_map/all_to_all | solution.py:175
  82.1 9.9 %all-to-all-done.3 = bf16[16,4,16,128]{3,2,1,0:T(8,128)(2,1)S(1)} async-done(((bf16[16,4,16,128]{3,2,1,0:T(8,128)(2,1)}), bf16[16,4,16,128]{3,2,1,0:T(8,128)(2,1)S(1)}, u32[]{:S(2)}, u32[]{:S(2)}) %all-to-all-start.3) | async-done | bytes 262176 | tf_op jit(solution)/shard_map/all_to_all | solution.py:175
  92.4 0.3 multiply_reduce_fusion.5
  92.7 1.2 %fusion.30 = f32[256,128]{0,1:T(8,128)S(1)} fusion(bf16[2,256,256]{2,1,0:T(8,128)(2,1)} %param.32, f32[256,128]{0,1:T(8,128)S(1)} %get-tuple-element.79, f32[256]{0:T(256)S(1)} %bitcast.449, f32[128]{0:T(128)S(1)} %add_rsqrt_fusion.1), kind=kOutput, calls=%fused_computation.55 | convolution fusion | flops 16973824 | bytes 394752 | tf_op jit(solution)/shard_map/dot_general | solution.py:193
  93.9 1.8 %fusion.37 = bf16[256,128]{0,1:T(8,128)(2,1)S(1)} fusion(f32[256,128]{0,1:T(8,128)S(1)} %get-tuple-element.79, bf16[2,256,1024]{2,1,0:T(8,128)(2,1)} %param.30, bf16[2,1024,256]{2,1,0:T(8,128)(2,1)} %param.29, f32[256]{0:T(256)S(1)} %bitcast.450, f32[128]{0:T(128)S(1)} %add_rsqrt_fusion.1), kind=kOutput, calls=%fused_computation.65 | convolution fusion | flops 135561216 | bytes 1377792 | tf_op jit(solution)/shard_map/dot_general | solution.py:194
  95.8 0.3 multiply_reduce_fusion
  96.5 0.8 copy.98
  97.3 0.7 copy.97
  (164 shorter events, 9.5 us)
Async XLA Ops:
  0.6 5.4 %copy-start = (bf16[2,768,256]{2,1,0:T(8,128)(2,1)S(1)}, bf16[2,768,256]{2,1,0:T(8,128)(2,1)}, u32[]{:S(2)}) copy-start(bf16[2,768,256]{2,1,0:T(8,128)(2,1)} %param.26) | copy-start | bytes 2359300
  6.0 0.8 copy-start.18
  6.1 1.2 %copy-start.1 = (bf16[2,768,256]{2,1,0:T(8,128)(2,1)S(1)}, bf16[2,768,256]{2,1,0:T(8,128)(2,1)}, u32[]{:S(2)}) copy-start(bf16[2,768,256]{2,1,0:T(8,128)(2,1)} %param.25) | copy-start | bytes 2359300
  7.5 8.6 %copy-start.27 = (f32[2,256]{1,0:T(2,128)S(1)}, f32[2,256]{1,0:T(2,128)}, u32[]{:S(2)}) copy-start(f32[2,256]{1,0:T(2,128)} %param.37) | copy-start | bytes 6148
  7.5 9.5 %copy-start.16 = (f32[2,256,64]{1,2,0:T(8,128)S(1)}, f32[2,256,64]{1,2,0:T(8,128)}, u32[]{:S(2)}) copy-start(f32[2,256,64]{1,2,0:T(8,128)} %param.36) | copy-start | bytes 393220
  7.6 9.6 %copy-start.22 = (f32[2,64,16]{1,2,0:T(8,128)S(1)}, f32[2,64,16]{1,2,0:T(8,128)}, u32[]{:S(2)}) copy-start(f32[2,64,16]{1,2,0:T(8,128)} %param.34) | copy-start | bytes 24580
  7.7 11.7 %copy-start.17 = (f32[2,64,64]{2,1,0:T(8,128)S(1)}, f32[2,64,64]{2,1,0:T(8,128)}, u32[]{:S(2)}) copy-start(f32[2,64,64]{2,1,0:T(8,128)} %param.35) | copy-start | bytes 98308
  8.5 13.7 %copy-start.14 = (bf16[32,16]{1,0:T(8,128)(2,1)S(1)}, bf16[32,16]{1,0:T(8,128)(2,1)}, u32[]{:S(2)}) copy-start(bf16[32,16]{1,0:T(8,128)(2,1)} %constant.352) | copy-start | bytes 3076
  8.5 20.8 %all-to-all-start = ((bf16[16,7,16,128]{3,2,1,0:T(8,128)(2,1)}), bf16[16,7,16,128]{3,2,1,0:T(8,128)(2,1)S(1)}, u32[]{:S(2)}, u32[]{:S(2)}) async-start(bf16[16,7,16,128]{3,2,1,0:T(8,128)(2,1)} %copy.72), calls=%async_computation | async-start | bytes 917504 | tf_op jit(solution)/shard_map/all_to_all | solution.py:168
  19.4 3.8 %copy-start.5 = (f32[16,128]{1,0:T(8,128)S(1)}, f32[16,128]{1,0:T(8,128)}, u32[]{:S(2)}) copy-start(f32[16,128]{1,0:T(8,128)} %constant.91) | copy-start | bytes 24580
  19.4 3.8 %copy-start.6 = (f32[16,128]{1,0:T(8,128)S(1)}, f32[16,128]{1,0:T(8,128)}, u32[]{:S(2)}) copy-start(f32[16,128]{1,0:T(8,128)} %constant.92) | copy-start | bytes 24580
  19.4 3.8 %copy-start.4 = (bf16[256,256,1]{1,0,2:T(8,128)(2,1)S(1)}, bf16[256,256,1]{1,0,2:T(8,128)(2,1)}, u32[]{:S(2)}) copy-start(bf16[256,256,1]{1,0,2:T(8,128)(2,1)} %constant.353) | copy-start | bytes 393220
  30.2 0.9 copy-start.3
  31.6 0.9 copy-start.35
  32.8 0.7 copy-start.20
  33.0 1.0 %copy-start.28 = (f32[4]{0:T(128)S(1)}, f32[4]{0:T(128)}, u32[]{:S(2)}) copy-start(f32[4]{0:T(128)} %constant.93) | copy-start | bytes 52
  33.1 5.7 %copy-start.19 = (f32[64,16]{0,1:T(8,128)S(1)}, f32[64,16]{0,1:T(8,128)}, u32[]{:S(2)}) copy-start(f32[64,16]{0,1:T(8,128)} %slice_bitcast_fusion.26) | copy-start | bytes 12292
  33.5 7.5 %copy-start.33 = (f32[1,256]{1,0:T(1,128)S(1)}, f32[1,256]{1,0:T(1,128)}, u32[]{:S(2)}) copy-start(f32[1,256]{1,0:T(1,128)} %get-tuple-element.66) | copy-start | bytes 3076
  34.9 13.9 %all-to-all-start.1 = ((bf16[16,4,16,128]{3,2,1,0:T(8,128)(2,1)}), bf16[16,4,16,128]{3,2,1,0:T(8,128)(2,1)S(1)}, u32[]{:S(2)}, u32[]{:S(2)}) async-start(bf16[16,4,16,128]{3,2,1,0:T(8,128)(2,1)} %multiply_convert_fusion.1), calls=%async_computation.1 | async-start | bytes 524288 | tf_op jit(solution)/shard_map/all_to_all | solution.py:175
  49.0 1.5 %copy-start.9 = (bf16[2,256,256]{2,1,0:T(8,128)(2,1)S(1)}, bf16[2,256,256]{2,1,0:T(8,128)(2,1)}, u32[]{:S(2)}) copy-start(bf16[2,256,256]{2,1,0:T(8,128)(2,1)} %param.28) | copy-start | bytes 786436
  49.0 1.9 %copy-start.31 = (f32[1,1,256]{2,1,0:T(1,128)S(1)}, f32[1,1,256]{2,1,0:T(1,128)}, u32[]{:S(2)}) copy-start(f32[1,1,256]{2,1,0:T(1,128)} %get-tuple-element.62) | copy-start | bytes 3076
  49.1 1.8 %copy-start.34 = (bf16[2,256,256]{2,1,0:T(8,128)(2,1)S(1)}, bf16[2,256,256]{2,1,0:T(8,128)(2,1)}, u32[]{:S(2)}) copy-start(bf16[2,256,256]{2,1,0:T(8,128)(2,1)} %param.32) | copy-start | bytes 786436
  49.1 2.1 %copy-start.11 = (bf16[2,256,256]{2,1,0:T(8,128)(2,1)S(1)}, bf16[2,256,256]{2,1,0:T(8,128)(2,1)}, u32[]{:S(2)}) copy-start(bf16[2,256,256]{2,1,0:T(8,128)(2,1)} %param.31) | copy-start | bytes 786436
  49.1 2.1 %copy-start.26 = (f32[1,1,256]{2,1,0:T(1,128)S(1)}, f32[1,1,256]{2,1,0:T(1,128)}, u32[]{:S(2)}) copy-start(f32[1,1,256]{2,1,0:T(1,128)} %get-tuple-element.60) | copy-start | bytes 3076
  49.3 2.3 %copy-start.24 = (f32[1,1,256]{2,1,0:T(1,128)S(1)}, f32[1,1,256]{2,1,0:T(1,128)}, u32[]{:S(2)}) copy-start(f32[1,1,256]{2,1,0:T(1,128)} %get-tuple-element.59) | copy-start | bytes 3076
  50.5 1.5 %copy-start.13 = (f32[256,128]{0,1:T(8,128)}, f32[256,128]{0,1:T(8,128)S(1)}, u32[]{:S(2)}) copy-start(f32[256,128]{0,1:T(8,128)S(1)} %get-tuple-element.71) | copy-start | bytes 393220
  51.2 1.4 %copy-start.32 = (f32[1,1,256]{2,1,0:T(1,128)S(1)}, f32[1,1,256]{2,1,0:T(1,128)}, u32[]{:S(2)}) copy-start(f32[1,1,256]{2,1,0:T(1,128)} %get-tuple-element.62) | copy-start | bytes 3076
  52.3 2.3 %copy-start.2 = (bf16[2,768,256]{2,1,0:T(8,128)(2,1)S(1)}, bf16[2,768,256]{2,1,0:T(8,128)(2,1)}, u32[]{:S(2)}) copy-start(bf16[2,768,256]{2,1,0:T(8,128)(2,1)} %param.25) | copy-start | bytes 2359300
  52.3 2.3 %copy-start.25 = (f32[1,1,256]{2,1,0:T(1,128)S(1)}, f32[1,1,256]{2,1,0:T(1,128)}, u32[]{:S(2)}) copy-start(f32[1,1,256]{2,1,0:T(1,128)} %get-tuple-element.61) | copy-start | bytes 3076
  55.1 4.8 %copy-start.8 = (bf16[2,16,8,128]{3,2,0,1:T(8,128)(2,1)S(1)}, bf16[2,16,8,128]{3,2,0,1:T(8,128)(2,1)}, u32[]{:S(2)}) copy-start(bf16[2,16,8,128]{3,2,0,1:T(8,128)(2,1)} %copy.161) | copy-start | bytes 196612
  55.1 4.8 %copy-start.15 = (bf16[32,16]{1,0:T(8,128)(2,1)S(1)}, bf16[32,16]{1,0:T(8,128)(2,1)}, u32[]{:S(2)}) copy-start(bf16[32,16]{1,0:T(8,128)(2,1)} %constant.352) | copy-start | bytes 3076
  56.3 16.8 %all-to-all-start.2 = ((bf16[16,7,16,128]{3,2,1,0:T(8,128)(2,1)}), bf16[16,7,16,128]{3,2,1,0:T(8,128)(2,1)S(1)}, u32[]{:S(2)}, u32[]{:S(2)}) async-start(bf16[16,7,16,128]{3,2,1,0:T(8,128)(2,1)} %copy.86), calls=%async_computation.2 | async-start | bytes 917504 | tf_op jit(solution)/shard_map/all_to_all | solution.py:168
  74.7 0.9 copy-start.36
  76.0 0.7 copy-start.21
  76.1 1.0 %copy-start.29 = (f32[4]{0:T(128)S(1)}, f32[4]{0:T(128)}, u32[]{:S(2)}) copy-start(f32[4]{0:T(128)} %constant.93) | copy-start | bytes 52
  78.0 14.4 %copy-start.7 = (bf16[2,256,256]{2,1,0:T(8,128)(2,1)S(1)}, bf16[2,256,256]{2,1,0:T(8,128)(2,1)}, u32[]{:S(2)}) copy-start(bf16[2,256,256]{2,1,0:T(8,128)(2,1)} %param.27) | copy-start | bytes 786436
  78.0 14.0 %all-to-all-start.3 = ((bf16[16,4,16,128]{3,2,1,0:T(8,128)(2,1)}), bf16[16,4,16,128]{3,2,1,0:T(8,128)(2,1)S(1)}, u32[]{:S(2)}, u32[]{:S(2)}) async-start(bf16[16,4,16,128]{3,2,1,0:T(8,128)(2,1)} %multiply_convert_fusion), calls=%async_computation.3 | async-start | bytes 524288 | tf_op jit(solution)/shard_map/all_to_all | solution.py:175
  82.0 10.7 %copy-start.30 = (f32[1,1,256]{2,1,0:T(1,128)S(1)}, f32[1,1,256]{2,1,0:T(1,128)}, u32[]{:S(2)}) copy-start(f32[1,1,256]{2,1,0:T(1,128)} %get-tuple-element.65) | copy-start | bytes 3076
  92.7 3.1 %copy-start.10 = (bf16[2,256,256]{2,1,0:T(8,128)(2,1)S(1)}, bf16[2,256,256]{2,1,0:T(8,128)(2,1)}, u32[]{:S(2)}) copy-start(bf16[2,256,256]{2,1,0:T(8,128)(2,1)} %param.28) | copy-start | bytes 786436
  93.9 2.3 %copy-start.12 = (bf16[2,256,256]{2,1,0:T(8,128)(2,1)S(1)}, bf16[2,256,256]{2,1,0:T(8,128)(2,1)}, u32[]{:S(2)}) copy-start(bf16[2,256,256]{2,1,0:T(8,128)(2,1)} %param.31) | copy-start | bytes 786436
  93.9 2.3 %copy-start.23 = (f32[1,1,256]{2,1,0:T(1,128)S(1)}, f32[1,1,256]{2,1,0:T(1,128)}, u32[]{:S(2)}) copy-start(f32[1,1,256]{2,1,0:T(1,128)} %get-tuple-element.58) | copy-start | bytes 3076

commit v3 on v2

--- a/solution.py
+++ b/solution.py
@@ -4,6 +4,7 @@
 import jax.numpy as jnp
 import numpy as np
 from jax import lax
+from jax.experimental import pallas as pl
 from jax.sharding import PartitionSpec as P
 
 HIGH = lax.Precision.HIGHEST
@@ -103,6 +104,108 @@
     inv_root = 1.0 / math.sqrt(length)
     scale = jnp.array([1.0, inv_root, inv_root, inv_root], dtype=jnp.float32) / length
     return (result * scale[None, :, None, None]).astype(jnp.bfloat16)
+
+
+def gelu_tanh(x):
+    return 0.5 * x * (1.0 + jnp.tanh(math.sqrt(2.0 / math.pi) * (x + 0.044715 * (x * x * x))))
+
+
+def token_step(post, pre, arrays, weights):
+    f32, bf16 = jnp.float32, jnp.bfloat16
+    state_s, state_v = arrays["state_s"], arrays["state_v"]
+    chans, tok = state_s.shape
+    full = lambda shape: pl.BlockSpec(shape, lambda i, n=len(shape): (0,) * n)
+
+    def layer_spec(w, layer):
+        return pl.BlockSpec((pl.Squeezed(),) + w.shape[1:], lambda i: (layer,) + (0,) * (w.ndim - 1))
+
+    ins, specs = [state_s, state_v], [full(state_s.shape), full(state_v.shape)]
+    post_names = ("w_out_s", "w_out_v", "w_up", "w_down", "w_mix", "w_gate")
+    if post is not None:
+        ins += [arrays["conv"], arrays["query"]]
+        specs += [full(arrays["conv"].shape), full(arrays["query"].shape)]
+        for name in post_names + ("gains_t",):
+            ins.append(weights[name])
+            specs.append(layer_spec(weights[name], post))
+    if pre is not None:
+        for name in ("w_qkw_s", "w_qkw_v", "gains_t"):
+            ins.append(weights[name])
+            specs.append(layer_spec(weights[name], pre))
+    outs = []
+    if pre is not None:
+        outs += [((7, chans, tok), bf16), ((4, chans, tok), bf16)]
+        if post is not None:
+            outs += [((chans, tok), f32), ((3, chans, tok), f32)]
+    else:
+        outs += [((chans, tok), bf16), ((3, chans, tok), bf16)]
+
+    def snorm(x, g):
+        return x * lax.rsqrt(jnp.mean(x * x, axis=0, keepdims=True) + 1e-05) * g
+
+    def vnorm(xs, g):
+        total = sum(jnp.sum(x * x, axis=0, keepdims=True) for x in xs)
+        scale = lax.rsqrt(total / (3 * chans) + 1e-05)
+        return [x * scale * g for x in xs]
+
+    def mm(w, x):
+        return jnp.dot(w, x, preferred_element_type=f32)
+
+    def kernel(*refs):
+        refs = list(refs)
+        ss_ref, sv_ref = refs.pop(0), refs.pop(0)
+        ss = ss_ref[...].astype(f32)
+        sv = [sv_ref[j].astype(f32) for j in range(3)]
+        if post is not None:
+            conv_ref, q_ref = refs.pop(0), refs.pop(0)
+            wos, wov, wup, wdn, wmx, wgt, gp = [refs.pop(0) for _ in range(7)]
+            g = gp[...]
+            qs = q_ref[0].astype(f32)
+            ys = conv_ref[0].astype(f32)
+            yv = [conv_ref[1 + j].astype(f32) for j in range(3)]
+            mix = q_ref[1].astype(f32) * yv[0]
+            mix = mix + q_ref[2].astype(f32) * yv[1]
+            mix = mix + q_ref[3].astype(f32) * yv[2]
+            out_s = (qs * ys + mix).astype(bf16)
+            ss = ss + mm(wos[...], out_s)
+            sv = [sv[j] + mm(wov[...], (qs * yv[j]).astype(bf16)) for j in range(3)]
+            mlp_s = snorm(ss, g[:, 2:3]).astype(bf16)
+            mlp_v = [v.astype(bf16) for v in vnorm(sv, g[:, 3:4])]
+            hidden = gelu_tanh(mm(wup[...], mlp_s)).astype(bf16)
+            gate = 1.0 / (1.0 + jnp.exp(-mm(wgt[...], mlp_s)))
+            ss = ss + mm(wdn[...], hidden)
+            sv = [sv[j] + mm(wmx[...], mlp_v[j]) * gate for j in range(3)]
+        if pre is not None:
+            wqs, wqv, gq = [refs.pop(0) for _ in range(3)]
+            g = gq[...]
+            planes_ref, query_ref = refs.pop(0), refs.pop(0)
+            normed_s = snorm(ss, g[:, 0:1]).astype(bf16)
+            normed_v = [v.astype(bf16) for v in vnorm(sv, g[:, 1:2])]
+            ps = mm(wqs[...], normed_s)
+            query_ref[0] = ps[:chans].astype(bf16)
+            planes_ref[0] = (ps[chans : 2 * chans] * ps[2 * chans :]).astype(bf16)
+            for j in range(3):
+                pv = mm(wqv[...], normed_v[j]).astype(bf16)
+                query_ref[1 + j] = pv[:chans]
+                planes_ref[1 + j] = pv[chans : 2 * chans]
+                planes_ref[4 + j] = pv[2 * chans :]
+            if post is not None:
+                ns_ref, nv_ref = refs.pop(0), refs.pop(0)
+                ns_ref[...] = ss
+                for j in range(3):
+                    nv_ref[j] = sv[j]
+        else:
+            os_ref, ov_ref = refs.pop(0), refs.pop(0)
+            os_ref[...] = ss.astype(bf16)
+            for j in range(3):
+                ov_ref[j] = sv[j].astype(bf16)
+
+    return pl.pallas_call(
+        kernel,
+        grid=(1,),
+        in_specs=specs,
+        out_specs=[full(shape) for shape, _ in outs],
+        out_shape=[jax.ShapeDtypeStruct(shape, dtype) for shape, dtype in outs],
+    )(*ins)
 
 
 def per_device(
@@ -140,31 +243,21 @@
         return forward_dft(made[:, None].astype(jnp.float32), tables, FAST)[:, 0]
 
     spec_next = filter_spec(pe_w1[0], pe_w2[0], pe_w3[0], rates[0])
-    state_s = scalars.astype(jnp.float32)
-    state_v = vectors.astype(jnp.float32)
+    weights = {
+        "w_qkw_s": w_qkw_s,
+        "w_qkw_v": w_qkw_v,
+        "w_out_s": w_out_s,
+        "w_out_v": w_out_v,
+        "w_up": w_up,
+        "w_down": w_down,
+        "w_mix": w_mix,
+        "w_gate": w_gate,
+        "gains_t": gains.transpose(0, 2, 1),
+    }
+    arrays = {"state_s": scalars, "state_v": vectors}
+    planes, query = token_step(None, 0, arrays, weights)
     for layer in range(depth):
-        normed_s = scalar_norm(state_s, gains[layer, 0]).astype(jnp.bfloat16)
-        normed_v = vector_norm(state_v, gains[layer, 1]).astype(jnp.bfloat16)
-        proj_s = jnp.dot(w_qkw_s[layer], normed_s, preferred_element_type=jnp.float32)
-        query_s = proj_s[:chans].astype(jnp.bfloat16)
-        signal_s = (proj_s[chans : 2 * chans] * proj_s[2 * chans :]).astype(jnp.bfloat16)
-        proj_v = jnp.stack(
-            [
-                jnp.dot(w_qkw_v[layer], normed_v[j], preferred_element_type=jnp.float32)
-                for j in range(3)
-            ]
-        ).astype(jnp.bfloat16)
-        query_v = proj_v[:, :chans]
-        key_v = proj_v[:, chans : 2 * chans].reshape(3, shards, own, tok_local)
-        val_v = proj_v[:, 2 * chans :].reshape(3, shards, own, tok_local)
-        outgoing = jnp.concatenate(
-            [
-                signal_s.reshape(shards, 1, own, tok_local),
-                key_v.transpose(1, 0, 2, 3),
-                val_v.transpose(1, 0, 2, 3),
-            ],
-            axis=1,
-        )
+        outgoing = planes.reshape(7, shards, own, tok_local).transpose(1, 0, 2, 3)
         regrouped = lax.all_to_all(outgoing, "seq", 0, 0, tiled=True)
         convolved = convolve(regrouped, spec_next, tables)
         if layer + 1 < depth:
@@ -173,31 +266,13 @@
             )
             spec_next = filter_spec(*tied[:4])
         returned = lax.all_to_all(convolved, "seq", 0, 0, tiled=True)
-        conv_s = returned[:, 0].reshape(chans, tok_local).astype(jnp.float32)
-        conv_v = returned[:, 1:].transpose(1, 0, 2, 3).reshape(3, chans, tok_local)
-        conv_v = conv_v.astype(jnp.float32)
-        qs_f = query_s.astype(jnp.float32)
-        out_s = (qs_f * conv_s + jnp.sum(query_v.astype(jnp.float32) * conv_v, axis=0)).astype(
-            jnp.bfloat16
-        )
-        out_v = (qs_f[None] * conv_v).astype(jnp.bfloat16)
-        state_s = state_s + jnp.dot(w_out_s[layer], out_s, preferred_element_type=jnp.float32)
-        state_v = state_v + jnp.einsum(
-            "oc,jct->jot", w_out_v[layer], out_v, preferred_element_type=jnp.float32
-        )
-        mlp_s = scalar_norm(state_s, gains[layer, 2]).astype(jnp.bfloat16)
-        mlp_v = vector_norm(state_v, gains[layer, 3]).astype(jnp.bfloat16)
-        hidden = jax.nn.gelu(
-            jnp.dot(w_up[layer], mlp_s, preferred_element_type=jnp.float32)
-        ).astype(jnp.bfloat16)
-        gate = jax.nn.sigmoid(jnp.dot(w_gate[layer], mlp_s, preferred_element_type=jnp.float32))
-        state_s = state_s + jnp.dot(w_down[layer], hidden, preferred_element_type=jnp.float32)
-        state_v = (
-            state_v
-            + jnp.einsum("oc,jct->jot", w_mix[layer], mlp_v, preferred_element_type=jnp.float32)
-            * gate[None]
-        )
-    return (state_s.astype(jnp.bfloat16), state_v.astype(jnp.bfloat16))
+        arrays["conv"] = returned.transpose(1, 0, 2, 3).reshape(4, chans, tok_local)
+        arrays["query"] = query
+        if layer + 1 < depth:
+            planes, query, new_s, new_v = token_step(layer, layer + 1, arrays, weights)
+            arrays["state_s"], arrays["state_v"] = new_s, new_v
+        else:
+            return tuple(token_step(layer, None, arrays, weights))
 
 
 def solution(mesh):

time: 98.9 us -> 92.3 us (0.933)
  blocking collectives: 0 us -> 13.7 us
  matrix products: 26 us -> 13.7 us
  Pallas kernels: 0 us -> 10.4 us
  waiting for transfers between devices: 32.6 us -> 24.6 us
  local copies, waits for them, and re-layouts: 13.8 us -> 9.85 us
  starting transfers between devices: 18.9 us -> 15 us
  other arithmetic: 4.88 us -> 3.12 us
    all_to_all x0 -> x1, blocking collectives: none -> 13.7 us  [per_device(): returned = lax.all_to_all(convolved, 'seq', 0, 0, tiled=True)]
    dot_general x18 -> x0, matrix products: 12.3 us -> none  [the longest x2 3.78 us: per_device(): jnp.dot(w_down[layer], hidden, preferred_element_type=jnp.float32)]
    pallas_call x0 -> x3, Pallas kernels: none -> 10.4 us  [token_step(): pl.pallas_call(kernel, grid=(1,), in_specs=specs, out_specs=[full(shape)...]
    all_to_all x2 -> x1, waiting for transfers between devices: 14.1 us -> 4.78 us  [per_device(): returned = lax.all_to_all(convolved, 'seq', 0, 0, tiled=True)]
    all_to_all x2 -> x1, starting transfers between devices: 7.84 us -> 3.9 us  [per_device(): returned = lax.all_to_all(convolved, 'seq', 0, 0, tiled=True)]
    reshape x0 -> x2, local copies, waits for them, and re-layouts: none -> 3.7 us  [per_device(): outgoing = planes.reshape(7, shards, own, tok_local).transpose(1, 0, 2, 3)]
    unnamed x92 -> x39, local copies, waits for them, and re-layouts: 7.24 us -> 4.66 us
    slice x9 -> x0, local copies, waits for them, and re-layouts: 2.22 us -> none  [the longest x1 1.49 us: per_device(): mlp_v = vector_norm(state_v, gains[layer, 3]).astype(jnp.bfloat16)]
  transfers between devices with their start and end apart: 4 -> 3, of which waited for: 4 -> 3; matrix products, arithmetic and copies ran while one was open for 14% -> 13% of each run, Pallas kernels for 0% -> 0%
where the time goes in v3:
time: 92.3 us; the launch traced here: 91.5 us
  waiting for transfers between devices  24.6 us (27%)
  starting transfers between devices  15 us (16%)
  matrix products  13.7 us (15%)
  blocking collectives  13.7 us (15%)
  Pallas kernels  10.4 us (11%)
  local copies, waits for them, and re-layouts  9.85 us (11%)
  other arithmetic  3.12 us (3%)
  between operations  1.16 us (1%)
    all_to_all x2, waiting for transfers between devices, per_device(): regrouped = lax.all_to_all(outgoing, 'seq', 0, 0, tiled=True)  19.8 us
    all_to_all x1, blocking collectives, per_device(): returned = lax.all_to_all(convolved, 'seq', 0, 0, tiled=True)  13.7 us
    all_to_all x2, starting transfers between devices, per_device(): regrouped = lax.all_to_all(outgoing, 'seq', 0, 0, tiled=True)  11.1 us
    pallas_call x3, Pallas kernels, token_step(): pl.pallas_call(kernel, grid=(1,), in_specs=specs, out_specs=[full(shape)...  10.4 us
    all_to_all x1, waiting for transfers between devices, per_device(): returned = lax.all_to_all(convolved, 'seq', 0, 0, tiled=True)  4.78 us
    unnamed x39, local copies, waits for them, and re-layouts  4.66 us
    dot_general x2, matrix products, filter_values(): hid_two = jnp.sin(jnp.dot(second, hid_one, precision=HIGH))  4.66 us
    dot_general x2, matrix products, filter_values(): hid_one = jnp.sin(jnp.dot(first, feats, precision=HIGH))  4.52 us
  transfers between devices with their start and end apart: 3, of which 3 were waited for; matrix products, arithmetic and copies ran while one was open for 13% of the time, Pallas kernels for 0%

profile of v3, /device:TPU:0, one launch (start us, length us, event | category | flops | bytes accessed | tf_op | source)
XLA Modules:
  0.0 91.5 jit_solution(15480913799493522475)
XLA Ops:
  0.6 1.6 %copy.47 = f32[2,4,256]{1,2,0:T(8,128)} copy(f32[2,4,256]{2,1,0:T(4,128)} %param.33) | data formatting | bytes 16384 | tf_op args[10]
  2.2 2.8 %shard_map.230 = (bf16[7,256,128]{2,1,0:T(8,128)(2,1)}, bf16[4,256,128]{2,1,0:T(8,128)(2,1)}) custom-call(bf16[256,128]{1,0:T(8,128)(2,1)} %refs_0_.3, bf16[3,256,128]{2,1,0:T(8,128)(2,1)} %refs_1_.3, bf16[2,768,256]{2,1,0:T(8,128)(2,1)} %refs_11_.1, bf16[2,768,256]{2,1,0:T(8,128)(2,1)} %refs_12_.1, f32[2,256,4]{2,1,0:T(8,128)} %bitcast.200), custom_call_target="tpu_custom_call" | custom-call | tf_op jit(solution)/shard_map/pallas_call | solution.py:202
  5.0 1.9 %copy.113 = bf16[7,16,16,128]{3,2,0,1:T(8,128)(2,1)} copy(bf16[7,16,16,128]{3,2,1,0:T(8,128)(2,1)} %bitcast.219) | data formatting | bytes 917504 | tf_op jit(solution)/shard_map/reshape | solution.py:260
  6.9 7.5 %all-to-all-start = ((bf16[16,7,16,128]{3,2,1,0:T(8,128)(2,1)}), bf16[16,7,16,128]{3,2,1,0:T(8,128)(2,1)S(1)}, u32[]{:S(2)}, u32[]{:S(2)}) async-start(bf16[16,7,16,128]{3,2,1,0:T(8,128)(2,1)} %bitcast.197), calls=%async_computation | async-start | bytes 917504 | tf_op jit(solution)/shard_map/all_to_all | solution.py:261
  14.4 0.3 fusion.85
  14.9 2.3 %convolution_sine_fusion.3 = f32[2048,64]{0,1:T(8,128)S(1)} fusion(f32[8,2048]{1,0:T(8,128)S(1)} %get-tuple-element.63, f32[8,2048]{1,0:T(8,128)S(1)} %get-tuple-element.62, f32[2,64,16]{1,2,0:T(8,128)S(1)} %copy-done.8), kind=kOutput, calls=%fused_computation.3 | convolution fusion | flops 25198592 | bytes 663552 | tf_op jit(solution)/shard_map/dot_general | solution.py:20
  17.2 2.3 %convolution_sine_fusion.2 = f32[2048,64]{0,1:T(8,128)S(1)} fusion(f32[2048,64]{0,1:T(8,128)S(1)} %convolution_sine_fusion.3, f32[2,64,64]{2,1,0:T(8,128)S(1)} %copy-done.6), kind=kOutput, calls=%fused_computation.2 | convolution fusion | flops 100663296 | bytes 1081344 | tf_op jit(solution)/shard_map/dot_general | solution.py:21
  19.4 0.5 fusion.13
  19.9 0.2 fusion.74
  20.3 0.2 fusion.56
  20.5 7.1 %all-to-all-done = bf16[16,7,16,128]{3,2,1,0:T(8,128)(2,1)S(1)} async-done(((bf16[16,7,16,128]{3,2,1,0:T(8,128)(2,1)}), bf16[16,7,16,128]{3,2,1,0:T(8,128)(2,1)S(1)}, u32[]{:S(2)}, u32[]{:S(2)}) %all-to-all-start) | async-done | bytes 458784 | tf_op jit(solution)/shard_map/all_to_all | solution.py:261
  27.6 0.4 fusion.53
  28.0 0.1 slice_bitcast_fusion.2
  28.1 0.2 copy.70
  28.3 0.2 copy.69
  28.5 0.3 multiply_add_fusion.1
  28.8 0.6 copy-done
  29.4 0.4 fusion.4
  30.2 0.7 copy-done.11
  30.8 0.3 fusion.18
  31.1 0.1 multiply_subtract_fusion.3
  31.4 0.5 copy-done.7
  31.8 0.4 convolution_bitcast_fusion.1
  32.3 0.8 multiply_convert_fusion.1
  33.2 3.9 %all-to-all-start.1 = ((bf16[16,4,16,128]{3,2,1,0:T(8,128)(2,1)}), bf16[16,4,16,128]{3,2,1,0:T(8,128)(2,1)S(1)}, u32[]{:S(2)}, u32[]{:S(2)}) async-start(bf16[16,4,16,128]{3,2,1,0:T(8,128)(2,1)} %multiply_convert_fusion.1), calls=%async_computation.1 | async-start | bytes 524288 | tf_op jit(solution)/shard_map/all_to_all | solution.py:268
  37.1 2.3 %convolution_sine_fusion.1 = f32[64,2048]{1,0:T(8,128)S(1)} fusion(f32[64,16]{0,1:T(8,128)S(1)} %slice_bitcast_fusion.14, f32[8,2048]{1,0:T(8,128)S(1)} %get-tuple-element.63, f32[8,2048]{1,0:T(8,128)S(1)} %get-tuple-element.62), kind=kOutput, calls=%fused_computation.1 | convolution fusion | flops 25198592 | bytes 659456 | tf_op jit(solution)/shard_map/dot_general | solution.py:20
  39.4 2.4 %convolution_sine_fusion = f32[64,2048]{1,0:T(8,128)S(1)} fusion(f32[64,64]{1,0:T(8,128)S(1)} %slice_bitcast_fusion.13, f32[64,2048]{1,0:T(8,128)S(1)} %convolution_sine_fusion.1), kind=kOutput, calls=%fused_computation | convolution fusion | flops 100663296 | bytes 1064960 | tf_op jit(solution)/shard_map/dot_general | solution.py:21
  41.8 0.5 fusion.12
  42.3 4.8 %all-to-all-done.1 = bf16[16,4,16,128]{3,2,1,0:T(8,128)(2,1)S(1)} async-done(((bf16[16,4,16,128]{3,2,1,0:T(8,128)(2,1)}), bf16[16,4,16,128]{3,2,1,0:T(8,128)(2,1)S(1)}, u32[]{:S(2)}, u32[]{:S(2)}) %all-to-all-start.1) | async-done | bytes 262176 | tf_op jit(solution)/shard_map/all_to_all | solution.py:268
  47.1 0.7 copy.53
  47.8 4.3 %shard_map.231 = (bf16[7,256,128]{2,1,0:T(8,128)(2,1)}, bf16[4,256,128]{2,1,0:T(8,128)(2,1)}, f32[256,128]{1,0:T(8,128)}, f32[3,256,128]{2,1,0:T(8,128)}) custom-call(bf16[256,128]{1,0:T(8,128)(2,1)} %refs_0_.3, bf16[3,256,128]{2,1,0:T(8,128)(2,1)} %refs_1_.3, bf16[4,256,128]{2,1,0:T(8,128)(2,1)} %bitcast.215, ...), custom_call_target="tpu_custom_call" | custom-call | tf_op jit(solution)/shard_map/pallas_call | solution.py:202
  52.2 1.8 %copy.112 = bf16[7,16,16,128]{3,2,0,1:T(8,128)(2,1)} copy(bf16[7,16,16,128]{3,2,1,0:T(8,128)(2,1)} %bitcast.218) | data formatting | bytes 917504 | tf_op jit(solution)/shard_map/reshape | solution.py:260
  54.0 3.6 %all-to-all-start.2 = ((bf16[16,7,16,128]{3,2,1,0:T(8,128)(2,1)}), bf16[16,7,16,128]{3,2,1,0:T(8,128)(2,1)S(1)}, u32[]{:S(2)}, u32[]{:S(2)}) async-start(bf16[16,7,16,128]{3,2,1,0:T(8,128)(2,1)} %bitcast.196), calls=%async_computation.2 | async-start | bytes 917504 | tf_op jit(solution)/shard_map/all_to_all | solution.py:261
  57.6 0.2 fusion.71
  57.9 0.2 fusion.60
  58.1 12.7 %all-to-all-done.2 = bf16[16,7,16,128]{3,2,1,0:T(8,128)(2,1)S(1)} async-done(((bf16[16,7,16,128]{3,2,1,0:T(8,128)(2,1)}), bf16[16,7,16,128]{3,2,1,0:T(8,128)(2,1)S(1)}, u32[]{:S(2)}, u32[]{:S(2)}) %all-to-all-start.2) | async-done | bytes 458784 | tf_op jit(solution)/shard_map/all_to_all | solution.py:261
  70.8 0.4 fusion.50
  71.3 0.2 copy.78
  71.5 0.2 copy.77
  71.7 0.3 multiply_add_fusion
  71.9 0.4 fusion.8
  72.7 0.3 fusion.34
  73.0 0.1 multiply_subtract_fusion.2
  73.2 0.4 convolution_bitcast_fusion
  73.7 0.1 multiply_convert_fusion
  73.8 13.7 %all_to_all.20 = bf16[16,4,16,128]{3,2,1,0:T(8,128)(2,1)S(1)} all-to-all(bf16[16,4,16,128]{3,2,1,0:T(8,128)(2,1)S(1)} %multiply_convert_fusion), channel_id=1, replica_groups=mesh['grp'=2,'seq'=16] {'seq'}, dimensions={0} | all-to-all | bytes 524288 | tf_op jit(solution)/shard_map/all_to_all | solution.py:268
  87.5 0.7 copy.59
  88.2 3.3 %shard_map.232 = (bf16[256,128]{1,0:T(8,128)(2,1)}, bf16[3,256,128]{2,1,0:T(8,128)(2,1)}) custom-call(f32[256,128]{1,0:T(8,128)} %get-tuple-element.14.refs_0_, f32[3,256,128]{2,1,0:T(8,128)} %get-tuple-element.15.refs_1_, bf16[4,256,128]{2,1,0:T(8,128)(2,1)} %bitcast.214, bf16[4,256,128]{2,1,0:T(8,128)(2,1)} %get-tuple-element.21.refs_3_, ...), custom_call_target="tpu_custom_call" | custom-call | tf_op jit(solution)/shard_map/pallas_call | solution.py:202
  (52 shorter events, 1.6 us)
Async XLA Ops:
  2.2 12.2 %copy-start.9 = (f32[2,256]{1,0:T(2,128)S(1)}, f32[2,256]{1,0:T(2,128)}, u32[]{:S(2)}) copy-start(f32[2,256]{1,0:T(2,128)} %param.37) | copy-start | bytes 6148
  2.2 12.6 %copy-start.5 = (f32[2,256,64]{1,2,0:T(8,128)S(1)}, f32[2,256,64]{1,2,0:T(8,128)}, u32[]{:S(2)}) copy-start(f32[2,256,64]{1,2,0:T(8,128)} %param.36) | copy-start | bytes 393220
  2.2 12.7 %copy-start.8 = (f32[2,64,16]{1,2,0:T(8,128)S(1)}, f32[2,64,16]{1,2,0:T(8,128)}, u32[]{:S(2)}) copy-start(f32[2,64,16]{1,2,0:T(8,128)} %param.34) | copy-start | bytes 24580
  5.0 12.2 %copy-start.6 = (f32[2,64,64]{2,1,0:T(8,128)S(1)}, f32[2,64,64]{2,1,0:T(8,128)}, u32[]{:S(2)}) copy-start(f32[2,64,64]{2,1,0:T(8,128)} %param.35) | copy-start | bytes 98308
  6.8 13.1 %copy-start.4 = (bf16[32,16]{1,0:T(8,128)(2,1)S(1)}, bf16[32,16]{1,0:T(8,128)(2,1)}, u32[]{:S(2)}) copy-start(bf16[32,16]{1,0:T(8,128)(2,1)} %constant.208) | copy-start | bytes 3076
  6.9 20.8 %all-to-all-start = ((bf16[16,7,16,128]{3,2,1,0:T(8,128)(2,1)}), bf16[16,7,16,128]{3,2,1,0:T(8,128)(2,1)S(1)}, u32[]{:S(2)}, u32[]{:S(2)}) async-start(bf16[16,7,16,128]{3,2,1,0:T(8,128)(2,1)} %bitcast.197), calls=%async_computation | async-start | bytes 917504 | tf_op jit(solution)/shard_map/all_to_all | solution.py:261
  14.9 5.4 %copy-start.2 = (f32[16,128]{1,0:T(8,128)S(1)}, f32[16,128]{1,0:T(8,128)}, u32[]{:S(2)}) copy-start(f32[16,128]{1,0:T(8,128)} %constant.66) | copy-start | bytes 24580
  14.9 5.4 %copy-start.3 = (f32[16,128]{1,0:T(8,128)S(1)}, f32[16,128]{1,0:T(8,128)}, u32[]{:S(2)}) copy-start(f32[16,128]{1,0:T(8,128)} %constant.65) | copy-start | bytes 24580
  17.2 3.1 %copy-start.1 = (bf16[256,256,1]{1,0,2:T(8,128)(2,1)S(1)}, bf16[256,256,1]{1,0,2:T(8,128)(2,1)}, u32[]{:S(2)}) copy-start(bf16[256,256,1]{1,0,2:T(8,128)(2,1)} %constant.209) | copy-start | bytes 393220
  28.5 0.9 copy-start
  29.9 0.9 copy-start.11
  31.1 0.7 copy-start.7
  31.3 1.0 %copy-start.10 = (f32[4]{0:T(128)S(1)}, f32[4]{0:T(128)}, u32[]{:S(2)}) copy-start(f32[4]{0:T(128)} %constant.67) | copy-start | bytes 52
  33.2 13.9 %all-to-all-start.1 = ((bf16[16,4,16,128]{3,2,1,0:T(8,128)(2,1)}), bf16[16,4,16,128]{3,2,1,0:T(8,128)(2,1)S(1)}, u32[]{:S(2)}, u32[]{:S(2)}) async-start(bf16[16,4,16,128]{3,2,1,0:T(8,128)(2,1)} %multiply_convert_fusion.1), calls=%async_computation.1 | async-start | bytes 524288 | tf_op jit(solution)/shard_map/all_to_all | solution.py:268
  54.0 16.8 %all-to-all-start.2 = ((bf16[16,7,16,128]{3,2,1,0:T(8,128)(2,1)}), bf16[16,7,16,128]{3,2,1,0:T(8,128)(2,1)S(1)}, u32[]{:S(2)}, u32[]{:S(2)}) async-start(bf16[16,7,16,128]{3,2,1,0:T(8,128)(2,1)} %bitcast.196), calls=%async_computation.2 | async-start | bytes 917504 | tf_op jit(solution)/shard_map/all_to_all | solution.py:261

commit v4 on v3

--- a/solution.py
+++ b/solution.py
@@ -110,10 +110,12 @@
     return 0.5 * x * (1.0 + jnp.tanh(math.sqrt(2.0 / math.pi) * (x + 0.044715 * (x * x * x))))
 
 
-def token_step(post, pre, arrays, weights):
+def token_step(post, pre, arrays, weights, shards):
     f32, bf16 = jnp.float32, jnp.bfloat16
     state_s, state_v = arrays["state_s"], arrays["state_v"]
     chans, tok = state_s.shape
+    own = chans // shards
+    packed = own % 16 == 0
     full = lambda shape: pl.BlockSpec(shape, lambda i, n=len(shape): (0,) * n)
 
     def layer_spec(w, layer):
@@ -133,7 +135,8 @@
             specs.append(layer_spec(weights[name], pre))
     outs = []
     if pre is not None:
-        outs += [((7, chans, tok), bf16), ((4, chans, tok), bf16)]
+        plane_shape = (shards, 7, own, tok) if packed else (7, chans, tok)
+        outs += [(plane_shape, bf16), ((4, chans, tok), bf16)]
         if post is not None:
             outs += [((chans, tok), f32), ((3, chans, tok), f32)]
     else:
@@ -158,10 +161,14 @@
         if post is not None:
             conv_ref, q_ref = refs.pop(0), refs.pop(0)
             wos, wov, wup, wdn, wmx, wgt, gp = [refs.pop(0) for _ in range(7)]
-            g = gp[...]
+            g = gp[...].T
             qs = q_ref[0].astype(f32)
-            ys = conv_ref[0].astype(f32)
-            yv = [conv_ref[1 + j].astype(f32) for j in range(3)]
+            if packed:
+                planes = [jnp.concatenate([conv_ref[d, p] for d in range(shards)], axis=0) for p in range(4)]
+            else:
+                planes = [conv_ref[p] for p in range(4)]
+            ys = planes[0].astype(f32)
+            yv = [planes[1 + j].astype(f32) for j in range(3)]
             mix = q_ref[1].astype(f32) * yv[0]
             mix = mix + q_ref[2].astype(f32) * yv[1]
             mix = mix + q_ref[3].astype(f32) * yv[2]
@@ -176,18 +183,26 @@
             sv = [sv[j] + mm(wmx[...], mlp_v[j]) * gate for j in range(3)]
         if pre is not None:
             wqs, wqv, gq = [refs.pop(0) for _ in range(3)]
-            g = gq[...]
+            g = gq[...].T
             planes_ref, query_ref = refs.pop(0), refs.pop(0)
+
+            def put(p, value):
+                if packed:
+                    for d in range(shards):
+                        planes_ref[d, p] = value[d * own : (d + 1) * own]
+                else:
+                    planes_ref[p] = value
+
             normed_s = snorm(ss, g[:, 0:1]).astype(bf16)
             normed_v = [v.astype(bf16) for v in vnorm(sv, g[:, 1:2])]
             ps = mm(wqs[...], normed_s)
             query_ref[0] = ps[:chans].astype(bf16)
-            planes_ref[0] = (ps[chans : 2 * chans] * ps[2 * chans :]).astype(bf16)
+            put(0, (ps[chans : 2 * chans] * ps[2 * chans :]).astype(bf16))
             for j in range(3):
                 pv = mm(wqv[...], normed_v[j]).astype(bf16)
                 query_ref[1 + j] = pv[:chans]
-                planes_ref[1 + j] = pv[chans : 2 * chans]
-                planes_ref[4 + j] = pv[2 * chans :]
+                put(1 + j, pv[chans : 2 * chans])
+                put(4 + j, pv[2 * chans :])
             if post is not None:
                 ns_ref, nv_ref = refs.pop(0), refs.pop(0)
                 ns_ref[...] = ss
@@ -252,12 +267,15 @@
         "w_down": w_down,
         "w_mix": w_mix,
         "w_gate": w_gate,
-        "gains_t": gains.transpose(0, 2, 1),
+        "gains_t": gains,
     }
     arrays = {"state_s": scalars, "state_v": vectors}
-    planes, query = token_step(None, 0, arrays, weights)
+    packed = own % 16 == 0
+    planes, query = token_step(None, 0, arrays, weights, shards)
     for layer in range(depth):
-        outgoing = planes.reshape(7, shards, own, tok_local).transpose(1, 0, 2, 3)
+        outgoing = planes
+        if not packed:
+            outgoing = planes.reshape(7, shards, own, tok_local).transpose(1, 0, 2, 3)
         regrouped = lax.all_to_all(outgoing, "seq", 0, 0, tiled=True)
         convolved = convolve(regrouped, spec_next, tables)
         if layer + 1 < depth:
@@ -266,13 +284,15 @@
             )
             spec_next = filter_spec(*tied[:4])
         returned = lax.all_to_all(convolved, "seq", 0, 0, tiled=True)
-        arrays["conv"] = returned.transpose(1, 0, 2, 3).reshape(4, chans, tok_local)
+        arrays["conv"] = returned
+        if not packed:
+            arrays["conv"] = returned.transpose(1, 0, 2, 3).reshape(4, chans, tok_local)
         arrays["query"] = query
         if layer + 1 < depth:
-            planes, query, new_s, new_v = token_step(layer, layer + 1, arrays, weights)
+            planes, query, new_s, new_v = token_step(layer, layer + 1, arrays, weights, shards)
             arrays["state_s"], arrays["state_v"] = new_s, new_v
         else:
-            return tuple(token_step(layer, None, arrays, weights))
+            return tuple(token_step(layer, None, arrays, weights, shards))
 
 
 def solution(mesh):

time: 92.3 us -> 86.6 us (0.938)
  local copies, waits for them, and re-layouts: 9.85 us -> 3.89 us
  matrix products: 13.7 us -> 19 us
  waiting for transfers between devices: 24.6 us -> 19.5 us
    all_to_all x2, waiting for transfers between devices: 19.8 us -> 14.7 us  [per_device(): regrouped = lax.all_to_all(outgoing, 'seq', 0, 0, tiled=True)]
    reshape x2 -> x0, local copies, waits for them, and re-layouts: 3.7 us -> none  [per_device(): outgoing = planes.reshape(7, shards, own, tok_local).transpose(1, 0, 2, 3)]
    dot_general x2, matrix products: 4.52 us -> 7.09 us  [filter_values(): hid_one = jnp.sin(jnp.dot(first, feats, precision=HIGH))]
    dot_general x2, matrix products: 4.66 us -> 6.57 us  [filter_values(): hid_two = jnp.sin(jnp.dot(second, hid_one, precision=HIGH))]
    transpose x2 -> x0, local copies, waits for them, and re-layouts: 1.44 us -> none  [per_device(): arrays['conv'] = returned.transpose(1, 0, 2, 3).reshape(4, chans, tok_local)]
    unnamed x39 -> x40, local copies, waits for them, and re-layouts: 4.66 us -> 3.84 us
  transfers between devices with their start and end apart: 3 -> 3, of which waited for: 3 -> 3; matrix products, arithmetic and copies ran while one was open for 13% -> 19% of each run, Pallas kernels for 0% -> 0%
where the time goes in v4:
time: 86.6 us; the launch traced here: 86 us
  waiting for transfers between devices  19.5 us (23%)
  matrix products  19 us (22%)
  starting transfers between devices  14.9 us (17%)
  blocking collectives  13.8 us (16%)
  Pallas kernels  10.6 us (12%)
  local copies, waits for them, and re-layouts  3.89 us (4%)
  other arithmetic  3.12 us (4%)
  between operations  1.19 us (1%)
    all_to_all x2, waiting for transfers between devices, per_device(): regrouped = lax.all_to_all(outgoing, 'seq', 0, 0, tiled=True)  14.7 us
    all_to_all x1, blocking collectives, per_device(): returned = lax.all_to_all(convolved, 'seq', 0, 0, tiled=True)  13.8 us
    all_to_all x2, starting transfers between devices, per_device(): regrouped = lax.all_to_all(outgoing, 'seq', 0, 0, tiled=True)  10.9 us
    pallas_call x3, Pallas kernels, token_step(): pl.pallas_call(kernel, grid=(1,), in_specs=specs, out_specs=[full(shape)...  10.6 us
    dot_general x2, matrix products, filter_values(): hid_one = jnp.sin(jnp.dot(first, feats, precision=HIGH))  7.09 us
    dot_general x2, matrix products, filter_values(): hid_two = jnp.sin(jnp.dot(second, hid_one, precision=HIGH))  6.57 us
    all_to_all x1, waiting for transfers between devices, per_device(): returned = lax.all_to_all(convolved, 'seq', 0, 0, tiled=True)  4.77 us
    all_to_all x1, starting transfers between devices, per_device(): returned = lax.all_to_all(convolved, 'seq', 0, 0, tiled=True)  3.99 us
  transfers between devices with their start and end apart: 3, of which 3 were waited for; matrix products, arithmetic and copies ran while one was open for 19% of the time, Pallas kernels for 0%

profile of v4, /device:TPU:0, one launch (start us, length us, event | category | flops | bytes accessed | tf_op | source)
XLA Modules:
  0.0 86.0 jit_solution(10226711355332378270)
XLA Ops:
  0.7 2.9 %shard_map.230 = (bf16[16,7,16,128]{3,2,1,0:T(8,128)(2,1)}, bf16[4,256,128]{2,1,0:T(8,128)(2,1)}) custom-call(bf16[256,128]{1,0:T(8,128)(2,1)} %refs_0_.3, bf16[3,256,128]{2,1,0:T(8,128)(2,1)} %refs_1_.3, bf16[2,768,256]{2,1,0:T(8,128)(2,1)} %refs_11_.1, bf16[2,768,256]{2,1,0:T(8,128)(2,1)} %refs_12_.1, f32[2,4,256]{2,1,0:T(4,128)} %refs_10_.3), custom_call_target="tpu_custom_call" | custom-call | tf_op jit(solution)/shard_map/pallas_call | solution.py:217
  3.6 7.4 %all-to-all-start = ((bf16[16,7,16,128]{3,2,1,0:T(8,128)(2,1)}), bf16[16,7,16,128]{3,2,1,0:T(8,128)(2,1)S(1)}, u32[]{:S(2)}, u32[]{:S(2)}) async-start(bf16[16,7,16,128]{3,2,1,0:T(8,128)(2,1)} %get-tuple-element.12), calls=%async_computation | async-start | bytes 917504 | tf_op jit(solution)/shard_map/all_to_all | solution.py:279
  11.0 0.3 fusion.85
  11.5 4.8 %convolution_sine_fusion.1 = f32[2048,64]{1,0:T(8,128)S(1)} fusion(f32[8,2048]{1,0:T(8,128)S(1)} %get-tuple-element.63, f32[8,2048]{1,0:T(8,128)S(1)} %get-tuple-element.62, f32[2,64,16]{1,2,0:T(8,128)S(1)} %copy-done.9), kind=kOutput, calls=%fused_computation.1 | convolution fusion | flops 25198592 | bytes 663552 | tf_op jit(solution)/shard_map/dot_general | solution.py:20
  16.3 4.2 %convolution_sine_fusion = f32[2048,64]{1,0:T(8,128)S(1)} fusion(f32[2048,64]{1,0:T(8,128)S(1)} %convolution_sine_fusion.1, f32[2,64,64]{2,1,0:T(8,128)S(1)} %copy-done.7), kind=kOutput, calls=%fused_computation | convolution fusion | flops 100663296 | bytes 1605632 | tf_op jit(solution)/shard_map/dot_general | solution.py:21
  20.5 1.1 %fusion.12 = bf16[2,16,8,128]{3,2,1,0:T(8,128)(2,1)S(1)} fusion(f32[2048,64]{1,0:T(8,128)S(1)} %convolution_sine_fusion, f32[2048]{0:T(1024)S(1)} %iota_convert_fusion, f32[16]{0:T(128)S(1)} %fusion.92, f32[1,256,64]{1,2,0:T(8,128)S(1)} %get-tuple-element.59, s32[]{:T(128)S(6)} %select_n.17), kind=kOutput, calls=%fused_computation.20 | convolution fusion | flops 25329664 | bytes 1155588 | tf_op jit(solution)/shard_map/dot_general | solution.py:22
  21.6 0.2 fusion.74
  22.0 0.2 fusion.56
  22.2 2.0 %all-to-all-done = bf16[16,7,16,128]{3,2,1,0:T(8,128)(2,1)S(1)} async-done(((bf16[16,7,16,128]{3,2,1,0:T(8,128)(2,1)}), bf16[16,7,16,128]{3,2,1,0:T(8,128)(2,1)S(1)}, u32[]{:S(2)}, u32[]{:S(2)}) %all-to-all-start) | async-done | bytes 458784 | tf_op jit(solution)/shard_map/all_to_all | solution.py:279
  24.2 0.4 fusion.53
  24.6 0.1 slice_bitcast_fusion.2
  24.7 0.2 copy.49
  24.9 0.2 copy.48
  25.1 0.3 multiply_add_fusion.1
  25.4 0.6 copy-done.1
  26.0 0.6 fusion.4
  26.6 0.1 subtract_subtract_fusion.5
  26.7 0.1 add_subtract_fusion.5
  27.0 0.7 copy-done.12
  27.6 0.3 fusion.18
  27.9 0.1 multiply_subtract_fusion.3
  28.2 0.5 copy-done.8
  28.6 0.4 convolution_bitcast_fusion.1
  29.1 0.8 multiply_convert_fusion.1
  30.0 4.0 %all-to-all-start.1 = ((bf16[16,4,16,128]{3,2,1,0:T(8,128)(2,1)}), bf16[16,4,16,128]{3,2,1,0:T(8,128)(2,1)S(1)}, u32[]{:S(2)}, u32[]{:S(2)}) async-start(bf16[16,4,16,128]{3,2,1,0:T(8,128)(2,1)} %multiply_convert_fusion.1), calls=%async_computation.1 | async-start | bytes 524288 | tf_op jit(solution)/shard_map/all_to_all | solution.py:286
  34.0 2.3 %convolution_sine_fusion.3 = f32[64,2048]{1,0:T(8,128)S(1)} fusion(f32[64,16]{0,1:T(8,128)S(1)} %slice_bitcast_fusion.14, f32[8,2048]{1,0:T(8,128)S(1)} %get-tuple-element.63, f32[8,2048]{1,0:T(8,128)S(1)} %get-tuple-element.62), kind=kOutput, calls=%fused_computation.3 | convolution fusion | flops 25198592 | bytes 659456 | tf_op jit(solution)/shard_map/dot_general | solution.py:20
  36.3 2.4 %convolution_sine_fusion.2 = f32[64,2048]{1,0:T(8,128)S(1)} fusion(f32[64,64]{1,0:T(8,128)S(1)} %slice_bitcast_fusion.13, f32[64,2048]{1,0:T(8,128)S(1)} %convolution_sine_fusion.3), kind=kOutput, calls=%fused_computation.2 | convolution fusion | flops 100663296 | bytes 1064960 | tf_op jit(solution)/shard_map/dot_general | solution.py:21
  38.7 0.5 fusion.13
  39.2 4.8 %all-to-all-done.1.refs_2_ = bf16[16,4,16,128]{3,2,1,0:T(8,128)(2,1)S(1)} async-done(((bf16[16,4,16,128]{3,2,1,0:T(8,128)(2,1)}), bf16[16,4,16,128]{3,2,1,0:T(8,128)(2,1)S(1)}, u32[]{:S(2)}, u32[]{:S(2)}) %all-to-all-start.1) | async-done | bytes 262176 | tf_op jit(solution)/shard_map/all_to_all | solution.py:286
  44.0 0.7 copy-done
  44.7 4.3 %shard_map.231 = (bf16[16,7,16,128]{3,2,1,0:T(8,128)(2,1)}, bf16[4,256,128]{2,1,0:T(8,128)(2,1)}, f32[256,128]{1,0:T(8,128)}, f32[3,256,128]{2,1,0:T(8,128)}) custom-call(bf16[256,128]{1,0:T(8,128)(2,1)} %refs_0_.3, bf16[3,256,128]{2,1,0:T(8,128)(2,1)} %refs_1_.3, bf16[16,4,16,128]{3,2,1,0:T(8,128)(2,1)} %copy-done, ...), custom_call_target="tpu_custom_call" | custom-call | tf_op jit(solution)/shard_map/pallas_call | solution.py:217
  49.0 3.6 %all-to-all-start.2 = ((bf16[16,7,16,128]{3,2,1,0:T(8,128)(2,1)}), bf16[16,7,16,128]{3,2,1,0:T(8,128)(2,1)S(1)}, u32[]{:S(2)}, u32[]{:S(2)}) async-start(bf16[16,7,16,128]{3,2,1,0:T(8,128)(2,1)} %get-tuple-element.16), calls=%async_computation.2 | async-start | bytes 917504 | tf_op jit(solution)/shard_map/all_to_all | solution.py:279
  52.6 0.2 fusion.71
  52.9 0.2 fusion.60
  53.1 12.7 %all-to-all-done.2 = bf16[16,7,16,128]{3,2,1,0:T(8,128)(2,1)S(1)} async-done(((bf16[16,7,16,128]{3,2,1,0:T(8,128)(2,1)}), bf16[16,7,16,128]{3,2,1,0:T(8,128)(2,1)S(1)}, u32[]{:S(2)}, u32[]{:S(2)}) %all-to-all-start.2) | async-done | bytes 458784 | tf_op jit(solution)/shard_map/all_to_all | solution.py:279
  65.8 0.4 fusion.50
  66.2 0.1 slice_bitcast_fusion
  66.3 0.2 copy.57
  66.5 0.2 copy.56
  66.7 0.3 multiply_add_fusion
  67.0 0.4 fusion.8
  67.4 0.1 subtract_subtract_fusion.2
  67.7 0.3 fusion.34
  68.0 0.1 multiply_subtract_fusion.2
  68.2 0.4 convolution_bitcast_fusion
  68.7 0.1 multiply_convert_fusion
  68.9 13.8 %all_to_all.20.refs_2_ = bf16[16,4,16,128]{3,2,1,0:T(8,128)(2,1)} all-to-all(bf16[16,4,16,128]{3,2,1,0:T(8,128)(2,1)S(1)} %multiply_convert_fusion), channel_id=1, replica_groups=mesh['grp'=2,'seq'=16] {'seq'}, dimensions={0} | all-to-all | bytes 524288 | tf_op jit(solution)/shard_map/all_to_all | solution.py:286
  82.6 3.3 %shard_map.232 = (bf16[256,128]{1,0:T(8,128)(2,1)}, bf16[3,256,128]{2,1,0:T(8,128)(2,1)}) custom-call(f32[256,128]{1,0:T(8,128)} %get-tuple-element.14.refs_0_, f32[3,256,128]{2,1,0:T(8,128)} %get-tuple-element.15.refs_1_, bf16[16,4,16,128]{3,2,1,0:T(8,128)(2,1)} %all_to_all.20.refs_2_, bf16[4,256,128]{2,1,0:T(8,128)(2,1)} %get-tuple-element.21.refs_3_, ...), custom_call_target="tpu_custom_call" | custom-call | tf_op jit(solution)/shard_map/pallas_call | solution.py:217
  (49 shorter events, 1.2 us)
Async XLA Ops:
  0.6 10.4 %copy-start.10 = (f32[2,256]{1,0:T(2,128)S(1)}, f32[2,256]{1,0:T(2,128)}, u32[]{:S(2)}) copy-start(f32[2,256]{1,0:T(2,128)} %param.37) | copy-start | bytes 6148
  0.6 10.7 %copy-start.6 = (f32[2,256,64]{1,2,0:T(8,128)S(1)}, f32[2,256,64]{1,2,0:T(8,128)}, u32[]{:S(2)}) copy-start(f32[2,256,64]{1,2,0:T(8,128)} %param.36) | copy-start | bytes 393220
  0.7 10.8 %copy-start.9 = (f32[2,64,16]{1,2,0:T(8,128)S(1)}, f32[2,64,16]{1,2,0:T(8,128)}, u32[]{:S(2)}) copy-start(f32[2,64,16]{1,2,0:T(8,128)} %param.34) | copy-start | bytes 24580
  0.7 15.7 %copy-start.7 = (f32[2,64,64]{2,1,0:T(8,128)S(1)}, f32[2,64,64]{2,1,0:T(8,128)}, u32[]{:S(2)}) copy-start(f32[2,64,64]{2,1,0:T(8,128)} %param.35) | copy-start | bytes 98308
  3.6 20.6 %all-to-all-start = ((bf16[16,7,16,128]{3,2,1,0:T(8,128)(2,1)}), bf16[16,7,16,128]{3,2,1,0:T(8,128)(2,1)S(1)}, u32[]{:S(2)}, u32[]{:S(2)}) async-start(bf16[16,7,16,128]{3,2,1,0:T(8,128)(2,1)} %get-tuple-element.12), calls=%async_computation | async-start | bytes 917504 | tf_op jit(solution)/shard_map/all_to_all | solution.py:279
  16.3 5.3 %copy-start.5 = (bf16[32,16]{1,0:T(8,128)(2,1)S(1)}, bf16[32,16]{1,0:T(8,128)(2,1)}, u32[]{:S(2)}) copy-start(bf16[32,16]{1,0:T(8,128)(2,1)} %constant.208) | copy-start | bytes 3076
  20.5 1.4 %copy-start.3 = (f32[16,128]{1,0:T(8,128)S(1)}, f32[16,128]{1,0:T(8,128)}, u32[]{:S(2)}) copy-start(f32[16,128]{1,0:T(8,128)} %constant.66) | copy-start | bytes 24580
  20.5 1.4 %copy-start.4 = (f32[16,128]{1,0:T(8,128)S(1)}, f32[16,128]{1,0:T(8,128)}, u32[]{:S(2)}) copy-start(f32[16,128]{1,0:T(8,128)} %constant.65) | copy-start | bytes 24580
  20.5 1.5 %copy-start.2 = (bf16[256,256,1]{1,0,2:T(8,128)(2,1)S(1)}, bf16[256,256,1]{1,0,2:T(8,128)(2,1)}, u32[]{:S(2)}) copy-start(bf16[256,256,1]{1,0,2:T(8,128)(2,1)} %constant.209) | copy-start | bytes 393220
  25.1 0.9 %copy-start.1 = (bf16[256,256,1,1]{1,0,3,2:T(8,128)(2,1)S(1)}, bf16[256,256,1,1]{1,0,3,2:T(8,128)(2,1)}, u32[]{:S(2)}) copy-start(bf16[256,256,1,1]{1,0,3,2:T(8,128)(2,1)} %constant.207) | copy-start | bytes 393220
  26.7 0.9 %copy-start.12 = (bf16[256,256,1,1]{1,0,3,2:T(8,128)(2,1)S(1)}, bf16[256,256,1,1]{1,0,3,2:T(8,128)(2,1)}, u32[]{:S(2)}) copy-start(bf16[256,256,1,1]{1,0,3,2:T(8,128)(2,1)} %constant.206) | copy-start | bytes 393220
  27.9 0.7 copy-start.8
  28.1 1.0 %copy-start.11 = (f32[4]{0:T(128)S(1)}, f32[4]{0:T(128)}, u32[]{:S(2)}) copy-start(f32[4]{0:T(128)} %constant.67) | copy-start | bytes 52
  30.0 14.0 %all-to-all-start.1 = ((bf16[16,4,16,128]{3,2,1,0:T(8,128)(2,1)}), bf16[16,4,16,128]{3,2,1,0:T(8,128)(2,1)S(1)}, u32[]{:S(2)}, u32[]{:S(2)}) async-start(bf16[16,4,16,128]{3,2,1,0:T(8,128)(2,1)} %multiply_convert_fusion.1), calls=%async_computation.1 | async-start | bytes 524288 | tf_op jit(solution)/shard_map/all_to_all | solution.py:286
  44.0 0.7 copy-start
  49.0 16.8 %all-to-all-start.2 = ((bf16[16,7,16,128]{3,2,1,0:T(8,128)(2,1)}), bf16[16,7,16,128]{3,2,1,0:T(8,128)(2,1)S(1)}, u32[]{:S(2)}, u32[]{:S(2)}) async-start(bf16[16,7,16,128]{3,2,1,0:T(8,128)(2,1)} %get-tuple-element.16), calls=%async_computation.2 | async-start | bytes 917504 | tf_op jit(solution)/shard_map/all_to_all | solution.py:279

commit v5 on v4

--- a/solution.py
+++ b/solution.py
@@ -51,19 +51,21 @@
     lane_fwd = np.block([[cos_l, -sin_l], [sin_l, cos_l]])
     lane_inv = np.block([[cos_l, sin_l], [-sin_l, cos_l]])
     f32 = lambda v: jnp.asarray(v, dtype=jnp.float32)
-    return tuple(f32(v) for v in (lead_fwd, lead_inv, tw_c, tw_s, lane_fwd, lane_inv))
+    bf16 = lambda v: jnp.asarray(v, dtype=jnp.bfloat16)
+    return (bf16(lead_fwd), bf16(lead_inv), f32(tw_c), f32(tw_s), bf16(lane_fwd), bf16(lane_inv))
 
 
 def forward_dft(field, tables, prec):
     lead_fwd, _, tw_c, tw_s, lane_fwd, _ = tables
     shards, planes, chans, local = field.shape
-    stage = jnp.dot(lead_fwd, field.reshape(shards, -1), precision=prec)
+    flat = field.reshape(shards, -1).astype(jnp.bfloat16)
+    stage = jnp.dot(lead_fwd, flat, preferred_element_type=jnp.float32)
     stage = stage.reshape(2 * shards, planes, chans, local)
     st_r, st_i = stage[:shards], stage[shards:]
     tw_r = st_r * tw_c + st_i * tw_s
     tw_i = st_i * tw_c - st_r * tw_s
-    joined = jnp.concatenate([tw_r, tw_i], axis=-1).reshape(-1, 2 * local)
-    spec = jnp.dot(joined, lane_fwd, precision=prec)
+    joined = jnp.concatenate([tw_r, tw_i], axis=-1).reshape(-1, 2 * local).astype(jnp.bfloat16)
+    spec = jnp.dot(joined, lane_fwd, preferred_element_type=jnp.float32)
     return spec.reshape(shards, planes, chans, 2 * local)
 
 
@@ -71,13 +73,14 @@
     _, lead_inv, tw_c, tw_s, _, lane_inv = tables
     shards, planes, chans, width = spec.shape
     local = width // 2
-    back = jnp.dot(spec.reshape(-1, width), lane_inv, precision=prec)
+    flat = spec.reshape(-1, width).astype(jnp.bfloat16)
+    back = jnp.dot(flat, lane_inv, preferred_element_type=jnp.float32)
     back = back.reshape(shards, planes, chans, width)
     bk_r, bk_i = back[..., :local], back[..., local:]
     un_r = bk_r * tw_c - bk_i * tw_s
     un_i = bk_r * tw_s + bk_i * tw_c
-    stacked = jnp.concatenate([un_r, un_i], axis=0).reshape(2 * shards, -1)
-    whole = jnp.dot(lead_inv, stacked, precision=prec)
+    stacked = jnp.concatenate([un_r, un_i], axis=0).reshape(2 * shards, -1).astype(jnp.bfloat16)
+    whole = jnp.dot(lead_inv, stacked, preferred_element_type=jnp.float32)
     return whole.reshape(shards, planes, chans, local)
 
 

time: 86.6 us -> 86.6 us (level)
    another operation x0 -> x12, other arithmetic: none -> 1.47 us
where the time goes in v5:
time: 86.6 us; the launch traced here: 86 us
  waiting for transfers between devices  19.5 us (23%)
  matrix products  19 us (22%)
  starting transfers between devices  14.9 us (17%)
  blocking collectives  13.8 us (16%)
  Pallas kernels  10.6 us (12%)
  local copies, waits for them, and re-layouts  3.89 us (4%)
  other arithmetic  3.12 us (4%)
  between operations  1.19 us (1%)
    all_to_all x2, waiting for transfers between devices, per_device(): regrouped = lax.all_to_all(outgoing, 'seq', 0, 0, tiled=True)  14.7 us
    all_to_all x1, blocking collectives, per_device(): returned = lax.all_to_all(convolved, 'seq', 0, 0, tiled=True)  13.8 us
    all_to_all x2, starting transfers between devices, per_device(): regrouped = lax.all_to_all(outgoing, 'seq', 0, 0, tiled=True)  10.9 us
    pallas_call x3, Pallas kernels, token_step(): pl.pallas_call(kernel, grid=(1,), in_specs=specs, out_specs=[full(shape)...  10.6 us
    dot_general x2, matrix products, filter_values(): hid_one = jnp.sin(jnp.dot(first, feats, precision=HIGH))  7.09 us
    dot_general x2, matrix products, filter_values(): hid_two = jnp.sin(jnp.dot(second, hid_one, precision=HIGH))  6.57 us
    all_to_all x1, waiting for transfers between devices, per_device(): returned = lax.all_to_all(convolved, 'seq', 0, 0, tiled=True)  4.77 us
    all_to_all x1, starting transfers between devices, per_device(): returned = lax.all_to_all(convolved, 'seq', 0, 0, tiled=True)  3.99 us
  transfers between devices with their start and end apart: 3, of which 3 were waited for; matrix products, arithmetic and copies ran while one was open for 19% of the time, Pallas kernels for 0%

profile of v5, /device:TPU:0, one launch (start us, length us, event | category | flops | bytes accessed | tf_op | source)
XLA Modules:
  0.0 86.0 jit_solution(5186840657610594666)
XLA Ops:
  0.7 2.9 %shard_map.230 = (bf16[16,7,16,128]{3,2,1,0:T(8,128)(2,1)}, bf16[4,256,128]{2,1,0:T(8,128)(2,1)}) custom-call(bf16[256,128]{1,0:T(8,128)(2,1)} %refs_0_.3, bf16[3,256,128]{2,1,0:T(8,128)(2,1)} %refs_1_.3, bf16[2,768,256]{2,1,0:T(8,128)(2,1)} %refs_11_.1, bf16[2,768,256]{2,1,0:T(8,128)(2,1)} %refs_12_.1, f32[2,4,256]{2,1,0:T(4,128)} %refs_10_.3), custom_call_target="tpu_custom_call" | custom-call | tf_op jit(solution)/shard_map/pallas_call | solution.py:220
  3.6 7.4 %all-to-all-start = ((bf16[16,7,16,128]{3,2,1,0:T(8,128)(2,1)}), bf16[16,7,16,128]{3,2,1,0:T(8,128)(2,1)S(1)}, u32[]{:S(2)}, u32[]{:S(2)}) async-start(bf16[16,7,16,128]{3,2,1,0:T(8,128)(2,1)} %get-tuple-element.12), calls=%async_computation | async-start | bytes 917504 | tf_op jit(solution)/shard_map/all_to_all | solution.py:282
  11.0 0.3 fusion.93
  11.5 4.8 %convolution_sine_fusion.1 = f32[2048,64]{1,0:T(8,128)S(1)} fusion(f32[8,2048]{1,0:T(8,128)S(1)} %get-tuple-element.63, f32[8,2048]{1,0:T(8,128)S(1)} %get-tuple-element.62, f32[2,64,16]{1,2,0:T(8,128)S(1)} %copy-done.9), kind=kOutput, calls=%fused_computation.1 | convolution fusion | flops 25198592 | bytes 663552 | tf_op jit(solution)/shard_map/dot_general | solution.py:20
  16.3 4.2 %convolution_sine_fusion = f32[2048,64]{1,0:T(8,128)S(1)} fusion(f32[2048,64]{1,0:T(8,128)S(1)} %convolution_sine_fusion.1, f32[2,64,64]{2,1,0:T(8,128)S(1)} %copy-done.7), kind=kOutput, calls=%fused_computation | convolution fusion | flops 100663296 | bytes 1605632 | tf_op jit(solution)/shard_map/dot_general | solution.py:21
  20.5 1.1 %fusion.4 = bf16[2,16,8,128]{3,2,1,0:T(8,128)(2,1)S(1)} fusion(f32[2048,64]{1,0:T(8,128)S(1)} %convolution_sine_fusion, f32[2048]{0:T(1024)S(1)} %iota_convert_fusion, f32[16]{0:T(128)S(1)} %fusion.100, f32[1,256,64]{1,2,0:T(8,128)S(1)} %get-tuple-element.59, s32[]{:T(128)S(6)} %select_n.17), kind=kOutput, calls=%fused_computation.12 | convolution fusion | flops 25329664 | bytes 1155588 | tf_op jit(solution)/shard_map/dot_general | solution.py:22
  21.6 0.2 fusion.82
  22.0 0.2 fusion.64
  22.2 2.0 %all-to-all-done = bf16[16,7,16,128]{3,2,1,0:T(8,128)(2,1)S(1)} async-done(((bf16[16,7,16,128]{3,2,1,0:T(8,128)(2,1)}), bf16[16,7,16,128]{3,2,1,0:T(8,128)(2,1)S(1)}, u32[]{:S(2)}, u32[]{:S(2)}) %all-to-all-start) | async-done | bytes 458784 | tf_op jit(solution)/shard_map/all_to_all | solution.py:282
  24.2 0.4 fusion.53
  24.6 0.1 slice_bitcast_fusion.2
  24.7 0.2 copy.49
  24.9 0.2 copy.48
  25.1 0.3 add_convert_fusion.1
  25.4 0.6 copy-done.1
  26.0 0.6 fusion.6
  26.6 0.1 subtract_convert_fusion.16
  26.7 0.1 subtract_convert_fusion.13
  27.0 0.7 copy-done.12
  27.6 0.3 fusion.18
  27.9 0.1 subtract_convert_fusion.3
  28.2 0.5 copy-done.8
  28.6 0.4 convolution_bitcast_fusion.1
  29.1 0.8 multiply_convert_fusion.1
  30.0 4.0 %all-to-all-start.1 = ((bf16[16,4,16,128]{3,2,1,0:T(8,128)(2,1)}), bf16[16,4,16,128]{3,2,1,0:T(8,128)(2,1)S(1)}, u32[]{:S(2)}, u32[]{:S(2)}) async-start(bf16[16,4,16,128]{3,2,1,0:T(8,128)(2,1)} %multiply_convert_fusion.1), calls=%async_computation.1 | async-start | bytes 524288 | tf_op jit(solution)/shard_map/all_to_all | solution.py:289
  34.0 2.3 %convolution_sine_fusion.3 = f32[64,2048]{1,0:T(8,128)S(1)} fusion(f32[64,16]{0,1:T(8,128)S(1)} %slice_bitcast_fusion.14, f32[8,2048]{1,0:T(8,128)S(1)} %get-tuple-element.63, f32[8,2048]{1,0:T(8,128)S(1)} %get-tuple-element.62), kind=kOutput, calls=%fused_computation.3 | convolution fusion | flops 25198592 | bytes 659456 | tf_op jit(solution)/shard_map/dot_general | solution.py:20
  36.3 2.4 %convolution_sine_fusion.2 = f32[64,2048]{1,0:T(8,128)S(1)} fusion(f32[64,64]{1,0:T(8,128)S(1)} %slice_bitcast_fusion.13, f32[64,2048]{1,0:T(8,128)S(1)} %convolution_sine_fusion.3), kind=kOutput, calls=%fused_computation.2 | convolution fusion | flops 100663296 | bytes 1064960 | tf_op jit(solution)/shard_map/dot_general | solution.py:21
  38.7 0.5 fusion.5
  39.2 4.8 %all-to-all-done.1.refs_2_ = bf16[16,4,16,128]{3,2,1,0:T(8,128)(2,1)S(1)} async-done(((bf16[16,4,16,128]{3,2,1,0:T(8,128)(2,1)}), bf16[16,4,16,128]{3,2,1,0:T(8,128)(2,1)S(1)}, u32[]{:S(2)}, u32[]{:S(2)}) %all-to-all-start.1) | async-done | bytes 262176 | tf_op jit(solution)/shard_map/all_to_all | solution.py:289
  44.0 0.7 copy-done
  44.7 4.3 %shard_map.231 = (bf16[16,7,16,128]{3,2,1,0:T(8,128)(2,1)}, bf16[4,256,128]{2,1,0:T(8,128)(2,1)}, f32[256,128]{1,0:T(8,128)}, f32[3,256,128]{2,1,0:T(8,128)}) custom-call(bf16[256,128]{1,0:T(8,128)(2,1)} %refs_0_.3, bf16[3,256,128]{2,1,0:T(8,128)(2,1)} %refs_1_.3, bf16[16,4,16,128]{3,2,1,0:T(8,128)(2,1)} %copy-done, ...), custom_call_target="tpu_custom_call" | custom-call | tf_op jit(solution)/shard_map/pallas_call | solution.py:220
  49.0 3.6 %all-to-all-start.2 = ((bf16[16,7,16,128]{3,2,1,0:T(8,128)(2,1)}), bf16[16,7,16,128]{3,2,1,0:T(8,128)(2,1)S(1)}, u32[]{:S(2)}, u32[]{:S(2)}) async-start(bf16[16,7,16,128]{3,2,1,0:T(8,128)(2,1)} %get-tuple-element.16), calls=%async_computation.2 | async-start | bytes 917504 | tf_op jit(solution)/shard_map/all_to_all | solution.py:282
  52.6 0.2 fusion.79
  52.9 0.2 fusion.68
  53.1 12.7 %all-to-all-done.2 = bf16[16,7,16,128]{3,2,1,0:T(8,128)(2,1)S(1)} async-done(((bf16[16,7,16,128]{3,2,1,0:T(8,128)(2,1)}), bf16[16,7,16,128]{3,2,1,0:T(8,128)(2,1)S(1)}, u32[]{:S(2)}, u32[]{:S(2)}) %all-to-all-start.2) | async-done | bytes 458784 | tf_op jit(solution)/shard_map/all_to_all | solution.py:282
  65.8 0.4 fusion.50
  66.2 0.1 slice_bitcast_fusion
  66.3 0.2 copy.57
  66.5 0.2 copy.56
  66.7 0.3 add_convert_fusion
  67.0 0.4 fusion.10
  67.4 0.1 subtract_convert_fusion.9
  67.7 0.3 fusion.34
  68.0 0.1 subtract_convert_fusion.2
  68.2 0.4 convolution_bitcast_fusion
  68.7 0.1 multiply_convert_fusion
  68.9 13.8 %all_to_all.20.refs_2_ = bf16[16,4,16,128]{3,2,1,0:T(8,128)(2,1)} all-to-all(bf16[16,4,16,128]{3,2,1,0:T(8,128)(2,1)S(1)} %multiply_convert_fusion), channel_id=1, replica_groups=mesh['grp'=2,'seq'=16] {'seq'}, dimensions={0} | all-to-all | bytes 524288 | tf_op jit(solution)/shard_map/all_to_all | solution.py:289
  82.6 3.3 %shard_map.232 = (bf16[256,128]{1,0:T(8,128)(2,1)}, bf16[3,256,128]{2,1,0:T(8,128)(2,1)}) custom-call(f32[256,128]{1,0:T(8,128)} %get-tuple-element.14.refs_0_, f32[3,256,128]{2,1,0:T(8,128)} %get-tuple-element.15.refs_1_, bf16[16,4,16,128]{3,2,1,0:T(8,128)(2,1)} %all_to_all.20.refs_2_, bf16[4,256,128]{2,1,0:T(8,128)(2,1)} %get-tuple-element.21.refs_3_, ...), custom_call_target="tpu_custom_call" | custom-call | tf_op jit(solution)/shard_map/pallas_call | solution.py:220
  (49 shorter events, 1.2 us)
Async XLA Ops:
  0.6 10.4 %copy-start.10 = (f32[2,256]{1,0:T(2,128)S(1)}, f32[2,256]{1,0:T(2,128)}, u32[]{:S(2)}) copy-start(f32[2,256]{1,0:T(2,128)} %param.37) | copy-start | bytes 6148
  0.6 10.7 %copy-start.6 = (f32[2,256,64]{1,2,0:T(8,128)S(1)}, f32[2,256,64]{1,2,0:T(8,128)}, u32[]{:S(2)}) copy-start(f32[2,256,64]{1,2,0:T(8,128)} %param.36) | copy-start | bytes 393220
  0.7 10.8 %copy-start.9 = (f32[2,64,16]{1,2,0:T(8,128)S(1)}, f32[2,64,16]{1,2,0:T(8,128)}, u32[]{:S(2)}) copy-start(f32[2,64,16]{1,2,0:T(8,128)} %param.34) | copy-start | bytes 24580
  0.7 15.7 %copy-start.7 = (f32[2,64,64]{2,1,0:T(8,128)S(1)}, f32[2,64,64]{2,1,0:T(8,128)}, u32[]{:S(2)}) copy-start(f32[2,64,64]{2,1,0:T(8,128)} %param.35) | copy-start | bytes 98308
  3.6 20.6 %all-to-all-start = ((bf16[16,7,16,128]{3,2,1,0:T(8,128)(2,1)}), bf16[16,7,16,128]{3,2,1,0:T(8,128)(2,1)S(1)}, u32[]{:S(2)}, u32[]{:S(2)}) async-start(bf16[16,7,16,128]{3,2,1,0:T(8,128)(2,1)} %get-tuple-element.12), calls=%async_computation | async-start | bytes 917504 | tf_op jit(solution)/shard_map/all_to_all | solution.py:282
  16.3 5.3 %copy-start.5 = (bf16[32,16]{1,0:T(8,128)(2,1)S(1)}, bf16[32,16]{1,0:T(8,128)(2,1)}, u32[]{:S(2)}) copy-start(bf16[32,16]{1,0:T(8,128)(2,1)} %constant.58.clone) | copy-start | bytes 3076
  20.5 1.4 %copy-start.3 = (f32[16,128]{1,0:T(8,128)S(1)}, f32[16,128]{1,0:T(8,128)}, u32[]{:S(2)}) copy-start(f32[16,128]{1,0:T(8,128)} %constant.66) | copy-start | bytes 24580
  20.5 1.4 %copy-start.4 = (f32[16,128]{1,0:T(8,128)S(1)}, f32[16,128]{1,0:T(8,128)}, u32[]{:S(2)}) copy-start(f32[16,128]{1,0:T(8,128)} %constant.65) | copy-start | bytes 24580
  20.5 1.5 %copy-start.2 = (bf16[256,256,1]{1,0,2:T(8,128)(2,1)S(1)}, bf16[256,256,1]{1,0,2:T(8,128)(2,1)}, u32[]{:S(2)}) copy-start(bf16[256,256,1]{1,0,2:T(8,128)(2,1)} %constant.69) | copy-start | bytes 393220
  25.1 0.9 %copy-start.1 = (bf16[256,256,1,1]{1,0,3,2:T(8,128)(2,1)S(1)}, bf16[256,256,1,1]{1,0,3,2:T(8,128)(2,1)}, u32[]{:S(2)}) copy-start(bf16[256,256,1,1]{1,0,3,2:T(8,128)(2,1)} %constant.68) | copy-start | bytes 393220
  26.7 0.9 %copy-start.12 = (bf16[256,256,1,1]{1,0,3,2:T(8,128)(2,1)S(1)}, bf16[256,256,1,1]{1,0,3,2:T(8,128)(2,1)}, u32[]{:S(2)}) copy-start(bf16[256,256,1,1]{1,0,3,2:T(8,128)(2,1)} %constant.70) | copy-start | bytes 393220
  27.9 0.7 copy-start.8
  28.1 1.0 %copy-start.11 = (f32[4]{0:T(128)S(1)}, f32[4]{0:T(128)}, u32[]{:S(2)}) copy-start(f32[4]{0:T(128)} %constant.67) | copy-start | bytes 52
  30.0 14.0 %all-to-all-start.1 = ((bf16[16,4,16,128]{3,2,1,0:T(8,128)(2,1)}), bf16[16,4,16,128]{3,2,1,0:T(8,128)(2,1)S(1)}, u32[]{:S(2)}, u32[]{:S(2)}) async-start(bf16[16,4,16,128]{3,2,1,0:T(8,128)(2,1)} %multiply_convert_fusion.1), calls=%async_computation.1 | async-start | bytes 524288 | tf_op jit(solution)/shard_map/all_to_all | solution.py:289
  44.0 0.7 copy-start
  49.0 16.8 %all-to-all-start.2 = ((bf16[16,7,16,128]{3,2,1,0:T(8,128)(2,1)}), bf16[16,7,16,128]{3,2,1,0:T(8,128)(2,1)S(1)}, u32[]{:S(2)}, u32[]{:S(2)}) async-start(bf16[16,7,16,128]{3,2,1,0:T(8,128)(2,1)} %get-tuple-element.16), calls=%async_computation.2 | async-start | bytes 917504 | tf_op jit(solution)/shard_map/all_to_all | solution.py:282

commit v6 on v5

--- a/solution.py
+++ b/solution.py
@@ -38,21 +38,32 @@
 
 def make_tables(shards, local):
     length = shards * local
-    a = np.arange(shards)
-    ang_s = 2.0 * np.pi * np.outer(a, a) / shards
-    lead_fwd = np.concatenate([np.cos(ang_s), -np.sin(ang_s)], axis=0)
-    lead_inv = np.concatenate([np.cos(ang_s), -np.sin(ang_s)], axis=1)
-    b = np.arange(local)
-    ang_t = 2.0 * np.pi * np.outer(a, b) / length
-    tw_c = np.cos(ang_t)[:, None, None, :]
-    tw_s = np.sin(ang_t)[:, None, None, :]
-    ang_l = 2.0 * np.pi * np.outer(b, b) / local
-    cos_l, sin_l = np.cos(ang_l), np.sin(ang_l)
-    lane_fwd = np.block([[cos_l, -sin_l], [sin_l, cos_l]])
-    lane_inv = np.block([[cos_l, sin_l], [-sin_l, cos_l]])
-    f32 = lambda v: jnp.asarray(v, dtype=jnp.float32)
-    bf16 = lambda v: jnp.asarray(v, dtype=jnp.bfloat16)
-    return (bf16(lead_fwd), bf16(lead_inv), f32(tw_c), f32(tw_s), bf16(lane_fwd), bf16(lane_inv))
+    f32, bf16 = jnp.float32, jnp.bfloat16
+
+    def turns(rows, cols, period):
+        rows = jnp.arange(rows, dtype=jnp.int32)[:, None]
+        cols = jnp.arange(cols, dtype=jnp.int32)[None, :]
+        return ((rows * cols) % period).astype(f32) * (2.0 * math.pi / period)
+
+    ang_s = turns(shards, shards, shards)
+    cos_s, sin_s = jnp.cos(ang_s), jnp.sin(ang_s)
+    lead_fwd = jnp.concatenate([cos_s, -sin_s], axis=0)
+    lead_inv = jnp.concatenate([cos_s, -sin_s], axis=1)
+    ang_t = turns(shards, local, length)
+    tw_c = jnp.cos(ang_t)[:, None, None, :]
+    tw_s = jnp.sin(ang_t)[:, None, None, :]
+    ang_l = turns(local, local, local)
+    cos_l, sin_l = jnp.cos(ang_l), jnp.sin(ang_l)
+    lane_fwd = jnp.block([[cos_l, -sin_l], [sin_l, cos_l]])
+    lane_inv = jnp.block([[cos_l, sin_l], [-sin_l, cos_l]])
+    return (
+        lead_fwd.astype(bf16),
+        lead_inv.astype(bf16),
+        tw_c,
+        tw_s,
+        lane_fwd.astype(bf16),
+        lane_inv.astype(bf16),
+    )
 
 
 def forward_dft(field, tables, prec):

time: 86.6 us -> 86.1 us (level)
  local copies, waits for them, and re-layouts: 3.89 us -> 2.98 us
    all_to_all x2, waiting for transfers between devices: 14.7 us -> 13.7 us  [per_device(): regrouped = lax.all_to_all(outgoing, 'seq', 0, 0, tiled=True)]
    unnamed x40 -> x28, local copies, waits for them, and re-layouts: 3.84 us -> 2.93 us
    another operation x12 -> x15, other arithmetic: 1.47 us -> 2.08 us
  transfers between devices with their start and end apart: 3 -> 3, of which waited for: 3 -> 3; matrix products, arithmetic and copies ran while one was open for 19% -> 20% of each run, Pallas kernels for 0% -> 0%
where the time goes in v6:
time: 86.1 us; the launch traced here: 85.6 us
  matrix products  18.9 us (22%)
  waiting for transfers between devices  18.9 us (22%)
  starting transfers between devices  15.5 us (18%)
  blocking collectives  13.8 us (16%)
  Pallas kernels  10.6 us (12%)
  other arithmetic  3.91 us (5%)
  local copies, waits for them, and re-layouts  2.98 us (3%)
  between operations  1.14 us (1%)
    all_to_all x1, blocking collectives, per_device(): returned = lax.all_to_all(convolved, 'seq', 0, 0, tiled=True)  13.8 us
    all_to_all x2, waiting for transfers between devices, per_device(): regrouped = lax.all_to_all(outgoing, 'seq', 0, 0, tiled=True)  13.7 us
    all_to_all x2, starting transfers between devices, per_device(): regrouped = lax.all_to_all(outgoing, 'seq', 0, 0, tiled=True)  10.9 us
    pallas_call x3, Pallas kernels, token_step(): pl.pallas_call(kernel, grid=(1,), in_specs=specs, out_specs=[full(shape)...  10.6 us
    dot_general x2, matrix products, filter_values(): hid_one = jnp.sin(jnp.dot(first, feats, precision=HIGH))  7.09 us
    dot_general x2, matrix products, filter_values(): hid_two = jnp.sin(jnp.dot(second, hid_one, precision=HIGH))  6.59 us
    all_to_all x1, waiting for transfers between devices, per_device(): returned = lax.all_to_all(convolved, 'seq', 0, 0, tiled=True)  5.25 us
    all_to_all x1, starting transfers between devices, per_device(): returned = lax.all_to_all(convolved, 'seq', 0, 0, tiled=True)  4.54 us
  transfers between devices with their start and end apart: 3, of which 3 were waited for; matrix products, arithmetic and copies ran while one was open for 20% of the time, Pallas kernels for 0%

profile of v6, /device:TPU:0, one launch (start us, length us, event | category | flops | bytes accessed | tf_op | source)
XLA Modules:
  0.0 85.6 jit_solution(1239608462964563902)
XLA Ops:
  0.7 2.9 %shard_map.176 = (bf16[16,7,16,128]{3,2,1,0:T(8,128)(2,1)}, bf16[4,256,128]{2,1,0:T(8,128)(2,1)}) custom-call(bf16[256,128]{1,0:T(8,128)(2,1)} %refs_0_.3, bf16[3,256,128]{2,1,0:T(8,128)(2,1)} %refs_1_.3, bf16[2,768,256]{2,1,0:T(8,128)(2,1)} %refs_11_.1, bf16[2,768,256]{2,1,0:T(8,128)(2,1)} %refs_12_.1, f32[2,4,256]{2,1,0:T(4,128)} %refs_10_.3), custom_call_target="tpu_custom_call" | custom-call | tf_op jit(solution)/shard_map/pallas_call | solution.py:231
  3.6 7.4 %all-to-all-start = ((bf16[16,7,16,128]{3,2,1,0:T(8,128)(2,1)}), bf16[16,7,16,128]{3,2,1,0:T(8,128)(2,1)S(1)}, u32[]{:S(2)}, u32[]{:S(2)}) async-start(bf16[16,7,16,128]{3,2,1,0:T(8,128)(2,1)} %get-tuple-element.12), calls=%async_computation | async-start | bytes 917504 | tf_op jit(solution)/shard_map/all_to_all | solution.py:293
  11.1 0.3 fusion.113
  11.3 0.3 negate_convert_fusion
  11.6 0.3 fusion.110
  12.1 4.8 %convolution_sine_fusion.1 = f32[2048,64]{1,0:T(8,128)S(1)} fusion(f32[8,2048]{1,0:T(8,128)S(1)} %get-tuple-element.63, f32[8,2048]{1,0:T(8,128)S(1)} %get-tuple-element.62, f32[2,64,16]{1,2,0:T(8,128)S(1)} %copy-done.3), kind=kOutput, calls=%fused_computation.1 | convolution fusion | flops 25198592 | bytes 663552 | tf_op jit(solution)/shard_map/dot_general | solution.py:20
  16.9 4.2 %convolution_sine_fusion = f32[2048,64]{1,0:T(8,128)S(1)} fusion(f32[2048,64]{1,0:T(8,128)S(1)} %convolution_sine_fusion.1, f32[2,64,64]{2,1,0:T(8,128)S(1)} %copy-done.2), kind=kOutput, calls=%fused_computation | convolution fusion | flops 100663296 | bytes 1605632 | tf_op jit(solution)/shard_map/dot_general | solution.py:21
  21.1 1.1 %fusion.4 = bf16[2,16,8,128]{3,2,1,0:T(8,128)(2,1)S(1)} fusion(f32[2048,64]{1,0:T(8,128)S(1)} %convolution_sine_fusion, f32[2048]{0:T(1024)S(1)} %iota_convert_fusion, f32[16]{0:T(128)S(1)} %fusion.133, f32[1,256,64]{1,2,0:T(8,128)S(1)} %get-tuple-element.59, s32[]{:T(128)S(6)} %select_n.108), kind=kOutput, calls=%fused_computation.10 | convolution fusion | flops 25329664 | bytes 1155588 | tf_op jit(solution)/shard_map/dot_general | solution.py:22
  22.2 0.2 fusion.96
  22.6 0.2 fusion.69
  22.8 1.4 %all-to-all-done = bf16[16,7,16,128]{3,2,1,0:T(8,128)(2,1)S(1)} async-done(((bf16[16,7,16,128]{3,2,1,0:T(8,128)(2,1)}), bf16[16,7,16,128]{3,2,1,0:T(8,128)(2,1)S(1)}, u32[]{:S(2)}, u32[]{:S(2)}) %all-to-all-start) | async-done | bytes 458784 | tf_op jit(solution)/shard_map/all_to_all | solution.py:293
  24.2 0.4 fusion.55
  24.6 0.1 slice_bitcast_fusion.2
  24.7 0.4 copy.50
  25.1 0.2 copy.49
  25.3 0.3 add_convert_fusion.1
  25.6 0.4 fusion.6
  26.3 0.3 fusion.14
  26.6 0.1 subtract_convert_fusion.3
  26.8 0.3 copy.95
  27.2 0.1 copy.55
  27.3 0.4 fusion.50
  27.7 0.9 %fusion.49 = bf16[16,4,16,128]{3,2,1,0:T(8,128)(2,1)} fusion(f32[16,4,16,128]{3,0,2,1:T(8,128)S(1)} %fusion.50, f32[4]{0:T(128)S(1)} %copy-done.5), kind=kLoop, calls=%fused_computation.69 | loop fusion | flops 262144 | bytes 786448 | tf_op jit(solution)/shard_map/convert_element_type | solution.py:120
  28.6 4.5 %all-to-all-start.1 = ((bf16[16,4,16,128]{3,2,1,0:T(8,128)(2,1)}), bf16[16,4,16,128]{3,2,1,0:T(8,128)(2,1)S(1)}, u32[]{:S(2)}, u32[]{:S(2)}) async-start(bf16[16,4,16,128]{3,2,1,0:T(8,128)(2,1)} %fusion.49), calls=%async_computation.1 | async-start | bytes 524288 | tf_op jit(solution)/shard_map/all_to_all | solution.py:300
  33.2 2.3 %convolution_sine_fusion.3 = f32[64,2048]{1,0:T(8,128)S(1)} fusion(f32[64,16]{0,1:T(8,128)S(1)} %slice_bitcast_fusion.14, f32[8,2048]{1,0:T(8,128)S(1)} %get-tuple-element.63, f32[8,2048]{1,0:T(8,128)S(1)} %get-tuple-element.62), kind=kOutput, calls=%fused_computation.3 | convolution fusion | flops 25198592 | bytes 659456 | tf_op jit(solution)/shard_map/dot_general | solution.py:20
  35.5 2.4 %convolution_sine_fusion.2 = f32[64,2048]{1,0:T(8,128)S(1)} fusion(f32[64,64]{1,0:T(8,128)S(1)} %slice_bitcast_fusion.13, f32[64,2048]{1,0:T(8,128)S(1)} %convolution_sine_fusion.3), kind=kOutput, calls=%fused_computation.2 | convolution fusion | flops 100663296 | bytes 1064960 | tf_op jit(solution)/shard_map/dot_general | solution.py:21
  38.0 5.3 %all-to-all-done.1.refs_2_ = bf16[16,4,16,128]{3,2,1,0:T(8,128)(2,1)S(1)} async-done(((bf16[16,4,16,128]{3,2,1,0:T(8,128)(2,1)}), bf16[16,4,16,128]{3,2,1,0:T(8,128)(2,1)S(1)}, u32[]{:S(2)}, u32[]{:S(2)}) %all-to-all-start.1) | async-done | bytes 262176 | tf_op jit(solution)/shard_map/all_to_all | solution.py:300
  43.2 0.7 copy-done
  43.9 4.3 %shard_map.177 = (bf16[16,7,16,128]{3,2,1,0:T(8,128)(2,1)}, bf16[4,256,128]{2,1,0:T(8,128)(2,1)}, f32[256,128]{1,0:T(8,128)}, f32[3,256,128]{2,1,0:T(8,128)}) custom-call(bf16[256,128]{1,0:T(8,128)(2,1)} %refs_0_.3, bf16[3,256,128]{2,1,0:T(8,128)(2,1)} %refs_1_.3, bf16[16,4,16,128]{3,2,1,0:T(8,128)(2,1)} %copy-done, ...), custom_call_target="tpu_custom_call" | custom-call | tf_op jit(solution)/shard_map/pallas_call | solution.py:231
  48.2 3.6 %all-to-all-start.2 = ((bf16[16,7,16,128]{3,2,1,0:T(8,128)(2,1)}), bf16[16,7,16,128]{3,2,1,0:T(8,128)(2,1)S(1)}, u32[]{:S(2)}, u32[]{:S(2)}) async-start(bf16[16,7,16,128]{3,2,1,0:T(8,128)(2,1)} %get-tuple-element.16), calls=%async_computation.2 | async-start | bytes 917504 | tf_op jit(solution)/shard_map/all_to_all | solution.py:293
  51.8 0.5 fusion.5
  52.3 0.2 fusion.93
  52.6 0.2 fusion.73
  52.8 12.2 %all-to-all-done.2 = bf16[16,7,16,128]{3,2,1,0:T(8,128)(2,1)S(1)} async-done(((bf16[16,7,16,128]{3,2,1,0:T(8,128)(2,1)}), bf16[16,7,16,128]{3,2,1,0:T(8,128)(2,1)S(1)}, u32[]{:S(2)}, u32[]{:S(2)}) %all-to-all-start.2) | async-done | bytes 458784 | tf_op jit(solution)/shard_map/all_to_all | solution.py:293
  65.0 0.4 fusion.52
  65.4 0.1 slice_bitcast_fusion
  65.5 0.2 copy.58
  65.7 0.2 copy.57
  65.9 0.3 add_convert_fusion
  66.2 0.4 fusion.10
  66.9 0.3 fusion.30
  67.2 0.1 subtract_convert_fusion.2
  67.4 0.3 copy.94
  67.8 0.1 copy.63
  67.9 0.4 fusion.47
  68.3 0.2 fusion.46
  68.5 13.8 %all_to_all.20.refs_2_ = bf16[16,4,16,128]{3,2,1,0:T(8,128)(2,1)} all-to-all(bf16[16,4,16,128]{3,2,1,0:T(8,128)(2,1)S(1)} %fusion.46), channel_id=1, replica_groups=mesh['grp'=2,'seq'=16] {'seq'}, dimensions={0} | all-to-all | bytes 524288 | tf_op jit(solution)/shard_map/all_to_all | solution.py:300
  82.3 3.4 %shard_map.178 = (bf16[256,128]{1,0:T(8,128)(2,1)}, bf16[3,256,128]{2,1,0:T(8,128)(2,1)}) custom-call(f32[256,128]{1,0:T(8,128)} %get-tuple-element.14.refs_0_, f32[3,256,128]{2,1,0:T(8,128)} %get-tuple-element.15.refs_1_, bf16[16,4,16,128]{3,2,1,0:T(8,128)(2,1)} %all_to_all.20.refs_2_, bf16[4,256,128]{2,1,0:T(8,128)(2,1)} %get-tuple-element.21.refs_3_, ...), custom_call_target="tpu_custom_call" | custom-call | tf_op jit(solution)/shard_map/pallas_call | solution.py:231
  (41 shorter events, 1.4 us)
Async XLA Ops:
  0.6 11.0 %copy-start.4 = (f32[2,256]{1,0:T(2,128)S(1)}, f32[2,256]{1,0:T(2,128)}, u32[]{:S(2)}) copy-start(f32[2,256]{1,0:T(2,128)} %param.31) | copy-start | bytes 6148
  0.6 11.3 %copy-start.1 = (f32[2,256,64]{1,2,0:T(8,128)S(1)}, f32[2,256,64]{1,2,0:T(8,128)}, u32[]{:S(2)}) copy-start(f32[2,256,64]{1,2,0:T(8,128)} %param.30) | copy-start | bytes 393220
  0.7 11.4 %copy-start.3 = (f32[2,64,16]{1,2,0:T(8,128)S(1)}, f32[2,64,16]{1,2,0:T(8,128)}, u32[]{:S(2)}) copy-start(f32[2,64,16]{1,2,0:T(8,128)} %param.28) | copy-start | bytes 24580
  0.7 16.3 %copy-start.2 = (f32[2,64,64]{2,1,0:T(8,128)S(1)}, f32[2,64,64]{2,1,0:T(8,128)}, u32[]{:S(2)}) copy-start(f32[2,64,64]{2,1,0:T(8,128)} %param.29) | copy-start | bytes 98308
  3.6 20.6 %all-to-all-start = ((bf16[16,7,16,128]{3,2,1,0:T(8,128)(2,1)}), bf16[16,7,16,128]{3,2,1,0:T(8,128)(2,1)S(1)}, u32[]{:S(2)}, u32[]{:S(2)}) async-start(bf16[16,7,16,128]{3,2,1,0:T(8,128)(2,1)} %get-tuple-element.12), calls=%async_computation | async-start | bytes 917504 | tf_op jit(solution)/shard_map/all_to_all | solution.py:293
  26.8 0.9 %copy-start.5 = (f32[4]{0:T(128)S(1)}, f32[4]{0:T(128)}, u32[]{:S(2)}) copy-start(f32[4]{0:T(128)} %constant.86) | copy-start | bytes 52
  28.6 14.6 %all-to-all-start.1 = ((bf16[16,4,16,128]{3,2,1,0:T(8,128)(2,1)}), bf16[16,4,16,128]{3,2,1,0:T(8,128)(2,1)S(1)}, u32[]{:S(2)}, u32[]{:S(2)}) async-start(bf16[16,4,16,128]{3,2,1,0:T(8,128)(2,1)} %fusion.49), calls=%async_computation.1 | async-start | bytes 524288 | tf_op jit(solution)/shard_map/all_to_all | solution.py:300
  43.2 0.7 copy-start
  48.2 16.8 %all-to-all-start.2 = ((bf16[16,7,16,128]{3,2,1,0:T(8,128)(2,1)}), bf16[16,7,16,128]{3,2,1,0:T(8,128)(2,1)S(1)}, u32[]{:S(2)}, u32[]{:S(2)}) async-start(bf16[16,7,16,128]{3,2,1,0:T(8,128)(2,1)} %get-tuple-element.16), calls=%async_computation.2 | async-start | bytes 917504 | tf_op jit(solution)/shard_map/all_to_all | solution.py:293

commit v7 on v6

--- a/solution.py
+++ b/solution.py
@@ -5,6 +5,7 @@
 import numpy as np
 from jax import lax
 from jax.experimental import pallas as pl
+from jax.experimental.pallas import tpu as pltpu
 from jax.sharding import PartitionSpec as P
 
 HIGH = lax.Precision.HIGHEST
@@ -136,13 +137,19 @@
         return pl.BlockSpec((pl.Squeezed(),) + w.shape[1:], lambda i: (layer,) + (0,) * (w.ndim - 1))
 
     ins, specs = [state_s, state_v], [full(state_s.shape), full(state_v.shape)]
-    post_names = ("w_out_s", "w_out_v", "w_up", "w_down", "w_mix", "w_gate")
+    late_names = ("w_up", "w_down", "w_mix", "w_gate")
+    scratch = []
     if post is not None:
         ins += [arrays["conv"], arrays["query"]]
         specs += [full(arrays["conv"].shape), full(arrays["query"].shape)]
-        for name in post_names + ("gains_t",):
+        for name in ("w_out_s", "w_out_v", "gains_t"):
             ins.append(weights[name])
             specs.append(layer_spec(weights[name], post))
+        for name in late_names:
+            ins.append(weights[name])
+            specs.append(pl.BlockSpec(memory_space=pl.ANY))
+            scratch.append(pltpu.VMEM(weights[name].shape[1:], weights[name].dtype))
+        scratch.append(pltpu.SemaphoreType.DMA((len(late_names),)))
     if pre is not None:
         for name in ("w_qkw_s", "w_qkw_v", "gains_t"):
             ins.append(weights[name])
@@ -169,12 +176,20 @@
 
     def kernel(*refs):
         refs = list(refs)
+        if post is not None:
+            sems = refs.pop()
+            bufs = [refs.pop() for _ in late_names][::-1]
         ss_ref, sv_ref = refs.pop(0), refs.pop(0)
         ss = ss_ref[...].astype(f32)
         sv = [sv_ref[j].astype(f32) for j in range(3)]
         if post is not None:
             conv_ref, q_ref = refs.pop(0), refs.pop(0)
-            wos, wov, wup, wdn, wmx, wgt, gp = [refs.pop(0) for _ in range(7)]
+            wos, wov, gp = [refs.pop(0) for _ in range(3)]
+            copies = []
+            for slot in range(len(late_names)):
+                src_ref = refs.pop(0)
+                copies.append(pltpu.make_async_copy(src_ref.at[post], bufs[slot], sems.at[slot]))
+                copies[-1].start()
             g = gp[...].T
             qs = q_ref[0].astype(f32)
             if packed:
@@ -191,9 +206,14 @@
             sv = [sv[j] + mm(wov[...], (qs * yv[j]).astype(bf16)) for j in range(3)]
             mlp_s = snorm(ss, g[:, 2:3]).astype(bf16)
             mlp_v = [v.astype(bf16) for v in vnorm(sv, g[:, 3:4])]
+            wup, wdn, wmx, wgt = bufs
+            copies[0].wait()
             hidden = gelu_tanh(mm(wup[...], mlp_s)).astype(bf16)
+            copies[3].wait()
             gate = 1.0 / (1.0 + jnp.exp(-mm(wgt[...], mlp_s)))
+            copies[1].wait()
             ss = ss + mm(wdn[...], hidden)
+            copies[2].wait()
             sv = [sv[j] + mm(wmx[...], mlp_v[j]) * gate for j in range(3)]
         if pre is not None:
             wqs, wqv, gq = [refs.pop(0) for _ in range(3)]
@@ -234,6 +254,7 @@
         in_specs=specs,
         out_specs=[full(shape) for shape, _ in outs],
         out_shape=[jax.ShapeDtypeStruct(shape, dtype) for shape, dtype in outs],
+        scratch_shapes=scratch,
     )(*ins)
 
 

time: 86.1 us -> 88.3 us (1.026)
  Pallas kernels: 10.6 us -> 12.5 us
    pallas_call x3, Pallas kernels: 10.6 us -> 12.5 us  [token_step(): pl.pallas_call(kernel, grid=(1,), in_specs=specs, out_specs=[full(shape)...]
where the time goes in v7:
time: 88.3 us; the launch traced here: 87.7 us
  matrix products  18.9 us (21%)
  waiting for transfers between devices  18.9 us (21%)
  starting transfers between devices  15.5 us (18%)
  blocking collectives  13.8 us (16%)
  Pallas kernels  12.5 us (14%)
  other arithmetic  3.91 us (4%)
  local copies, waits for them, and re-layouts  2.98 us (3%)
  between operations  1.3 us (1%)
    all_to_all x1, blocking collectives, per_device(): returned = lax.all_to_all(convolved, 'seq', 0, 0, tiled=True)  13.8 us
    all_to_all x2, waiting for transfers between devices, per_device(): regrouped = lax.all_to_all(outgoing, 'seq', 0, 0, tiled=True)  13.7 us
    pallas_call x3, Pallas kernels, token_step(): pl.pallas_call(kernel, grid=(1,), in_specs=specs, out_specs=[full(shape)...  12.5 us
    all_to_all x2, starting transfers between devices, per_device(): regrouped = lax.all_to_all(outgoing, 'seq', 0, 0, tiled=True)  11 us
    dot_general x2, matrix products, filter_values(): hid_one = jnp.sin(jnp.dot(first, feats, precision=HIGH))  7.09 us
    dot_general x2, matrix products, filter_values(): hid_two = jnp.sin(jnp.dot(second, hid_one, precision=HIGH))  6.59 us
    all_to_all x1, waiting for transfers between devices, per_device(): returned = lax.all_to_all(convolved, 'seq', 0, 0, tiled=True)  5.25 us
    all_to_all x1, starting transfers between devices, per_device(): returned = lax.all_to_all(convolved, 'seq', 0, 0, tiled=True)  4.54 us
  transfers between devices with their start and end apart: 3, of which 3 were waited for; matrix products, arithmetic and copies ran while one was open for 20% of the time, Pallas kernels for 0%

profile of v7, /device:TPU:0, one launch (start us, length us, event | category | flops | bytes accessed | tf_op | source)
XLA Modules:
  0.0 87.7 jit_solution(1198432575388643351)
XLA Ops:
  0.7 2.9 %shard_map.176 = (bf16[16,7,16,128]{3,2,1,0:T(8,128)(2,1)}, bf16[4,256,128]{2,1,0:T(8,128)(2,1)}) custom-call(bf16[256,128]{1,0:T(8,128)(2,1)} %refs_0_.3, bf16[3,256,128]{2,1,0:T(8,128)(2,1)} %refs_1_.3, bf16[2,768,256]{2,1,0:T(8,128)(2,1)} %refs_11_.1, bf16[2,768,256]{2,1,0:T(8,128)(2,1)} %refs_12_.1, f32[2,4,256]{2,1,0:T(4,128)} %refs_6_.3), custom_call_target="tpu_custom_call" | custom-call | tf_op jit(solution)/shard_map/pallas_call | solution.py:251
  3.6 7.4 %all-to-all-start = ((bf16[16,7,16,128]{3,2,1,0:T(8,128)(2,1)}), bf16[16,7,16,128]{3,2,1,0:T(8,128)(2,1)S(1)}, u32[]{:S(2)}, u32[]{:S(2)}) async-start(bf16[16,7,16,128]{3,2,1,0:T(8,128)(2,1)} %get-tuple-element.12), calls=%async_computation | async-start | bytes 917504 | tf_op jit(solution)/shard_map/all_to_all | solution.py:314
  11.1 0.3 fusion.113
  11.3 0.3 negate_convert_fusion
  11.6 0.3 fusion.110
  12.1 4.8 %convolution_sine_fusion.1 = f32[2048,64]{1,0:T(8,128)S(1)} fusion(f32[8,2048]{1,0:T(8,128)S(1)} %get-tuple-element.63, f32[8,2048]{1,0:T(8,128)S(1)} %get-tuple-element.62, f32[2,64,16]{1,2,0:T(8,128)S(1)} %copy-done.3), kind=kOutput, calls=%fused_computation.1 | convolution fusion | flops 25198592 | bytes 663552 | tf_op jit(solution)/shard_map/dot_general | solution.py:21
  16.9 4.2 %convolution_sine_fusion = f32[2048,64]{1,0:T(8,128)S(1)} fusion(f32[2048,64]{1,0:T(8,128)S(1)} %convolution_sine_fusion.1, f32[2,64,64]{2,1,0:T(8,128)S(1)} %copy-done.2), kind=kOutput, calls=%fused_computation | convolution fusion | flops 100663296 | bytes 1605632 | tf_op jit(solution)/shard_map/dot_general | solution.py:22
  21.1 1.1 %fusion.4 = bf16[2,16,8,128]{3,2,1,0:T(8,128)(2,1)S(1)} fusion(f32[2048,64]{1,0:T(8,128)S(1)} %convolution_sine_fusion, f32[2048]{0:T(1024)S(1)} %iota_convert_fusion, f32[16]{0:T(128)S(1)} %fusion.133, f32[1,256,64]{1,2,0:T(8,128)S(1)} %get-tuple-element.59, s32[]{:T(128)S(6)} %select_n.108), kind=kOutput, calls=%fused_computation.10 | convolution fusion | flops 25329664 | bytes 1155588 | tf_op jit(solution)/shard_map/dot_general | solution.py:23
  22.2 0.2 fusion.96
  22.6 0.2 fusion.69
  22.8 1.4 %all-to-all-done = bf16[16,7,16,128]{3,2,1,0:T(8,128)(2,1)S(1)} async-done(((bf16[16,7,16,128]{3,2,1,0:T(8,128)(2,1)}), bf16[16,7,16,128]{3,2,1,0:T(8,128)(2,1)S(1)}, u32[]{:S(2)}, u32[]{:S(2)}) %all-to-all-start) | async-done | bytes 458784 | tf_op jit(solution)/shard_map/all_to_all | solution.py:314
  24.2 0.4 fusion.55
  24.6 0.1 slice_bitcast_fusion.2
  24.7 0.4 copy.50
  25.1 0.2 copy.49
  25.3 0.3 add_convert_fusion.1
  25.6 0.4 fusion.6
  26.3 0.3 fusion.14
  26.6 0.1 subtract_convert_fusion.3
  26.8 0.3 copy.95
  27.2 0.1 copy.55
  27.3 0.4 fusion.50
  27.7 0.9 %fusion.49 = bf16[16,4,16,128]{3,2,1,0:T(8,128)(2,1)} fusion(f32[16,4,16,128]{3,0,2,1:T(8,128)S(1)} %fusion.50, f32[4]{0:T(128)S(1)} %copy-done.5), kind=kLoop, calls=%fused_computation.69 | loop fusion | flops 262144 | bytes 786448 | tf_op jit(solution)/shard_map/convert_element_type | solution.py:121
  28.6 4.5 %all-to-all-start.1 = ((bf16[16,4,16,128]{3,2,1,0:T(8,128)(2,1)}), bf16[16,4,16,128]{3,2,1,0:T(8,128)(2,1)S(1)}, u32[]{:S(2)}, u32[]{:S(2)}) async-start(bf16[16,4,16,128]{3,2,1,0:T(8,128)(2,1)} %fusion.49), calls=%async_computation.1 | async-start | bytes 524288 | tf_op jit(solution)/shard_map/all_to_all | solution.py:321
  33.2 2.3 %convolution_sine_fusion.3 = f32[64,2048]{1,0:T(8,128)S(1)} fusion(f32[64,16]{0,1:T(8,128)S(1)} %slice_bitcast_fusion.14, f32[8,2048]{1,0:T(8,128)S(1)} %get-tuple-element.63, f32[8,2048]{1,0:T(8,128)S(1)} %get-tuple-element.62), kind=kOutput, calls=%fused_computation.3 | convolution fusion | flops 25198592 | bytes 659456 | tf_op jit(solution)/shard_map/dot_general | solution.py:21
  35.5 2.4 %convolution_sine_fusion.2 = f32[64,2048]{1,0:T(8,128)S(1)} fusion(f32[64,64]{1,0:T(8,128)S(1)} %slice_bitcast_fusion.13, f32[64,2048]{1,0:T(8,128)S(1)} %convolution_sine_fusion.3), kind=kOutput, calls=%fused_computation.2 | convolution fusion | flops 100663296 | bytes 1064960 | tf_op jit(solution)/shard_map/dot_general | solution.py:22
  38.0 5.3 %all-to-all-done.1.refs_2_ = bf16[16,4,16,128]{3,2,1,0:T(8,128)(2,1)S(1)} async-done(((bf16[16,4,16,128]{3,2,1,0:T(8,128)(2,1)}), bf16[16,4,16,128]{3,2,1,0:T(8,128)(2,1)S(1)}, u32[]{:S(2)}, u32[]{:S(2)}) %all-to-all-start.1) | async-done | bytes 262176 | tf_op jit(solution)/shard_map/all_to_all | solution.py:321
  43.2 0.7 copy-done
  43.9 5.3 %shard_map.177 = (bf16[16,7,16,128]{3,2,1,0:T(8,128)(2,1)}, bf16[4,256,128]{2,1,0:T(8,128)(2,1)}, f32[256,128]{1,0:T(8,128)}, f32[3,256,128]{2,1,0:T(8,128)}) custom-call(bf16[256,128]{1,0:T(8,128)(2,1)} %refs_0_.3, bf16[3,256,128]{2,1,0:T(8,128)(2,1)} %refs_1_.3, bf16[16,4,16,128]{3,2,1,0:T(8,128)(2,1)} %copy-done, ...), custom_call_target="tpu_custom_call" | custom-call | tf_op jit(solution)/shard_map/pallas_call | solution.py:251
  49.2 3.6 %all-to-all-start.2 = ((bf16[16,7,16,128]{3,2,1,0:T(8,128)(2,1)}), bf16[16,7,16,128]{3,2,1,0:T(8,128)(2,1)S(1)}, u32[]{:S(2)}, u32[]{:S(2)}) async-start(bf16[16,7,16,128]{3,2,1,0:T(8,128)(2,1)} %get-tuple-element.16), calls=%async_computation.2 | async-start | bytes 917504 | tf_op jit(solution)/shard_map/all_to_all | solution.py:314
  52.8 0.5 fusion.5
  53.3 0.2 fusion.93
  53.6 0.2 fusion.73
  53.8 12.2 %all-to-all-done.2 = bf16[16,7,16,128]{3,2,1,0:T(8,128)(2,1)S(1)} async-done(((bf16[16,7,16,128]{3,2,1,0:T(8,128)(2,1)}), bf16[16,7,16,128]{3,2,1,0:T(8,128)(2,1)S(1)}, u32[]{:S(2)}, u32[]{:S(2)}) %all-to-all-start.2) | async-done | bytes 458784 | tf_op jit(solution)/shard_map/all_to_all | solution.py:314
  66.0 0.4 fusion.52
  66.4 0.1 slice_bitcast_fusion
  66.5 0.2 copy.58
  66.7 0.2 copy.57
  66.9 0.3 add_convert_fusion
  67.1 0.4 fusion.10
  67.9 0.3 fusion.30
  68.2 0.1 subtract_convert_fusion.2
  68.4 0.3 copy.94
  68.8 0.1 copy.63
  68.9 0.4 fusion.47
  69.3 0.2 fusion.46
  69.5 13.8 %all_to_all.20.refs_2_ = bf16[16,4,16,128]{3,2,1,0:T(8,128)(2,1)} all-to-all(bf16[16,4,16,128]{3,2,1,0:T(8,128)(2,1)S(1)} %fusion.46), channel_id=1, replica_groups=mesh['grp'=2,'seq'=16] {'seq'}, dimensions={0} | all-to-all | bytes 524288 | tf_op jit(solution)/shard_map/all_to_all | solution.py:321
  83.3 4.3 %shard_map.178 = (bf16[256,128]{1,0:T(8,128)(2,1)}, bf16[3,256,128]{2,1,0:T(8,128)(2,1)}) custom-call(f32[256,128]{1,0:T(8,128)} %get-tuple-element.14.refs_0_, f32[3,256,128]{2,1,0:T(8,128)} %get-tuple-element.15.refs_1_, bf16[16,4,16,128]{3,2,1,0:T(8,128)(2,1)} %all_to_all.20.refs_2_, bf16[4,256,128]{2,1,0:T(8,128)(2,1)} %get-tuple-element.21.refs_3_, ...), custom_call_target="tpu_custom_call" | custom-call | tf_op jit(solution)/shard_map/pallas_call | solution.py:251
  (41 shorter events, 1.4 us)
Async XLA Ops:
  0.6 11.0 %copy-start.4 = (f32[2,256]{1,0:T(2,128)S(1)}, f32[2,256]{1,0:T(2,128)}, u32[]{:S(2)}) copy-start(f32[2,256]{1,0:T(2,128)} %param.31) | copy-start | bytes 6148
  0.6 11.3 %copy-start.1 = (f32[2,256,64]{1,2,0:T(8,128)S(1)}, f32[2,256,64]{1,2,0:T(8,128)}, u32[]{:S(2)}) copy-start(f32[2,256,64]{1,2,0:T(8,128)} %param.30) | copy-start | bytes 393220
  0.7 11.4 %copy-start.3 = (f32[2,64,16]{1,2,0:T(8,128)S(1)}, f32[2,64,16]{1,2,0:T(8,128)}, u32[]{:S(2)}) copy-start(f32[2,64,16]{1,2,0:T(8,128)} %param.28) | copy-start | bytes 24580
  0.7 16.3 %copy-start.2 = (f32[2,64,64]{2,1,0:T(8,128)S(1)}, f32[2,64,64]{2,1,0:T(8,128)}, u32[]{:S(2)}) copy-start(f32[2,64,64]{2,1,0:T(8,128)} %param.29) | copy-start | bytes 98308
  3.6 20.6 %all-to-all-start = ((bf16[16,7,16,128]{3,2,1,0:T(8,128)(2,1)}), bf16[16,7,16,128]{3,2,1,0:T(8,128)(2,1)S(1)}, u32[]{:S(2)}, u32[]{:S(2)}) async-start(bf16[16,7,16,128]{3,2,1,0:T(8,128)(2,1)} %get-tuple-element.12), calls=%async_computation | async-start | bytes 917504 | tf_op jit(solution)/shard_map/all_to_all | solution.py:314
  26.8 0.9 %copy-start.5 = (f32[4]{0:T(128)S(1)}, f32[4]{0:T(128)}, u32[]{:S(2)}) copy-start(f32[4]{0:T(128)} %constant.86) | copy-start | bytes 52
  28.6 14.6 %all-to-all-start.1 = ((bf16[16,4,16,128]{3,2,1,0:T(8,128)(2,1)}), bf16[16,4,16,128]{3,2,1,0:T(8,128)(2,1)S(1)}, u32[]{:S(2)}, u32[]{:S(2)}) async-start(bf16[16,4,16,128]{3,2,1,0:T(8,128)(2,1)} %fusion.49), calls=%async_computation.1 | async-start | bytes 524288 | tf_op jit(solution)/shard_map/all_to_all | solution.py:321
  43.2 0.7 copy-start
  49.2 16.8 %all-to-all-start.2 = ((bf16[16,7,16,128]{3,2,1,0:T(8,128)(2,1)}), bf16[16,7,16,128]{3,2,1,0:T(8,128)(2,1)S(1)}, u32[]{:S(2)}, u32[]{:S(2)}) async-start(bf16[16,7,16,128]{3,2,1,0:T(8,128)(2,1)} %get-tuple-element.16), calls=%async_computation.2 | async-start | bytes 917504 | tf_op jit(solution)/shard_map/all_to_all | solution.py:314

commit v8 on v6

--- a/solution.py
+++ b/solution.py
@@ -271,7 +271,6 @@
         made = made.reshape(own, shards, tok_local).transpose(1, 0, 2)
         return forward_dft(made[:, None].astype(jnp.float32), tables, FAST)[:, 0]
 
-    spec_next = filter_spec(pe_w1[0], pe_w2[0], pe_w3[0], rates[0])
     weights = {
         "w_qkw_s": w_qkw_s,
         "w_qkw_v": w_qkw_v,
@@ -286,6 +285,8 @@
     arrays = {"state_s": scalars, "state_v": vectors}
     packed = own % 16 == 0
     planes, query = token_step(None, 0, arrays, weights, shards)
+    tied = lax.optimization_barrier((pe_w1[0], pe_w2[0], pe_w3[0], rates[0], planes))
+    spec_next = filter_spec(*tied[:4])
     for layer in range(depth):
         outgoing = planes
         if not packed:

time: 86.1 us -> 85.3 us (level)
  matrix products: 18.9 us -> 13.9 us
  waiting for transfers between devices: 18.9 us -> 23.8 us
    all_to_all x2, waiting for transfers between devices: 13.7 us -> 18.5 us  [per_device(): regrouped = lax.all_to_all(outgoing, 'seq', 0, 0, tiled=True)]
    dot_general x2, matrix products: 7.09 us -> 4.53 us  [filter_values(): hid_one = jnp.sin(jnp.dot(first, feats, precision=HIGH))]
    dot_general x2, matrix products: 6.59 us -> 4.86 us  [filter_values(): hid_two = jnp.sin(jnp.dot(second, hid_one, precision=HIGH))]
  transfers between devices with their start and end apart: 3 -> 3, of which waited for: 3 -> 3; matrix products, arithmetic and copies ran while one was open for 20% -> 15% of each run, Pallas kernels for 0% -> 0%
where the time goes in v8:
time: 85.3 us; the launch traced here: 84.8 us
  waiting for transfers between devices  23.8 us (28%)
  starting transfers between devices  14.9 us (17%)
  matrix products  13.9 us (16%)
  blocking collectives  13.8 us (16%)
  Pallas kernels  10.5 us (12%)
  other arithmetic  3.92 us (5%)
  local copies, waits for them, and re-layouts  2.82 us (3%)
  between operations  1.15 us (1%)
    all_to_all x2, waiting for transfers between devices, per_device(): regrouped = lax.all_to_all(outgoing, 'seq', 0, 0, tiled=True)  18.5 us
    all_to_all x1, blocking collectives, per_device(): returned = lax.all_to_all(convolved, 'seq', 0, 0, tiled=True)  13.8 us
    all_to_all x2, starting transfers between devices, per_device(): regrouped = lax.all_to_all(outgoing, 'seq', 0, 0, tiled=True)  10.9 us
    pallas_call x3, Pallas kernels, token_step(): pl.pallas_call(kernel, grid=(1,), in_specs=specs, out_specs=[full(shape)...  10.5 us
    all_to_all x1, waiting for transfers between devices, per_device(): returned = lax.all_to_all(convolved, 'seq', 0, 0, tiled=True)  5.25 us
    dot_general x2, matrix products, filter_values(): hid_two = jnp.sin(jnp.dot(second, hid_one, precision=HIGH))  4.86 us
    dot_general x2, matrix products, filter_values(): hid_one = jnp.sin(jnp.dot(first, feats, precision=HIGH))  4.53 us
    all_to_all x1, starting transfers between devices, per_device(): returned = lax.all_to_all(convolved, 'seq', 0, 0, tiled=True)  3.9 us
  transfers between devices with their start and end apart: 3, of which 3 were waited for; matrix products, arithmetic and copies ran while one was open for 15% of the time, Pallas kernels for 0%

profile of v8, /device:TPU:0, one launch (start us, length us, event | category | flops | bytes accessed | tf_op | source)
XLA Modules:
  0.0 84.8 jit_solution(18060058877906739987)
XLA Ops:
  0.7 2.9 %shard_map.176 = (bf16[16,7,16,128]{3,2,1,0:T(8,128)(2,1)}, bf16[4,256,128]{2,1,0:T(8,128)(2,1)}) custom-call(bf16[256,128]{1,0:T(8,128)(2,1)} %refs_0_.3, bf16[3,256,128]{2,1,0:T(8,128)(2,1)} %refs_1_.3, bf16[2,768,256]{2,1,0:T(8,128)(2,1)} %refs_11_.1, bf16[2,768,256]{2,1,0:T(8,128)(2,1)} %refs_12_.1, f32[2,4,256]{2,1,0:T(4,128)} %refs_10_.3), custom_call_target="tpu_custom_call" | custom-call | tf_op jit(solution)/shard_map/pallas_call | solution.py:231
  3.6 7.4 %all-to-all-start = ((bf16[16,7,16,128]{3,2,1,0:T(8,128)(2,1)}), bf16[16,7,16,128]{3,2,1,0:T(8,128)(2,1)S(1)}, u32[]{:S(2)}, u32[]{:S(2)}) async-start(bf16[16,7,16,128]{3,2,1,0:T(8,128)(2,1)} %get-tuple-element.16), calls=%async_computation | async-start | bytes 917504 | tf_op jit(solution)/shard_map/all_to_all | solution.py:294
  11.1 0.3 fusion.107
  11.6 2.3 %convolution_sine_fusion.3 = f32[64,2048]{1,0:T(8,128)S(1)} fusion(f32[64,16]{0,1:T(8,128)S(1)} %get-tuple-element.19, f32[8,2048]{1,0:T(8,128)S(1)} %get-tuple-element.75, f32[8,2048]{1,0:T(8,128)S(1)} %get-tuple-element.74), kind=kOutput, calls=%fused_computation.3 | convolution fusion | flops 25198592 | bytes 659456 | tf_op jit(solution)/shard_map/dot_general | solution.py:20
  13.8 2.4 %convolution_sine_fusion.2 = f32[64,2048]{1,0:T(8,128)S(1)} fusion(f32[64,64]{1,0:T(8,128)S(1)} %get-tuple-element.18, f32[64,2048]{1,0:T(8,128)S(1)} %convolution_sine_fusion.3), kind=kOutput, calls=%fused_computation.2 | convolution fusion | flops 100663296 | bytes 1064960 | tf_op jit(solution)/shard_map/dot_general | solution.py:21
  16.3 0.5 fusion.5
  16.8 0.2 fusion.96
  17.1 0.3 fusion.110
  17.4 0.3 negate_convert_fusion
  17.7 0.2 fusion.69
  17.9 6.3 %all-to-all-done = bf16[16,7,16,128]{3,2,1,0:T(8,128)(2,1)S(1)} async-done(((bf16[16,7,16,128]{3,2,1,0:T(8,128)(2,1)}), bf16[16,7,16,128]{3,2,1,0:T(8,128)(2,1)S(1)}, u32[]{:S(2)}, u32[]{:S(2)}) %all-to-all-start) | async-done | bytes 458784 | tf_op jit(solution)/shard_map/all_to_all | solution.py:294
  24.2 0.4 fusion.55
  24.6 0.1 slice_bitcast_fusion.2
  24.7 0.2 copy.50
  24.9 0.2 copy.49
  25.1 0.3 add_convert_fusion.1
  25.4 0.4 fusion.6
  26.1 0.3 fusion.14
  26.4 0.1 subtract_convert_fusion.3
  26.6 0.3 copy.95
  27.0 0.1 copy.55
  27.1 0.4 fusion.50
  27.5 0.9 %fusion.49 = bf16[16,4,16,128]{3,2,1,0:T(8,128)(2,1)} fusion(f32[16,4,16,128]{3,0,2,1:T(8,128)S(1)} %fusion.50, f32[4]{0:T(128)S(1)} %copy-done.5), kind=kLoop, calls=%fused_computation.69 | loop fusion | flops 262144 | bytes 786448 | tf_op jit(solution)/shard_map/convert_element_type | solution.py:120
  28.4 3.9 %all-to-all-start.1 = ((bf16[16,4,16,128]{3,2,1,0:T(8,128)(2,1)}), bf16[16,4,16,128]{3,2,1,0:T(8,128)(2,1)S(1)}, u32[]{:S(2)}, u32[]{:S(2)}) async-start(bf16[16,4,16,128]{3,2,1,0:T(8,128)(2,1)} %fusion.49), calls=%async_computation.1 | async-start | bytes 524288 | tf_op jit(solution)/shard_map/all_to_all | solution.py:301
  32.4 2.3 %convolution_sine_fusion.1 = f32[64,2048]{1,0:T(8,128)S(1)} fusion(f32[64,16]{0,1:T(8,128)S(1)} %get-tuple-element.27, f32[8,2048]{1,0:T(8,128)S(1)} %get-tuple-element.75, f32[8,2048]{1,0:T(8,128)S(1)} %get-tuple-element.74), kind=kOutput, calls=%fused_computation.1 | convolution fusion | flops 25198592 | bytes 659456 | tf_op jit(solution)/shard_map/dot_general | solution.py:20
  34.7 2.4 %convolution_sine_fusion = f32[64,2048]{1,0:T(8,128)S(1)} fusion(f32[64,64]{1,0:T(8,128)S(1)} %get-tuple-element.26, f32[64,2048]{1,0:T(8,128)S(1)} %convolution_sine_fusion.1), kind=kOutput, calls=%fused_computation | convolution fusion | flops 100663296 | bytes 1064960 | tf_op jit(solution)/shard_map/dot_general | solution.py:21
  37.1 5.3 %all-to-all-done.1.refs_2_ = bf16[16,4,16,128]{3,2,1,0:T(8,128)(2,1)S(1)} async-done(((bf16[16,4,16,128]{3,2,1,0:T(8,128)(2,1)}), bf16[16,4,16,128]{3,2,1,0:T(8,128)(2,1)S(1)}, u32[]{:S(2)}, u32[]{:S(2)}) %all-to-all-start.1) | async-done | bytes 262176 | tf_op jit(solution)/shard_map/all_to_all | solution.py:301
  42.4 0.7 copy-done
  43.1 4.3 %shard_map.177 = (bf16[16,7,16,128]{3,2,1,0:T(8,128)(2,1)}, bf16[4,256,128]{2,1,0:T(8,128)(2,1)}, f32[256,128]{1,0:T(8,128)}, f32[3,256,128]{2,1,0:T(8,128)}) custom-call(bf16[256,128]{1,0:T(8,128)(2,1)} %refs_0_.3, bf16[3,256,128]{2,1,0:T(8,128)(2,1)} %refs_1_.3, bf16[16,4,16,128]{3,2,1,0:T(8,128)(2,1)} %copy-done, ...), custom_call_target="tpu_custom_call" | custom-call | tf_op jit(solution)/shard_map/pallas_call | solution.py:231
  47.4 3.6 %all-to-all-start.2 = ((bf16[16,7,16,128]{3,2,1,0:T(8,128)(2,1)}), bf16[16,7,16,128]{3,2,1,0:T(8,128)(2,1)S(1)}, u32[]{:S(2)}, u32[]{:S(2)}) async-start(bf16[16,7,16,128]{3,2,1,0:T(8,128)(2,1)} %get-tuple-element.24), calls=%async_computation.2 | async-start | bytes 917504 | tf_op jit(solution)/shard_map/all_to_all | solution.py:294
  50.9 0.5 fusion.4
  51.4 0.2 fusion.93
  51.8 0.2 fusion.73
  51.9 12.2 %all-to-all-done.2 = bf16[16,7,16,128]{3,2,1,0:T(8,128)(2,1)S(1)} async-done(((bf16[16,7,16,128]{3,2,1,0:T(8,128)(2,1)}), bf16[16,7,16,128]{3,2,1,0:T(8,128)(2,1)S(1)}, u32[]{:S(2)}, u32[]{:S(2)}) %all-to-all-start.2) | async-done | bytes 458784 | tf_op jit(solution)/shard_map/all_to_all | solution.py:294
  64.2 0.4 fusion.52
  64.5 0.1 slice_bitcast_fusion
  64.7 0.2 copy.58
  64.9 0.2 copy.57
  65.0 0.3 add_convert_fusion
  65.3 0.4 fusion.10
  66.1 0.3 fusion.30
  66.3 0.1 subtract_convert_fusion.2
  66.6 0.3 copy.94
  66.9 0.1 copy.63
  67.0 0.4 fusion.47
  67.4 0.2 fusion.46
  67.6 13.8 %all_to_all.20.refs_2_ = bf16[16,4,16,128]{3,2,1,0:T(8,128)(2,1)} all-to-all(bf16[16,4,16,128]{3,2,1,0:T(8,128)(2,1)S(1)} %fusion.46), channel_id=1, replica_groups=mesh['grp'=2,'seq'=16] {'seq'}, dimensions={0} | all-to-all | bytes 524288 | tf_op jit(solution)/shard_map/all_to_all | solution.py:301
  81.4 3.4 %shard_map.178 = (bf16[256,128]{1,0:T(8,128)(2,1)}, bf16[3,256,128]{2,1,0:T(8,128)(2,1)}) custom-call(f32[256,128]{1,0:T(8,128)} %get-tuple-element.22.refs_0_, f32[3,256,128]{2,1,0:T(8,128)} %get-tuple-element.23.refs_1_, bf16[16,4,16,128]{3,2,1,0:T(8,128)(2,1)} %all_to_all.20.refs_2_, bf16[4,256,128]{2,1,0:T(8,128)(2,1)} %get-tuple-element.29.refs_3_, ...), custom_call_target="tpu_custom_call" | custom-call | tf_op jit(solution)/shard_map/pallas_call | solution.py:231
  (41 shorter events, 1.4 us)
Async XLA Ops:
  0.6 10.4 %copy-start.4 = (f32[2,256]{1,0:T(2,128)S(1)}, f32[2,256]{1,0:T(2,128)}, u32[]{:S(2)}) copy-start(f32[2,256]{1,0:T(2,128)} %param.31) | copy-start | bytes 6148
  0.6 10.4 %copy-start.3 = (f32[2,64,16]{1,2,0:T(8,128)S(1)}, f32[2,64,16]{1,2,0:T(8,128)}, u32[]{:S(2)}) copy-start(f32[2,64,16]{1,2,0:T(8,128)} %param.28) | copy-start | bytes 24580
  0.7 10.4 %copy-start.2 = (f32[2,64,64]{2,1,0:T(8,128)S(1)}, f32[2,64,64]{2,1,0:T(8,128)}, u32[]{:S(2)}) copy-start(f32[2,64,64]{2,1,0:T(8,128)} %param.29) | copy-start | bytes 98308
  0.7 10.8 %copy-start.1 = (f32[2,256,64]{1,2,0:T(8,128)S(1)}, f32[2,256,64]{1,2,0:T(8,128)}, u32[]{:S(2)}) copy-start(f32[2,256,64]{1,2,0:T(8,128)} %param.30) | copy-start | bytes 393220
  3.6 20.6 %all-to-all-start = ((bf16[16,7,16,128]{3,2,1,0:T(8,128)(2,1)}), bf16[16,7,16,128]{3,2,1,0:T(8,128)(2,1)S(1)}, u32[]{:S(2)}, u32[]{:S(2)}) async-start(bf16[16,7,16,128]{3,2,1,0:T(8,128)(2,1)} %get-tuple-element.16), calls=%async_computation | async-start | bytes 917504 | tf_op jit(solution)/shard_map/all_to_all | solution.py:294
  26.6 0.9 %copy-start.5 = (f32[4]{0:T(128)S(1)}, f32[4]{0:T(128)}, u32[]{:S(2)}) copy-start(f32[4]{0:T(128)} %constant.84) | copy-start | bytes 52
  28.4 13.9 %all-to-all-start.1 = ((bf16[16,4,16,128]{3,2,1,0:T(8,128)(2,1)}), bf16[16,4,16,128]{3,2,1,0:T(8,128)(2,1)S(1)}, u32[]{:S(2)}, u32[]{:S(2)}) async-start(bf16[16,4,16,128]{3,2,1,0:T(8,128)(2,1)} %fusion.49), calls=%async_computation.1 | async-start | bytes 524288 | tf_op jit(solution)/shard_map/all_to_all | solution.py:301
  42.4 0.7 copy-start
  47.4 16.8 %all-to-all-start.2 = ((bf16[16,7,16,128]{3,2,1,0:T(8,128)(2,1)}), bf16[16,7,16,128]{3,2,1,0:T(8,128)(2,1)S(1)}, u32[]{:S(2)}, u32[]{:S(2)}) async-start(bf16[16,7,16,128]{3,2,1,0:T(8,128)(2,1)} %get-tuple-element.24), calls=%async_computation.2 | async-start | bytes 917504 | tf_op jit(solution)/shard_map/all_to_all | solution.py:294

commit v9 on v8

--- a/solution.py
+++ b/solution.py
@@ -45,11 +45,16 @@
         cols = jnp.arange(cols, dtype=jnp.int32)[None, :]
         return ((rows * cols) % period).astype(f32) * (2.0 * math.pi / period)
 
-    ang_s = turns(shards, shards, shards)
+    half = shards // 2 + 1 if shards % 2 == 0 else shards
+    ang_s = turns(half, shards, shards)
     cos_s, sin_s = jnp.cos(ang_s), jnp.sin(ang_s)
     lead_fwd = jnp.concatenate([cos_s, -sin_s], axis=0)
-    lead_inv = jnp.concatenate([cos_s, -sin_s], axis=1)
-    ang_t = turns(shards, local, length)
+    if half == shards:
+        weight = jnp.ones((half,), f32)
+    else:
+        weight = jnp.full((half,), 2.0, f32).at[0].set(1.0).at[half - 1].set(1.0)
+    lead_inv = jnp.concatenate([cos_s.T * weight, -sin_s.T * weight], axis=1)
+    ang_t = turns(half, local, length)
     tw_c = jnp.cos(ang_t)[:, None, None, :]
     tw_s = jnp.sin(ang_t)[:, None, None, :]
     ang_l = turns(local, local, local)
@@ -71,26 +76,28 @@
     shards, planes, chans, local = field.shape
     flat = field.reshape(shards, -1).astype(jnp.bfloat16)
     stage = jnp.dot(lead_fwd, flat, preferred_element_type=jnp.float32)
-    stage = stage.reshape(2 * shards, planes, chans, local)
-    st_r, st_i = stage[:shards], stage[shards:]
+    half = lead_fwd.shape[0] // 2
+    stage = stage.reshape(2 * half, planes, chans, local)
+    st_r, st_i = stage[:half], stage[half:]
     tw_r = st_r * tw_c + st_i * tw_s
     tw_i = st_i * tw_c - st_r * tw_s
     joined = jnp.concatenate([tw_r, tw_i], axis=-1).reshape(-1, 2 * local).astype(jnp.bfloat16)
     spec = jnp.dot(joined, lane_fwd, preferred_element_type=jnp.float32)
-    return spec.reshape(shards, planes, chans, 2 * local)
+    return spec.reshape(half, planes, chans, 2 * local)
 
 
 def inverse_dft(spec, tables, prec):
     _, lead_inv, tw_c, tw_s, _, lane_inv = tables
-    shards, planes, chans, width = spec.shape
+    half, planes, chans, width = spec.shape
+    shards = lead_inv.shape[0]
     local = width // 2
     flat = spec.reshape(-1, width).astype(jnp.bfloat16)
     back = jnp.dot(flat, lane_inv, preferred_element_type=jnp.float32)
-    back = back.reshape(shards, planes, chans, width)
+    back = back.reshape(half, planes, chans, width)
     bk_r, bk_i = back[..., :local], back[..., local:]
     un_r = bk_r * tw_c - bk_i * tw_s
     un_i = bk_r * tw_s + bk_i * tw_c
-    stacked = jnp.concatenate([un_r, un_i], axis=0).reshape(2 * shards, -1).astype(jnp.bfloat16)
+    stacked = jnp.concatenate([un_r, un_i], axis=0).reshape(2 * half, -1).astype(jnp.bfloat16)
     whole = jnp.dot(lead_inv, stacked, preferred_element_type=jnp.float32)
     return whole.reshape(shards, planes, chans, local)
 

time: 85.3 us -> 83.6 us (0.980)
    unnamed x28 -> x26, local copies, waits for them, and re-layouts: 2.76 us -> 1.88 us
    another operation x15 -> x16, other arithmetic: 2.08 us -> 1.53 us
where the time goes in v9:
time: 83.6 us; the launch traced here: 83.1 us
  waiting for transfers between devices  23.8 us (28%)
  starting transfers between devices  14.9 us (18%)
  blocking collectives  13.8 us (17%)
  matrix products  13.4 us (16%)
  Pallas kernels  10.5 us (13%)
  other arithmetic  3.32 us (4%)
  local copies, waits for them, and re-layouts  2.23 us (3%)
  between operations  1.15 us (1%)
    all_to_all x2, waiting for transfers between devices, per_device(): regrouped = lax.all_to_all(outgoing, 'seq', 0, 0, tiled=True)  19 us
    all_to_all x1, blocking collectives, per_device(): returned = lax.all_to_all(convolved, 'seq', 0, 0, tiled=True)  13.8 us
    all_to_all x2, starting transfers between devices, per_device(): regrouped = lax.all_to_all(outgoing, 'seq', 0, 0, tiled=True)  10.9 us
    pallas_call x3, Pallas kernels, token_step(): pl.pallas_call(kernel, grid=(1,), in_specs=specs, out_specs=[full(shape)...  10.5 us
    dot_general x2, matrix products, filter_values(): hid_two = jnp.sin(jnp.dot(second, hid_one, precision=HIGH))  4.85 us
    all_to_all x1, waiting for transfers between devices, per_device(): returned = lax.all_to_all(convolved, 'seq', 0, 0, tiled=True)  4.77 us
    dot_general x2, matrix products, filter_values(): hid_one = jnp.sin(jnp.dot(first, feats, precision=HIGH))  4.53 us
    all_to_all x1, starting transfers between devices, per_device(): returned = lax.all_to_all(convolved, 'seq', 0, 0, tiled=True)  3.9 us
  transfers between devices with their start and end apart: 3, of which 3 were waited for; matrix products, arithmetic and copies ran while one was open for 15% of the time, Pallas kernels for 0%

profile of v9, /device:TPU:0, one launch (start us, length us, event | category | flops | bytes accessed | tf_op | source)
XLA Modules:
  0.0 83.1 jit_solution(14375019290633646097)
XLA Ops:
  0.7 2.9 %shard_map.176 = (bf16[16,7,16,128]{3,2,1,0:T(8,128)(2,1)}, bf16[4,256,128]{2,1,0:T(8,128)(2,1)}) custom-call(bf16[256,128]{1,0:T(8,128)(2,1)} %refs_0_.3, bf16[3,256,128]{2,1,0:T(8,128)(2,1)} %refs_1_.3, bf16[2,768,256]{2,1,0:T(8,128)(2,1)} %refs_11_.1, bf16[2,768,256]{2,1,0:T(8,128)(2,1)} %refs_12_.1, f32[2,4,256]{2,1,0:T(4,128)} %refs_10_.3), custom_call_target="tpu_custom_call" | custom-call | tf_op jit(solution)/shard_map/pallas_call | solution.py:238
  3.6 7.4 %all-to-all-start = ((bf16[16,7,16,128]{3,2,1,0:T(8,128)(2,1)}), bf16[16,7,16,128]{3,2,1,0:T(8,128)(2,1)S(1)}, u32[]{:S(2)}, u32[]{:S(2)}) async-start(bf16[16,7,16,128]{3,2,1,0:T(8,128)(2,1)} %get-tuple-element.40), calls=%async_computation | async-start | bytes 917504 | tf_op jit(solution)/shard_map/all_to_all | solution.py:301
  11.1 0.3 fusion.99
  11.5 0.1 dynamic-slice_negate_fusion.1
  11.6 2.3 %convolution_sine_fusion.3 = f32[64,2048]{1,0:T(8,128)S(1)} fusion(f32[64,16]{0,1:T(8,128)S(1)} %get-tuple-element.43, f32[8,2048]{1,0:T(8,128)S(1)} %get-tuple-element.101, f32[8,2048]{1,0:T(8,128)S(1)} %get-tuple-element.100), kind=kOutput, calls=%fused_computation.3 | convolution fusion | flops 25198592 | bytes 659456 | tf_op jit(solution)/shard_map/dot_general | solution.py:20
  13.8 2.4 %convolution_sine_fusion.2 = f32[64,2048]{1,0:T(8,128)S(1)} fusion(f32[64,64]{1,0:T(8,128)S(1)} %get-tuple-element.42, f32[64,2048]{1,0:T(8,128)S(1)} %convolution_sine_fusion.3), kind=kOutput, calls=%fused_computation.2 | convolution fusion | flops 100663296 | bytes 1064960 | tf_op jit(solution)/shard_map/dot_general | solution.py:21
  16.3 0.5 fusion.5
  16.8 0.2 fusion.84
  17.1 0.3 fusion.102
  17.4 0.3 negate_convert_fusion
  17.7 0.2 fusion.65
  17.9 0.1 multiply_convert_fusion.1
  17.9 6.3 %all-to-all-done = bf16[16,7,16,128]{3,2,1,0:T(8,128)(2,1)S(1)} async-done(((bf16[16,7,16,128]{3,2,1,0:T(8,128)(2,1)}), bf16[16,7,16,128]{3,2,1,0:T(8,128)(2,1)S(1)}, u32[]{:S(2)}, u32[]{:S(2)}) %all-to-all-start) | async-done | bytes 458784 | tf_op jit(solution)/shard_map/all_to_all | solution.py:301
  24.2 0.4 fusion.19
  24.6 0.1 fusion.140
  24.7 0.2 copy.50
  24.9 0.2 copy.49
  25.2 0.2 add_convert_fusion.1
  25.3 0.3 fusion.8
  25.8 0.2 fusion.26
  26.1 0.1 subtract_convert_fusion.3
  26.2 0.4 fusion.24
  26.6 0.2 copy-done.5
  26.7 0.9 %fusion.7 = bf16[16,4,16,128]{3,2,1,0:T(8,128)(2,1)} fusion(f32[16,4,16,128]{3,0,2,1:T(8,128)S(1)} %fusion.24, f32[4]{0:T(128)S(1)} %copy-done.5), kind=kLoop, calls=%fused_computation.15 | loop fusion | flops 262144 | bytes 786448 | tf_op jit(solution)/shard_map/convert_element_type | solution.py:127
  27.6 3.9 %all-to-all-start.1 = ((bf16[16,4,16,128]{3,2,1,0:T(8,128)(2,1)}), bf16[16,4,16,128]{3,2,1,0:T(8,128)(2,1)S(1)}, u32[]{:S(2)}, u32[]{:S(2)}) async-start(bf16[16,4,16,128]{3,2,1,0:T(8,128)(2,1)} %fusion.7), calls=%async_computation.1 | async-start | bytes 524288 | tf_op jit(solution)/shard_map/all_to_all | solution.py:308
  31.5 2.3 %convolution_sine_fusion.1 = f32[64,2048]{1,0:T(8,128)S(1)} fusion(f32[64,16]{0,1:T(8,128)S(1)} %get-tuple-element.51, f32[8,2048]{1,0:T(8,128)S(1)} %get-tuple-element.101, f32[8,2048]{1,0:T(8,128)S(1)} %get-tuple-element.100), kind=kOutput, calls=%fused_computation.1 | convolution fusion | flops 25198592 | bytes 659456 | tf_op jit(solution)/shard_map/dot_general | solution.py:20
  33.8 0.1 dynamic-slice_negate_fusion
  33.9 2.4 %convolution_sine_fusion = f32[64,2048]{1,0:T(8,128)S(1)} fusion(f32[64,64]{1,0:T(8,128)S(1)} %get-tuple-element.50, f32[64,2048]{1,0:T(8,128)S(1)} %convolution_sine_fusion.1), kind=kOutput, calls=%fused_computation | convolution fusion | flops 100663296 | bytes 1064960 | tf_op jit(solution)/shard_map/dot_general | solution.py:21
  36.3 0.5 fusion.4
  36.8 4.8 %all-to-all-done.1.refs_2_ = bf16[16,4,16,128]{3,2,1,0:T(8,128)(2,1)S(1)} async-done(((bf16[16,4,16,128]{3,2,1,0:T(8,128)(2,1)}), bf16[16,4,16,128]{3,2,1,0:T(8,128)(2,1)S(1)}, u32[]{:S(2)}, u32[]{:S(2)}) %all-to-all-start.1) | async-done | bytes 262176 | tf_op jit(solution)/shard_map/all_to_all | solution.py:308
  41.6 0.7 copy-done
  42.3 4.3 %shard_map.177 = (bf16[16,7,16,128]{3,2,1,0:T(8,128)(2,1)}, bf16[4,256,128]{2,1,0:T(8,128)(2,1)}, f32[256,128]{1,0:T(8,128)}, f32[3,256,128]{2,1,0:T(8,128)}) custom-call(bf16[256,128]{1,0:T(8,128)(2,1)} %refs_0_.3, bf16[3,256,128]{2,1,0:T(8,128)(2,1)} %refs_1_.3, bf16[16,4,16,128]{3,2,1,0:T(8,128)(2,1)} %copy-done, ...), custom_call_target="tpu_custom_call" | custom-call | tf_op jit(solution)/shard_map/pallas_call | solution.py:238
  46.6 3.6 %all-to-all-start.2 = ((bf16[16,7,16,128]{3,2,1,0:T(8,128)(2,1)}), bf16[16,7,16,128]{3,2,1,0:T(8,128)(2,1)S(1)}, u32[]{:S(2)}, u32[]{:S(2)}) async-start(bf16[16,7,16,128]{3,2,1,0:T(8,128)(2,1)} %get-tuple-element.48), calls=%async_computation.2 | async-start | bytes 917504 | tf_op jit(solution)/shard_map/all_to_all | solution.py:301
  50.2 0.2 fusion.81
  50.5 0.2 fusion.63
  50.6 12.8 %all-to-all-done.2 = bf16[16,7,16,128]{3,2,1,0:T(8,128)(2,1)S(1)} async-done(((bf16[16,7,16,128]{3,2,1,0:T(8,128)(2,1)}), bf16[16,7,16,128]{3,2,1,0:T(8,128)(2,1)S(1)}, u32[]{:S(2)}, u32[]{:S(2)}) %all-to-all-start.2) | async-done | bytes 458784 | tf_op jit(solution)/shard_map/all_to_all | solution.py:301
  63.4 0.4 fusion.16
  63.8 0.1 fusion.139
  63.9 0.2 copy.58
  64.1 0.2 copy.57
  64.3 0.2 add_convert_fusion
  64.5 0.3 fusion.12
  65.0 0.2 fusion.42
  65.3 0.1 subtract_convert_fusion.2
  65.4 0.4 fusion.22
  65.7 0.2 fusion.6
  66.0 13.8 %all_to_all.20.refs_2_ = bf16[16,4,16,128]{3,2,1,0:T(8,128)(2,1)} all-to-all(bf16[16,4,16,128]{3,2,1,0:T(8,128)(2,1)S(1)} %fusion.6), channel_id=1, replica_groups=mesh['grp'=2,'seq'=16] {'seq'}, dimensions={0} | all-to-all | bytes 524288 | tf_op jit(solution)/shard_map/all_to_all | solution.py:308
  79.7 3.4 %shard_map.178 = (bf16[256,128]{1,0:T(8,128)(2,1)}, bf16[3,256,128]{2,1,0:T(8,128)(2,1)}) custom-call(f32[256,128]{1,0:T(8,128)} %get-tuple-element.46.refs_0_, f32[3,256,128]{2,1,0:T(8,128)} %get-tuple-element.47.refs_1_, bf16[16,4,16,128]{3,2,1,0:T(8,128)(2,1)} %all_to_all.20.refs_2_, bf16[4,256,128]{2,1,0:T(8,128)(2,1)} %get-tuple-element.53.refs_3_, ...), custom_call_target="tpu_custom_call" | custom-call | tf_op jit(solution)/shard_map/pallas_call | solution.py:238
  (44 shorter events, 1.0 us)
Async XLA Ops:
  0.6 10.4 %copy-start.4 = (f32[2,256]{1,0:T(2,128)S(1)}, f32[2,256]{1,0:T(2,128)}, u32[]{:S(2)}) copy-start(f32[2,256]{1,0:T(2,128)} %param.35) | copy-start | bytes 6148
  0.6 10.4 %copy-start.3 = (f32[2,64,16]{1,2,0:T(8,128)S(1)}, f32[2,64,16]{1,2,0:T(8,128)}, u32[]{:S(2)}) copy-start(f32[2,64,16]{1,2,0:T(8,128)} %param.32) | copy-start | bytes 24580
  0.7 10.4 %copy-start.2 = (f32[2,64,64]{2,1,0:T(8,128)S(1)}, f32[2,64,64]{2,1,0:T(8,128)}, u32[]{:S(2)}) copy-start(f32[2,64,64]{2,1,0:T(8,128)} %param.33) | copy-start | bytes 98308
  0.7 10.8 %copy-start.1 = (f32[2,256,64]{1,2,0:T(8,128)S(1)}, f32[2,256,64]{1,2,0:T(8,128)}, u32[]{:S(2)}) copy-start(f32[2,256,64]{1,2,0:T(8,128)} %param.34) | copy-start | bytes 393220
  3.6 20.6 %all-to-all-start = ((bf16[16,7,16,128]{3,2,1,0:T(8,128)(2,1)}), bf16[16,7,16,128]{3,2,1,0:T(8,128)(2,1)S(1)}, u32[]{:S(2)}, u32[]{:S(2)}) async-start(bf16[16,7,16,128]{3,2,1,0:T(8,128)(2,1)} %get-tuple-element.40), calls=%async_computation | async-start | bytes 917504 | tf_op jit(solution)/shard_map/all_to_all | solution.py:301
  16.3 1.6 %copy-start.6 = (f32[9]{0:T(128)S(1)}, f32[9]{0:T(128)}, u32[]{:S(2)}) copy-start(f32[9]{0:T(128)} %constant.128.clone.1) | copy-start | bytes 112
  26.1 0.7 copy-start.5
  27.6 13.9 %all-to-all-start.1 = ((bf16[16,4,16,128]{3,2,1,0:T(8,128)(2,1)}), bf16[16,4,16,128]{3,2,1,0:T(8,128)(2,1)S(1)}, u32[]{:S(2)}, u32[]{:S(2)}) async-start(bf16[16,4,16,128]{3,2,1,0:T(8,128)(2,1)} %fusion.7), calls=%async_computation.1 | async-start | bytes 524288 | tf_op jit(solution)/shard_map/all_to_all | solution.py:308
  41.6 0.7 copy-start
  46.6 16.8 %all-to-all-start.2 = ((bf16[16,7,16,128]{3,2,1,0:T(8,128)(2,1)}), bf16[16,7,16,128]{3,2,1,0:T(8,128)(2,1)S(1)}, u32[]{:S(2)}, u32[]{:S(2)}) async-start(bf16[16,7,16,128]{3,2,1,0:T(8,128)(2,1)} %get-tuple-element.48), calls=%async_computation.2 | async-start | bytes 917504 | tf_op jit(solution)/shard_map/all_to_all | solution.py:301

commit v10 on v9

--- a/solution.py
+++ b/solution.py
@@ -53,6 +53,7 @@
         weight = jnp.ones((half,), f32)
     else:
         weight = jnp.full((half,), 2.0, f32).at[0].set(1.0).at[half - 1].set(1.0)
+    weight = weight / length
     lead_inv = jnp.concatenate([cos_s.T * weight, -sin_s.T * weight], axis=1)
     ang_t = turns(half, local, length)
     tw_c = jnp.cos(ang_t)[:, None, None, :]
@@ -112,19 +113,17 @@
     spec = forward_dft(received.astype(jnp.float32), tables, FAST)
     re, im = spec[..., :local], spec[..., local:]
     h_r, h_i = filt_spec[..., :local], filt_spec[..., local:]
+    inv_root = 1.0 / math.sqrt(length)
     p_r, p_i = cmul(re[:, 0], im[:, 0], h_r, h_i)
     outs_r, outs_i = [p_r], [p_i]
     for j in range(3):
         one, two = (j + 1) % 3, (j + 2) % 3
         a_r, a_i = cmul(re[:, 1 + one], im[:, 1 + one], re[:, 4 + two], im[:, 4 + two])
         b_r, b_i = cmul(re[:, 1 + two], im[:, 1 + two], re[:, 4 + one], im[:, 4 + one])
-        outs_r.append(a_r - b_r)
-        outs_i.append(a_i - b_i)
+        outs_r.append((a_r - b_r) * inv_root)
+        outs_i.append((a_i - b_i) * inv_root)
     prod = jnp.concatenate([jnp.stack(outs_r, axis=1), jnp.stack(outs_i, axis=1)], axis=-1)
-    result = inverse_dft(prod, tables, FAST)
-    inv_root = 1.0 / math.sqrt(length)
-    scale = jnp.array([1.0, inv_root, inv_root, inv_root], dtype=jnp.float32) / length
-    return (result * scale[None, :, None, None]).astype(jnp.bfloat16)
+    return inverse_dft(prod, tables, FAST).astype(jnp.bfloat16)
 
 
 def gelu_tanh(x):

time: 83.6 us -> 83.3 us (level)
  other arithmetic: 3.32 us -> 2.24 us
    convert_element_type x2 -> x0, other arithmetic: 1.1 us -> none  [convolve(): return (result * scale[None, :, None, None]).astype(jnp.bfloat16)]
    dot_general x0 -> x2, local copies, waits for them, and re-layouts: none -> 0.85 us  [inverse_dft(): whole = jnp.dot(lead_inv, stacked, preferred_element_type=jnp.float32)]
    unnamed x26 -> x24, local copies, waits for them, and re-layouts: 1.88 us -> 1.72 us
where the time goes in v10:
time: 83.3 us; the launch traced here: 82.7 us
  waiting for transfers between devices  23.8 us (29%)
  starting transfers between devices  14.9 us (18%)
  blocking collectives  13.8 us (17%)
  matrix products  13.4 us (16%)
  Pallas kernels  10.6 us (13%)
  local copies, waits for them, and re-layouts  2.92 us (4%)
  other arithmetic  2.24 us (3%)
  between operations  1.14 us (1%)
    all_to_all x2, waiting for transfers between devices, per_device(): regrouped = lax.all_to_all(outgoing, 'seq', 0, 0, tiled=True)  19 us
    all_to_all x1, blocking collectives, per_device(): returned = lax.all_to_all(convolved, 'seq', 0, 0, tiled=True)  13.8 us
    all_to_all x2, starting transfers between devices, per_device(): regrouped = lax.all_to_all(outgoing, 'seq', 0, 0, tiled=True)  10.9 us
    pallas_call x3, Pallas kernels, token_step(): pl.pallas_call(kernel, grid=(1,), in_specs=specs, out_specs=[full(shape)...  10.6 us
    dot_general x2, matrix products, filter_values(): hid_two = jnp.sin(jnp.dot(second, hid_one, precision=HIGH))  4.85 us
    all_to_all x1, waiting for transfers between devices, per_device(): returned = lax.all_to_all(convolved, 'seq', 0, 0, tiled=True)  4.76 us
    dot_general x2, matrix products, filter_values(): hid_one = jnp.sin(jnp.dot(first, feats, precision=HIGH))  4.53 us
    all_to_all x1, starting transfers between devices, per_device(): returned = lax.all_to_all(convolved, 'seq', 0, 0, tiled=True)  3.9 us
  transfers between devices with their start and end apart: 3, of which 3 were waited for; matrix products, arithmetic and copies ran while one was open for 15% of the time, Pallas kernels for 0%

profile of v10, /device:TPU:0, one launch (start us, length us, event | category | flops | bytes accessed | tf_op | source)
XLA Modules:
  0.0 82.7 jit_solution(16322770745413388648)
XLA Ops:
  0.7 2.9 %shard_map.158 = (bf16[16,7,16,128]{3,2,1,0:T(8,128)(2,1)}, bf16[4,256,128]{2,1,0:T(8,128)(2,1)}) custom-call(bf16[256,128]{1,0:T(8,128)(2,1)} %refs_0_.3, bf16[3,256,128]{2,1,0:T(8,128)(2,1)} %refs_1_.3, bf16[2,768,256]{2,1,0:T(8,128)(2,1)} %refs_11_.1, bf16[2,768,256]{2,1,0:T(8,128)(2,1)} %refs_12_.1, f32[2,4,256]{2,1,0:T(4,128)} %refs_10_.3), custom_call_target="tpu_custom_call" | custom-call | tf_op jit(solution)/shard_map/pallas_call | solution.py:237
  3.6 7.4 %all-to-all-start = ((bf16[16,7,16,128]{3,2,1,0:T(8,128)(2,1)}), bf16[16,7,16,128]{3,2,1,0:T(8,128)(2,1)S(1)}, u32[]{:S(2)}, u32[]{:S(2)}) async-start(bf16[16,7,16,128]{3,2,1,0:T(8,128)(2,1)} %get-tuple-element.40), calls=%async_computation | async-start | bytes 917504 | tf_op jit(solution)/shard_map/all_to_all | solution.py:300
  11.0 0.1 negate_convert_fusion.1
  11.1 0.3 fusion.97
  11.5 0.1 dynamic-slice_negate_fusion.1
  11.6 2.3 %convolution_sine_fusion.3 = f32[64,2048]{1,0:T(8,128)S(1)} fusion(f32[64,16]{0,1:T(8,128)S(1)} %get-tuple-element.43, f32[8,2048]{1,0:T(8,128)S(1)} %get-tuple-element.101, f32[8,2048]{1,0:T(8,128)S(1)} %get-tuple-element.100), kind=kOutput, calls=%fused_computation.3 | convolution fusion | flops 25198592 | bytes 659456 | tf_op jit(solution)/shard_map/dot_general | solution.py:20
  13.9 2.4 %convolution_sine_fusion.2 = f32[64,2048]{1,0:T(8,128)S(1)} fusion(f32[64,64]{1,0:T(8,128)S(1)} %get-tuple-element.42, f32[64,2048]{1,0:T(8,128)S(1)} %convolution_sine_fusion.3), kind=kOutput, calls=%fused_computation.2 | convolution fusion | flops 100663296 | bytes 1064960 | tf_op jit(solution)/shard_map/dot_general | solution.py:21
  16.3 0.5 fusion.5
  16.8 0.2 fusion.82
  17.1 0.3 fusion.100
  17.4 0.3 negate_convert_fusion
  17.7 0.2 fusion.63
  17.9 0.1 multiply_convert_fusion.13
  18.0 6.3 %all-to-all-done = bf16[16,7,16,128]{3,2,1,0:T(8,128)(2,1)S(1)} async-done(((bf16[16,7,16,128]{3,2,1,0:T(8,128)(2,1)}), bf16[16,7,16,128]{3,2,1,0:T(8,128)(2,1)S(1)}, u32[]{:S(2)}, u32[]{:S(2)}) %all-to-all-start) | async-done | bytes 458784 | tf_op jit(solution)/shard_map/all_to_all | solution.py:300
  24.2 0.4 fusion.17
  24.6 0.1 fusion.138
  24.7 0.2 copy.48
  25.0 0.2 copy.47
  25.2 0.2 add_convert_fusion.1
  25.3 0.3 fusion.6
  25.9 0.2 fusion.24
  26.1 0.1 subtract_convert_fusion.3
  26.2 0.4 fusion.22
  26.6 0.8 copy.87
  27.4 3.9 %all-to-all-start.1 = ((bf16[16,4,16,128]{3,2,1,0:T(8,128)(2,1)}), bf16[16,4,16,128]{3,2,1,0:T(8,128)(2,1)S(1)}, u32[]{:S(2)}, u32[]{:S(2)}) async-start(bf16[16,4,16,128]{3,2,1,0:T(8,128)(2,1)} %copy.87), calls=%async_computation.1 | async-start | bytes 524288 | tf_op jit(solution)/shard_map/all_to_all | solution.py:307
  31.3 2.3 %convolution_sine_fusion.1 = f32[64,2048]{1,0:T(8,128)S(1)} fusion(f32[64,16]{0,1:T(8,128)S(1)} %get-tuple-element.51, f32[8,2048]{1,0:T(8,128)S(1)} %get-tuple-element.101, f32[8,2048]{1,0:T(8,128)S(1)} %get-tuple-element.100), kind=kOutput, calls=%fused_computation.1 | convolution fusion | flops 25198592 | bytes 659456 | tf_op jit(solution)/shard_map/dot_general | solution.py:20
  33.6 0.1 dynamic-slice_negate_fusion
  33.6 2.4 %convolution_sine_fusion = f32[64,2048]{1,0:T(8,128)S(1)} fusion(f32[64,64]{1,0:T(8,128)S(1)} %get-tuple-element.50, f32[64,2048]{1,0:T(8,128)S(1)} %convolution_sine_fusion.1), kind=kOutput, calls=%fused_computation | convolution fusion | flops 100663296 | bytes 1064960 | tf_op jit(solution)/shard_map/dot_general | solution.py:21
  36.1 0.5 fusion.4
  36.6 4.8 %all-to-all-done.1.refs_2_ = bf16[16,4,16,128]{3,2,1,0:T(8,128)(2,1)S(1)} async-done(((bf16[16,4,16,128]{3,2,1,0:T(8,128)(2,1)}), bf16[16,4,16,128]{3,2,1,0:T(8,128)(2,1)S(1)}, u32[]{:S(2)}, u32[]{:S(2)}) %all-to-all-start.1) | async-done | bytes 262176 | tf_op jit(solution)/shard_map/all_to_all | solution.py:307
  41.3 0.7 copy-done
  42.1 4.3 %shard_map.159 = (bf16[16,7,16,128]{3,2,1,0:T(8,128)(2,1)}, bf16[4,256,128]{2,1,0:T(8,128)(2,1)}, f32[256,128]{1,0:T(8,128)}, f32[3,256,128]{2,1,0:T(8,128)}) custom-call(bf16[256,128]{1,0:T(8,128)(2,1)} %refs_0_.3, bf16[3,256,128]{2,1,0:T(8,128)(2,1)} %refs_1_.3, bf16[16,4,16,128]{3,2,1,0:T(8,128)(2,1)} %copy-done, ...), custom_call_target="tpu_custom_call" | custom-call | tf_op jit(solution)/shard_map/pallas_call | solution.py:237
  46.4 3.6 %all-to-all-start.2 = ((bf16[16,7,16,128]{3,2,1,0:T(8,128)(2,1)}), bf16[16,7,16,128]{3,2,1,0:T(8,128)(2,1)S(1)}, u32[]{:S(2)}, u32[]{:S(2)}) async-start(bf16[16,7,16,128]{3,2,1,0:T(8,128)(2,1)} %get-tuple-element.48), calls=%async_computation.2 | async-start | bytes 917504 | tf_op jit(solution)/shard_map/all_to_all | solution.py:300
  50.0 0.2 fusion.79
  50.2 0.2 fusion.61
  50.4 12.8 %all-to-all-done.2 = bf16[16,7,16,128]{3,2,1,0:T(8,128)(2,1)S(1)} async-done(((bf16[16,7,16,128]{3,2,1,0:T(8,128)(2,1)}), bf16[16,7,16,128]{3,2,1,0:T(8,128)(2,1)S(1)}, u32[]{:S(2)}, u32[]{:S(2)}) %all-to-all-start.2) | async-done | bytes 458784 | tf_op jit(solution)/shard_map/all_to_all | solution.py:300
  63.2 0.4 fusion.14
  63.5 0.1 fusion.137
  63.7 0.2 copy.56
  63.9 0.2 copy.55
  64.1 0.2 add_convert_fusion
  64.3 0.3 fusion.10
  64.8 0.2 fusion.40
  65.0 0.1 subtract_convert_fusion.2
  65.2 0.4 fusion.20
  65.5 0.1 copy.86
  65.6 13.8 %all_to_all.20.refs_2_ = bf16[16,4,16,128]{3,2,1,0:T(8,128)(2,1)} all-to-all(bf16[16,4,16,128]{3,2,1,0:T(8,128)(2,1)S(1)} %copy.86), channel_id=1, replica_groups=mesh['grp'=2,'seq'=16] {'seq'}, dimensions={0} | all-to-all | bytes 524288 | tf_op jit(solution)/shard_map/all_to_all | solution.py:307
  79.4 3.4 %shard_map.160 = (bf16[256,128]{1,0:T(8,128)(2,1)}, bf16[3,256,128]{2,1,0:T(8,128)(2,1)}) custom-call(f32[256,128]{1,0:T(8,128)} %get-tuple-element.46.refs_0_, f32[3,256,128]{2,1,0:T(8,128)} %get-tuple-element.47.refs_1_, bf16[16,4,16,128]{3,2,1,0:T(8,128)(2,1)} %all_to_all.20.refs_2_, bf16[4,256,128]{2,1,0:T(8,128)(2,1)} %get-tuple-element.53.refs_3_, ...), custom_call_target="tpu_custom_call" | custom-call | tf_op jit(solution)/shard_map/pallas_call | solution.py:237
  (42 shorter events, 1.0 us)
Async XLA Ops:
  0.6 10.4 %copy-start.4 = (f32[2,256]{1,0:T(2,128)S(1)}, f32[2,256]{1,0:T(2,128)}, u32[]{:S(2)}) copy-start(f32[2,256]{1,0:T(2,128)} %param.33) | copy-start | bytes 6148
  0.6 10.5 %copy-start.3 = (f32[2,64,16]{1,2,0:T(8,128)S(1)}, f32[2,64,16]{1,2,0:T(8,128)}, u32[]{:S(2)}) copy-start(f32[2,64,16]{1,2,0:T(8,128)} %param.30) | copy-start | bytes 24580
  0.7 10.5 %copy-start.2 = (f32[2,64,64]{2,1,0:T(8,128)S(1)}, f32[2,64,64]{2,1,0:T(8,128)}, u32[]{:S(2)}) copy-start(f32[2,64,64]{2,1,0:T(8,128)} %param.31) | copy-start | bytes 98308
  0.7 10.8 %copy-start.1 = (f32[2,256,64]{1,2,0:T(8,128)S(1)}, f32[2,256,64]{1,2,0:T(8,128)}, u32[]{:S(2)}) copy-start(f32[2,256,64]{1,2,0:T(8,128)} %param.32) | copy-start | bytes 393220
  3.6 20.6 %all-to-all-start = ((bf16[16,7,16,128]{3,2,1,0:T(8,128)(2,1)}), bf16[16,7,16,128]{3,2,1,0:T(8,128)(2,1)S(1)}, u32[]{:S(2)}, u32[]{:S(2)}) async-start(bf16[16,7,16,128]{3,2,1,0:T(8,128)(2,1)} %get-tuple-element.40), calls=%async_computation | async-start | bytes 917504 | tf_op jit(solution)/shard_map/all_to_all | solution.py:300
  16.3 1.6 %copy-start.5 = (f32[9]{0:T(128)S(1)}, f32[9]{0:T(128)}, u32[]{:S(2)}) copy-start(f32[9]{0:T(128)} %constant.125.clone.1) | copy-start | bytes 112
  27.4 13.9 %all-to-all-start.1 = ((bf16[16,4,16,128]{3,2,1,0:T(8,128)(2,1)}), bf16[16,4,16,128]{3,2,1,0:T(8,128)(2,1)S(1)}, u32[]{:S(2)}, u32[]{:S(2)}) async-start(bf16[16,4,16,128]{3,2,1,0:T(8,128)(2,1)} %copy.87), calls=%async_computation.1 | async-start | bytes 524288 | tf_op jit(solution)/shard_map/all_to_all | solution.py:307
  41.3 0.7 copy-start
  46.4 16.8 %all-to-all-start.2 = ((bf16[16,7,16,128]{3,2,1,0:T(8,128)(2,1)}), bf16[16,7,16,128]{3,2,1,0:T(8,128)(2,1)S(1)}, u32[]{:S(2)}, u32[]{:S(2)}) async-start(bf16[16,7,16,128]{3,2,1,0:T(8,128)(2,1)} %get-tuple-element.48), calls=%async_computation.2 | async-start | bytes 917504 | tf_op jit(solution)/shard_map/all_to_all | solution.py:300

commit v11 on v10

--- a/solution.py
+++ b/solution.py
@@ -299,11 +299,6 @@
             outgoing = planes.reshape(7, shards, own, tok_local).transpose(1, 0, 2, 3)
         regrouped = lax.all_to_all(outgoing, "seq", 0, 0, tiled=True)
         convolved = convolve(regrouped, spec_next, tables)
-        if layer + 1 < depth:
-            tied = lax.optimization_barrier(
-                (pe_w1[layer + 1], pe_w2[layer + 1], pe_w3[layer + 1], rates[layer + 1], convolved)
-            )
-            spec_next = filter_spec(*tied[:4])
         returned = lax.all_to_all(convolved, "seq", 0, 0, tiled=True)
         arrays["conv"] = returned
         if not packed:
@@ -311,6 +306,10 @@
         arrays["query"] = query
         if layer + 1 < depth:
             planes, query, new_s, new_v = token_step(layer, layer + 1, arrays, weights, shards)
+            tied = lax.optimization_barrier(
+                (pe_w1[layer + 1], pe_w2[layer + 1], pe_w3[layer + 1], rates[layer + 1], planes)
+            )
+            spec_next = filter_spec(*tied[:4])
             arrays["state_s"], arrays["state_v"] = new_s, new_v
         else:
             return tuple(token_step(layer, None, arrays, weights, shards))

time: 83.3 us -> 81.6 us (0.980)
  blocking collectives: 13.8 us -> 27.6 us
  waiting for transfers between devices: 23.8 us -> 13.5 us
  starting transfers between devices: 14.9 us -> 11.1 us
  local copies, waits for them, and re-layouts: 2.92 us -> 1.48 us
    all_to_all x1 -> x2, blocking collectives: 13.8 us -> 27.6 us  [per_device(): returned = lax.all_to_all(convolved, 'seq', 0, 0, tiled=True)]
    all_to_all x2, waiting for transfers between devices: 19 us -> 13.5 us  [per_device(): regrouped = lax.all_to_all(outgoing, 'seq', 0, 0, tiled=True)]
    all_to_all x1 -> x0, waiting for transfers between devices: 4.76 us -> none  [per_device(): returned = lax.all_to_all(convolved, 'seq', 0, 0, tiled=True)]
    all_to_all x1 -> x0, starting transfers between devices: 3.9 us -> none  [per_device(): returned = lax.all_to_all(convolved, 'seq', 0, 0, tiled=True)]
    unnamed x24 -> x22, local copies, waits for them, and re-layouts: 1.72 us -> 0.99 us
  transfers between devices with their start and end apart: 3 -> 2, of which waited for: 3 -> 2; matrix products, arithmetic and copies ran while one was open for 15% -> 15% of each run, Pallas kernels for 0% -> 0%
where the time goes in v11:
time: 81.6 us; the launch traced here: 81.2 us
  blocking collectives  27.6 us (34%)
  matrix products  13.5 us (17%)
  waiting for transfers between devices  13.5 us (17%)
  starting transfers between devices  11.1 us (14%)
  Pallas kernels  10.6 us (13%)
  other arithmetic  2.24 us (3%)
  local copies, waits for them, and re-layouts  1.48 us (2%)
  between operations  1.14 us (1%)
    all_to_all x2, blocking collectives, per_device(): returned = lax.all_to_all(convolved, 'seq', 0, 0, tiled=True)  27.6 us
    all_to_all x2, waiting for transfers between devices, per_device(): regrouped = lax.all_to_all(outgoing, 'seq', 0, 0, tiled=True)  13.5 us
    all_to_all x2, starting transfers between devices, per_device(): regrouped = lax.all_to_all(outgoing, 'seq', 0, 0, tiled=True)  11.1 us
    pallas_call x3, Pallas kernels, token_step(): pl.pallas_call(kernel, grid=(1,), in_specs=specs, out_specs=[full(shape)...  10.6 us
    dot_general x2, matrix products, filter_values(): hid_two = jnp.sin(jnp.dot(second, hid_one, precision=HIGH))  4.86 us
    dot_general x2, matrix products, filter_values(): hid_one = jnp.sin(jnp.dot(first, feats, precision=HIGH))  4.53 us
  transfers between devices with their start and end apart: 2, of which 2 were waited for; matrix products, arithmetic and copies ran while one was open for 15% of the time, Pallas kernels for 0%

profile of v11, /device:TPU:0, one launch (start us, length us, event | category | flops | bytes accessed | tf_op | source)
XLA Modules:
  0.0 81.2 jit_solution(4069862480557787248)
XLA Ops:
  0.7 2.9 %shard_map.158 = (bf16[16,7,16,128]{3,2,1,0:T(8,128)(2,1)}, bf16[4,256,128]{2,1,0:T(8,128)(2,1)}) custom-call(bf16[256,128]{1,0:T(8,128)(2,1)} %refs_0_.3, bf16[3,256,128]{2,1,0:T(8,128)(2,1)} %refs_1_.3, bf16[2,768,256]{2,1,0:T(8,128)(2,1)} %refs_11_.1, bf16[2,768,256]{2,1,0:T(8,128)(2,1)} %refs_12_.1, f32[2,4,256]{2,1,0:T(4,128)} %refs_10_.3), custom_call_target="tpu_custom_call" | custom-call | tf_op jit(solution)/shard_map/pallas_call | solution.py:237
  3.6 7.4 %all-to-all-start = ((bf16[16,7,16,128]{3,2,1,0:T(8,128)(2,1)}), bf16[16,7,16,128]{3,2,1,0:T(8,128)(2,1)S(1)}, u32[]{:S(2)}, u32[]{:S(2)}) async-start(bf16[16,7,16,128]{3,2,1,0:T(8,128)(2,1)} %get-tuple-element.40), calls=%async_computation | async-start | bytes 917504 | tf_op jit(solution)/shard_map/all_to_all | solution.py:300
  11.0 0.1 negate_convert_fusion.1
  11.1 0.3 fusion.97
  11.5 0.1 dynamic-slice_negate_fusion.1
  11.6 2.3 %convolution_sine_fusion.3 = f32[64,2048]{1,0:T(8,128)S(1)} fusion(f32[64,16]{0,1:T(8,128)S(1)} %get-tuple-element.43, f32[8,2048]{1,0:T(8,128)S(1)} %get-tuple-element.101, f32[8,2048]{1,0:T(8,128)S(1)} %get-tuple-element.100), kind=kOutput, calls=%fused_computation.3 | convolution fusion | flops 25198592 | bytes 659456 | tf_op jit(solution)/shard_map/dot_general | solution.py:20
  13.8 2.4 %convolution_sine_fusion.2 = f32[64,2048]{1,0:T(8,128)S(1)} fusion(f32[64,64]{1,0:T(8,128)S(1)} %get-tuple-element.42, f32[64,2048]{1,0:T(8,128)S(1)} %convolution_sine_fusion.3), kind=kOutput, calls=%fused_computation.2 | convolution fusion | flops 100663296 | bytes 1064960 | tf_op jit(solution)/shard_map/dot_general | solution.py:21
  16.3 0.5 fusion.5
  16.8 0.2 fusion.82
  17.1 0.3 fusion.100
  17.4 0.3 negate_convert_fusion
  17.7 0.2 fusion.63
  17.9 0.1 multiply_convert_fusion.13
  17.9 6.3 %all-to-all-done = bf16[16,7,16,128]{3,2,1,0:T(8,128)(2,1)S(1)} async-done(((bf16[16,7,16,128]{3,2,1,0:T(8,128)(2,1)}), bf16[16,7,16,128]{3,2,1,0:T(8,128)(2,1)S(1)}, u32[]{:S(2)}, u32[]{:S(2)}) %all-to-all-start) | async-done | bytes 458784 | tf_op jit(solution)/shard_map/all_to_all | solution.py:300
  24.2 0.4 fusion.17
  24.6 0.1 fusion.138
  24.7 0.2 copy.48
  24.9 0.2 copy.47
  25.2 0.2 add_convert_fusion.1
  25.3 0.3 fusion.6
  25.6 0.1 multiply_convert_fusion.11
  25.7 0.1 multiply_convert_fusion.8
  25.8 0.2 fusion.24
  26.1 0.1 subtract_convert_fusion.3
  26.2 0.4 fusion.22
  26.6 0.1 copy.87
  26.7 13.8 %all_to_all.20.refs_2_ = bf16[16,4,16,128]{3,2,1,0:T(8,128)(2,1)} all-to-all(bf16[16,4,16,128]{3,2,1,0:T(8,128)(2,1)S(1)} %copy.87), channel_id=1, replica_groups=mesh['grp'=2,'seq'=16] {'seq'}, dimensions={0} | all-to-all | bytes 524288 | tf_op jit(solution)/shard_map/all_to_all | solution.py:302
  40.5 4.3 %shard_map.159 = (bf16[16,7,16,128]{3,2,1,0:T(8,128)(2,1)}, bf16[4,256,128]{2,1,0:T(8,128)(2,1)}, f32[256,128]{1,0:T(8,128)}, f32[3,256,128]{2,1,0:T(8,128)}) custom-call(bf16[256,128]{1,0:T(8,128)(2,1)} %refs_0_.3, bf16[3,256,128]{2,1,0:T(8,128)(2,1)} %refs_1_.3, bf16[16,4,16,128]{3,2,1,0:T(8,128)(2,1)} %all_to_all.20.refs_2_, ...), custom_call_target="tpu_custom_call" | custom-call | tf_op jit(solution)/shard_map/pallas_call | solution.py:237
  44.8 3.7 %all-to-all-start.2 = ((bf16[16,7,16,128]{3,2,1,0:T(8,128)(2,1)}), bf16[16,7,16,128]{3,2,1,0:T(8,128)(2,1)S(1)}, u32[]{:S(2)}, u32[]{:S(2)}) async-start(bf16[16,7,16,128]{3,2,1,0:T(8,128)(2,1)} %get-tuple-element.48), calls=%async_computation.2 | async-start | bytes 917504 | tf_op jit(solution)/shard_map/all_to_all | solution.py:300
  48.6 0.1 dynamic-slice_negate_fusion
  48.6 2.3 %convolution_sine_fusion.1 = f32[64,2048]{1,0:T(8,128)S(1)} fusion(f32[64,16]{0,1:T(8,128)S(1)} %get-tuple-element.51, f32[8,2048]{1,0:T(8,128)S(1)} %get-tuple-element.101, f32[8,2048]{1,0:T(8,128)S(1)} %get-tuple-element.100), kind=kOutput, calls=%fused_computation.1 | convolution fusion | flops 25198592 | bytes 659456 | tf_op jit(solution)/shard_map/dot_general | solution.py:20
  50.9 2.4 %convolution_sine_fusion = f32[64,2048]{1,0:T(8,128)S(1)} fusion(f32[64,64]{1,0:T(8,128)S(1)} %get-tuple-element.50, f32[64,2048]{1,0:T(8,128)S(1)} %convolution_sine_fusion.1), kind=kOutput, calls=%fused_computation | convolution fusion | flops 100663296 | bytes 1064960 | tf_op jit(solution)/shard_map/dot_general | solution.py:21
  53.4 0.5 fusion.4
  53.8 0.2 fusion.79
  54.1 0.2 fusion.61
  54.3 7.3 %all-to-all-done.2 = bf16[16,7,16,128]{3,2,1,0:T(8,128)(2,1)S(1)} async-done(((bf16[16,7,16,128]{3,2,1,0:T(8,128)(2,1)}), bf16[16,7,16,128]{3,2,1,0:T(8,128)(2,1)S(1)}, u32[]{:S(2)}, u32[]{:S(2)}) %all-to-all-start.2) | async-done | bytes 458784 | tf_op jit(solution)/shard_map/all_to_all | solution.py:300
  61.6 0.4 fusion.14
  62.0 0.1 fusion.137
  62.1 0.2 copy.56
  62.3 0.2 copy.55
  62.5 0.2 add_convert_fusion
  62.7 0.3 fusion.10
  63.2 0.2 fusion.40
  63.5 0.1 subtract_convert_fusion.2
  63.6 0.4 fusion.20
  64.0 0.1 copy.86
  64.0 13.8 %all_to_all.21.refs_2_ = bf16[16,4,16,128]{3,2,1,0:T(8,128)(2,1)} all-to-all(bf16[16,4,16,128]{3,2,1,0:T(8,128)(2,1)S(1)} %copy.86), channel_id=1, replica_groups=mesh['grp'=2,'seq'=16] {'seq'}, dimensions={0} | all-to-all | bytes 524288 | tf_op jit(solution)/shard_map/all_to_all | solution.py:302
  77.8 3.4 %shard_map.160 = (bf16[256,128]{1,0:T(8,128)(2,1)}, bf16[3,256,128]{2,1,0:T(8,128)(2,1)}) custom-call(f32[256,128]{1,0:T(8,128)} %get-tuple-element.46.refs_0_, f32[3,256,128]{2,1,0:T(8,128)} %get-tuple-element.47.refs_1_, bf16[16,4,16,128]{3,2,1,0:T(8,128)(2,1)} %all_to_all.21.refs_2_, bf16[4,256,128]{2,1,0:T(8,128)(2,1)} %get-tuple-element.53.refs_3_, ...), custom_call_target="tpu_custom_call" | custom-call | tf_op jit(solution)/shard_map/pallas_call | solution.py:237
  (39 shorter events, 0.8 us)
Async XLA Ops:
  0.6 10.4 %copy-start.3 = (f32[2,256]{1,0:T(2,128)S(1)}, f32[2,256]{1,0:T(2,128)}, u32[]{:S(2)}) copy-start(f32[2,256]{1,0:T(2,128)} %param.33) | copy-start | bytes 6148
  0.6 10.4 %copy-start.2 = (f32[2,64,16]{1,2,0:T(8,128)S(1)}, f32[2,64,16]{1,2,0:T(8,128)}, u32[]{:S(2)}) copy-start(f32[2,64,16]{1,2,0:T(8,128)} %param.30) | copy-start | bytes 24580
  0.7 10.5 %copy-start.1 = (f32[2,64,64]{2,1,0:T(8,128)S(1)}, f32[2,64,64]{2,1,0:T(8,128)}, u32[]{:S(2)}) copy-start(f32[2,64,64]{2,1,0:T(8,128)} %param.31) | copy-start | bytes 98308
  0.7 10.8 %copy-start = (f32[2,256,64]{1,2,0:T(8,128)S(1)}, f32[2,256,64]{1,2,0:T(8,128)}, u32[]{:S(2)}) copy-start(f32[2,256,64]{1,2,0:T(8,128)} %param.32) | copy-start | bytes 393220
  3.6 20.6 %all-to-all-start = ((bf16[16,7,16,128]{3,2,1,0:T(8,128)(2,1)}), bf16[16,7,16,128]{3,2,1,0:T(8,128)(2,1)S(1)}, u32[]{:S(2)}, u32[]{:S(2)}) async-start(bf16[16,7,16,128]{3,2,1,0:T(8,128)(2,1)} %get-tuple-element.40), calls=%async_computation | async-start | bytes 917504 | tf_op jit(solution)/shard_map/all_to_all | solution.py:300
  16.3 1.6 %copy-start.4 = (f32[9]{0:T(128)S(1)}, f32[9]{0:T(128)}, u32[]{:S(2)}) copy-start(f32[9]{0:T(128)} %constant.125.clone.1) | copy-start | bytes 112
  44.8 16.8 %all-to-all-start.2 = ((bf16[16,7,16,128]{3,2,1,0:T(8,128)(2,1)}), bf16[16,7,16,128]{3,2,1,0:T(8,128)(2,1)S(1)}, u32[]{:S(2)}, u32[]{:S(2)}) async-start(bf16[16,7,16,128]{3,2,1,0:T(8,128)(2,1)} %get-tuple-element.48), calls=%async_computation.2 | async-start | bytes 917504 | tf_op jit(solution)/shard_map/all_to_all | solution.py:300

commit v12 on v11

--- a/solution.py
+++ b/solution.py
@@ -141,6 +141,9 @@
     def layer_spec(w, layer):
         return pl.BlockSpec((pl.Squeezed(),) + w.shape[1:], lambda i: (layer,) + (0,) * (w.ndim - 1))
 
+    def row_spec(w, layer, rows, block):
+        return pl.BlockSpec((pl.Squeezed(), rows, w.shape[2]), lambda i: (layer, block, 0))
+
     ins, specs = [state_s, state_v], [full(state_s.shape), full(state_v.shape)]
     post_names = ("w_out_s", "w_out_v", "w_up", "w_down", "w_mix", "w_gate")
     if post is not None:
@@ -150,13 +153,16 @@
             ins.append(weights[name])
             specs.append(layer_spec(weights[name], post))
     if pre is not None:
-        for name in ("w_qkw_s", "w_qkw_v", "gains_t"):
-            ins.append(weights[name])
-            specs.append(layer_spec(weights[name], pre))
+        for name in ("w_qkw_s", "w_qkw_v"):
+            for block in (1, 2):
+                ins.append(weights[name])
+                specs.append(row_spec(weights[name], pre, chans, block))
+        ins.append(weights["gains_t"])
+        specs.append(layer_spec(weights["gains_t"], pre))
     outs = []
     if pre is not None:
         plane_shape = (shards, 7, own, tok) if packed else (7, chans, tok)
-        outs += [(plane_shape, bf16), ((4, chans, tok), bf16)]
+        outs += [(plane_shape, bf16)]
         if post is not None:
             outs += [((chans, tok), f32), ((3, chans, tok), f32)]
     else:
@@ -202,9 +208,9 @@
             ss = ss + mm(wdn[...], hidden)
             sv = [sv[j] + mm(wmx[...], mlp_v[j]) * gate for j in range(3)]
         if pre is not None:
-            wqs, wqv, gq = [refs.pop(0) for _ in range(3)]
+            wqs_k, wqs_w, wqv_k, wqv_w, gq = [refs.pop(0) for _ in range(5)]
             g = gq[...].T
-            planes_ref, query_ref = refs.pop(0), refs.pop(0)
+            planes_ref = refs.pop(0)
 
             def put(p, value):
                 if packed:
@@ -215,14 +221,10 @@
 
             normed_s = snorm(ss, g[:, 0:1]).astype(bf16)
             normed_v = [v.astype(bf16) for v in vnorm(sv, g[:, 1:2])]
-            ps = mm(wqs[...], normed_s)
-            query_ref[0] = ps[:chans].astype(bf16)
-            put(0, (ps[chans : 2 * chans] * ps[2 * chans :]).astype(bf16))
+            put(0, (mm(wqs_k[...], normed_s) * mm(wqs_w[...], normed_s)).astype(bf16))
             for j in range(3):
-                pv = mm(wqv[...], normed_v[j]).astype(bf16)
-                query_ref[1 + j] = pv[:chans]
-                put(1 + j, pv[chans : 2 * chans])
-                put(4 + j, pv[2 * chans :])
+                put(1 + j, mm(wqv_k[...], normed_v[j]).astype(bf16))
+                put(4 + j, mm(wqv_w[...], normed_v[j]).astype(bf16))
             if post is not None:
                 ns_ref, nv_ref = refs.pop(0), refs.pop(0)
                 ns_ref[...] = ss
@@ -241,6 +243,35 @@
         out_specs=[full(shape) for shape, _ in outs],
         out_shape=[jax.ShapeDtypeStruct(shape, dtype) for shape, dtype in outs],
     )(*ins)
+
+
+def query_step(layer, state_s, state_v, weights):
+    f32, bf16 = jnp.float32, jnp.bfloat16
+    chans, tok = state_s.shape
+    w_s, w_v, gains = weights["w_qkw_s"], weights["w_qkw_v"], weights["gains_t"]
+    full = lambda shape: pl.BlockSpec(shape, lambda i, n=len(shape): (0,) * n)
+    rows = lambda w: pl.BlockSpec((pl.Squeezed(), chans, w.shape[2]), lambda i: (layer, 0, 0))
+    g_spec = pl.BlockSpec((pl.Squeezed(),) + gains.shape[1:], lambda i: (layer, 0, 0))
+
+    def kernel(ss_ref, sv_ref, ws_ref, wv_ref, g_ref, q_ref):
+        g = g_ref[...].T
+        ss = ss_ref[...].astype(f32)
+        sv = [sv_ref[j].astype(f32) for j in range(3)]
+        normed_s = (ss * lax.rsqrt(jnp.mean(ss * ss, axis=0, keepdims=True) + 1e-05) * g[:, 0:1]).astype(bf16)
+        total = sum(jnp.sum(x * x, axis=0, keepdims=True) for x in sv)
+        scale = lax.rsqrt(total / (3 * chans) + 1e-05)
+        q_ref[0] = jnp.dot(ws_ref[...], normed_s, preferred_element_type=f32).astype(bf16)
+        for j in range(3):
+            normed = (sv[j] * scale * g[:, 1:2]).astype(bf16)
+            q_ref[1 + j] = jnp.dot(wv_ref[...], normed, preferred_element_type=f32).astype(bf16)
+
+    return pl.pallas_call(
+        kernel,
+        grid=(1,),
+        in_specs=[full(state_s.shape), full(state_v.shape), rows(w_s), rows(w_v), g_spec],
+        out_specs=full((4, chans, tok)),
+        out_shape=jax.ShapeDtypeStruct((4, chans, tok), bf16),
+    )(state_s, state_v, w_s, w_v, gains)
 
 
 def per_device(
@@ -290,7 +321,9 @@
     }
     arrays = {"state_s": scalars, "state_v": vectors}
     packed = own % 16 == 0
-    planes, query = token_step(None, 0, arrays, weights, shards)
+    (planes,) = token_step(None, 0, arrays, weights, shards)
+    tied = lax.optimization_barrier((scalars, vectors, planes))
+    query = query_step(0, tied[0], tied[1], weights)
     tied = lax.optimization_barrier((pe_w1[0], pe_w2[0], pe_w3[0], rates[0], planes))
     spec_next = filter_spec(*tied[:4])
     for layer in range(depth):
@@ -298,6 +331,7 @@
         if not packed:
             outgoing = planes.reshape(7, shards, own, tok_local).transpose(1, 0, 2, 3)
         regrouped = lax.all_to_all(outgoing, "seq", 0, 0, tiled=True)
+        regrouped, query = lax.optimization_barrier((regrouped, query))
         convolved = convolve(regrouped, spec_next, tables)
         returned = lax.all_to_all(convolved, "seq", 0, 0, tiled=True)
         arrays["conv"] = returned
@@ -305,7 +339,8 @@
             arrays["conv"] = returned.transpose(1, 0, 2, 3).reshape(4, chans, tok_local)
         arrays["query"] = query
         if layer + 1 < depth:
-            planes, query, new_s, new_v = token_step(layer, layer + 1, arrays, weights, shards)
+            planes, new_s, new_v = token_step(layer, layer + 1, arrays, weights, shards)
+            query = query_step(layer + 1, new_s, new_v, weights)
             tied = lax.optimization_barrier(
                 (pe_w1[layer + 1], pe_w2[layer + 1], pe_w3[layer + 1], rates[layer + 1], planes)
             )

time: 81.6 us -> 81.2 us (level)
  waiting for transfers between devices: 13.5 us -> 8.73 us
  Pallas kernels: 10.6 us -> 14.9 us
    pallas_call x0 -> x2, Pallas kernels: none -> 4.83 us  [query_step(): pl.pallas_call(kernel, grid=(1,), in_specs=[full(state_s.shape), full(sta...]
    all_to_all x2, waiting for transfers between devices: 13.5 us -> 8.73 us  [per_device(): regrouped = lax.all_to_all(outgoing, 'seq', 0, 0, tiled=True)]
  transfers between devices with their start and end apart: 2 -> 2, of which waited for: 2 -> 2; matrix products, arithmetic and copies ran while one was open for 15% -> 15% of each run, Pallas kernels for 0% -> 6%
where the time goes in v12:
time: 81.2 us; the launch traced here: 80.7 us
  blocking collectives  27.6 us (34%)
  Pallas kernels  14.9 us (18%)
  matrix products  13.5 us (17%)
  starting transfers between devices  11.1 us (14%)
  waiting for transfers between devices  8.73 us (11%)
  other arithmetic  2.24 us (3%)
  local copies, waits for them, and re-layouts  1.48 us (2%)
  between operations  1.13 us (1%)
    all_to_all x2, blocking collectives, per_device(): returned = lax.all_to_all(convolved, 'seq', 0, 0, tiled=True)  27.6 us
    all_to_all x2, starting transfers between devices, per_device(): regrouped = lax.all_to_all(outgoing, 'seq', 0, 0, tiled=True)  11.1 us
    pallas_call x3, Pallas kernels, token_step(): pl.pallas_call(kernel, grid=(1,), in_specs=specs, out_specs=[full(shape)...  10.1 us
    all_to_all x2, waiting for transfers between devices, per_device(): regrouped = lax.all_to_all(outgoing, 'seq', 0, 0, tiled=True)  8.73 us
    dot_general x2, matrix products, filter_values(): hid_two = jnp.sin(jnp.dot(second, hid_one, precision=HIGH))  4.86 us
    pallas_call x2, Pallas kernels, query_step(): pl.pallas_call(kernel, grid=(1,), in_specs=[full(state_s.shape), full(sta...  4.83 us
    dot_general x2, matrix products, filter_values(): hid_one = jnp.sin(jnp.dot(first, feats, precision=HIGH))  4.53 us
  transfers between devices with their start and end apart: 2, of which 2 were waited for; matrix products, arithmetic and copies ran while one was open for 15% of the time, Pallas kernels for 6%

profile of v12, /device:TPU:0, one launch (start us, length us, event | category | flops | bytes accessed | tf_op | source)
XLA Modules:
  0.0 80.7 jit_solution(13090675356961932112)
XLA Ops:
  0.7 2.7 %shard_map.158 = bf16[16,7,16,128]{3,2,1,0:T(8,128)(2,1)} custom-call(bf16[256,128]{1,0:T(8,128)(2,1)} %refs_0_.3, bf16[3,256,128]{2,1,0:T(8,128)(2,1)} %refs_1_.3, bf16[2,768,256]{2,1,0:T(8,128)(2,1)} %ws_ref.3, bf16[2,768,256]{2,1,0:T(8,128)(2,1)} %ws_ref.3, bf16[2,768,256]{2,1,0:T(8,128)(2,1)} %wv_ref.3, bf16[2,768,256]{2,1,0:T(8,128)(2,1)} %wv_ref.3, ...), custom_call_target="tpu_custom_call" | custom-call | tf_op jit(solution)/shard_map/pallas_call | solution.py:239
  3.4 7.4 %all-to-all-start = ((bf16[16,7,16,128]{3,2,1,0:T(8,128)(2,1)}), bf16[16,7,16,128]{3,2,1,0:T(8,128)(2,1)S(1)}, u32[]{:S(2)}, u32[]{:S(2)}) async-start(bf16[16,7,16,128]{3,2,1,0:T(8,128)(2,1)} %shard_map.158), calls=%async_computation | async-start | bytes 917504 | tf_op jit(solution)/shard_map/all_to_all | solution.py:333
  10.8 0.1 negate_convert_fusion.1
  10.9 0.3 fusion.97
  11.3 0.1 dynamic-slice_negate_fusion.1
  11.4 2.3 %convolution_sine_fusion.3 = f32[64,2048]{1,0:T(8,128)S(1)} fusion(f32[64,16]{0,1:T(8,128)S(1)} %get-tuple-element.48, f32[8,2048]{1,0:T(8,128)S(1)} %get-tuple-element.107, f32[8,2048]{1,0:T(8,128)S(1)} %get-tuple-element.106), kind=kOutput, calls=%fused_computation.3 | convolution fusion | flops 25198592 | bytes 659456 | tf_op jit(solution)/shard_map/dot_general | solution.py:20
  13.7 2.4 %convolution_sine_fusion.2 = f32[64,2048]{1,0:T(8,128)S(1)} fusion(f32[64,64]{1,0:T(8,128)S(1)} %get-tuple-element.47, f32[64,2048]{1,0:T(8,128)S(1)} %convolution_sine_fusion.3), kind=kOutput, calls=%fused_computation.2 | convolution fusion | flops 100663296 | bytes 1064960 | tf_op jit(solution)/shard_map/dot_general | solution.py:21
  16.1 0.5 fusion.5
  16.6 0.2 fusion.82
  16.9 2.4 %shard_map.159.refs_3_ = bf16[4,256,128]{2,1,0:T(8,128)(2,1)} custom-call(bf16[256,128]{1,0:T(8,128)(2,1)} %refs_0_.3, bf16[3,256,128]{2,1,0:T(8,128)(2,1)} %refs_1_.3, bf16[2,768,256]{2,1,0:T(8,128)(2,1)} %ws_ref.3, bf16[2,768,256]{2,1,0:T(8,128)(2,1)} %wv_ref.3, f32[2,4,256]{2,1,0:T(4,128)} %refs_10_.3), custom_call_target="tpu_custom_call" | custom-call | tf_op jit(solution)/shard_map/pallas_call | solution.py:268
  19.3 0.3 fusion.100
  19.6 0.3 negate_convert_fusion
  19.9 0.2 fusion.63
  20.1 0.1 multiply_convert_fusion.13
  20.2 3.9 %all-to-all-done = bf16[16,7,16,128]{3,2,1,0:T(8,128)(2,1)S(1)} async-done(((bf16[16,7,16,128]{3,2,1,0:T(8,128)(2,1)}), bf16[16,7,16,128]{3,2,1,0:T(8,128)(2,1)S(1)}, u32[]{:S(2)}, u32[]{:S(2)}) %all-to-all-start) | async-done | bytes 458784 | tf_op jit(solution)/shard_map/all_to_all | solution.py:333
  24.0 0.4 fusion.17
  24.4 0.1 fusion.138
  24.5 0.2 copy.48
  24.7 0.2 copy.47
  25.0 0.2 add_convert_fusion.1
  25.1 0.3 fusion.6
  25.7 0.2 fusion.24
  25.9 0.1 subtract_convert_fusion.3
  26.0 0.4 fusion.22
  26.4 0.1 copy.87
  26.5 13.8 %all_to_all.20.refs_2_ = bf16[16,4,16,128]{3,2,1,0:T(8,128)(2,1)} all-to-all(bf16[16,4,16,128]{3,2,1,0:T(8,128)(2,1)S(1)} %copy.87), channel_id=1, replica_groups=mesh['grp'=2,'seq'=16] {'seq'}, dimensions={0} | all-to-all | bytes 524288 | tf_op jit(solution)/shard_map/all_to_all | solution.py:336
  40.3 4.0 %shard_map.160 = (bf16[16,7,16,128]{3,2,1,0:T(8,128)(2,1)}, f32[256,128]{1,0:T(8,128)}, f32[3,256,128]{2,1,0:T(8,128)}) custom-call(bf16[256,128]{1,0:T(8,128)(2,1)} %refs_0_.3, bf16[3,256,128]{2,1,0:T(8,128)(2,1)} %refs_1_.3, bf16[16,4,16,128]{3,2,1,0:T(8,128)(2,1)} %all_to_all.20.refs_2_, bf16[4,256,128]{2,1,0:T(8,128)(2,1)} %shard_map.159.refs_3_, ...), custom_call_target="tpu_custom_call" | custom-call | tf_op jit(solution)/shard_map/pallas_call | solution.py:239
  44.3 3.7 %all-to-all-start.2 = ((bf16[16,7,16,128]{3,2,1,0:T(8,128)(2,1)}), bf16[16,7,16,128]{3,2,1,0:T(8,128)(2,1)S(1)}, u32[]{:S(2)}, u32[]{:S(2)}) async-start(bf16[16,7,16,128]{3,2,1,0:T(8,128)(2,1)} %get-tuple-element.53), calls=%async_computation.2 | async-start | bytes 917504 | tf_op jit(solution)/shard_map/all_to_all | solution.py:333
  48.1 0.1 dynamic-slice_negate_fusion
  48.2 2.3 %convolution_sine_fusion.1 = f32[64,2048]{1,0:T(8,128)S(1)} fusion(f32[64,16]{0,1:T(8,128)S(1)} %get-tuple-element.57, f32[8,2048]{1,0:T(8,128)S(1)} %get-tuple-element.107, f32[8,2048]{1,0:T(8,128)S(1)} %get-tuple-element.106), kind=kOutput, calls=%fused_computation.1 | convolution fusion | flops 25198592 | bytes 659456 | tf_op jit(solution)/shard_map/dot_general | solution.py:20
  50.5 2.4 %convolution_sine_fusion = f32[64,2048]{1,0:T(8,128)S(1)} fusion(f32[64,64]{1,0:T(8,128)S(1)} %get-tuple-element.56, f32[64,2048]{1,0:T(8,128)S(1)} %convolution_sine_fusion.1), kind=kOutput, calls=%fused_computation | convolution fusion | flops 100663296 | bytes 1064960 | tf_op jit(solution)/shard_map/dot_general | solution.py:21
  52.9 0.5 fusion.4
  53.4 0.2 fusion.79
  53.6 2.4 %shard_map.161.refs_3_ = bf16[4,256,128]{2,1,0:T(8,128)(2,1)} custom-call(f32[256,128]{1,0:T(8,128)} %get-tuple-element.51.ss_ref.refs_0_, f32[3,256,128]{2,1,0:T(8,128)} %get-tuple-element.52.sv_ref.refs_1_, bf16[2,768,256]{2,1,0:T(8,128)(2,1)} %ws_ref.3, bf16[2,768,256]{2,1,0:T(8,128)(2,1)} %wv_ref.3, f32[2,4,256]{2,1,0:T(4,128)} %refs_10_.3), custom_call_target="tpu_custom_call" | custom-call | tf_op jit(solution)/shard_map/pallas_call | solution.py:268
  56.1 0.2 fusion.61
  56.3 4.9 %all-to-all-done.2 = bf16[16,7,16,128]{3,2,1,0:T(8,128)(2,1)S(1)} async-done(((bf16[16,7,16,128]{3,2,1,0:T(8,128)(2,1)}), bf16[16,7,16,128]{3,2,1,0:T(8,128)(2,1)S(1)}, u32[]{:S(2)}, u32[]{:S(2)}) %all-to-all-start.2) | async-done | bytes 458784 | tf_op jit(solution)/shard_map/all_to_all | solution.py:333
  61.1 0.4 fusion.14
  61.5 0.1 fusion.137
  61.6 0.2 copy.56
  61.9 0.2 copy.55
  62.1 0.2 add_convert_fusion
  62.2 0.3 fusion.10
  62.8 0.2 fusion.40
  63.0 0.1 subtract_convert_fusion.2
  63.1 0.4 fusion.20
  63.5 0.1 copy.86
  63.6 13.8 %all_to_all.21.refs_2_ = bf16[16,4,16,128]{3,2,1,0:T(8,128)(2,1)} all-to-all(bf16[16,4,16,128]{3,2,1,0:T(8,128)(2,1)S(1)} %copy.86), channel_id=1, replica_groups=mesh['grp'=2,'seq'=16] {'seq'}, dimensions={0} | all-to-all | bytes 524288 | tf_op jit(solution)/shard_map/all_to_all | solution.py:336
  77.3 3.4 %shard_map.162 = (bf16[256,128]{1,0:T(8,128)(2,1)}, bf16[3,256,128]{2,1,0:T(8,128)(2,1)}) custom-call(f32[256,128]{1,0:T(8,128)} %get-tuple-element.51.ss_ref.refs_0_, f32[3,256,128]{2,1,0:T(8,128)} %get-tuple-element.52.sv_ref.refs_1_, bf16[16,4,16,128]{3,2,1,0:T(8,128)(2,1)} %all_to_all.21.refs_2_, bf16[4,256,128]{2,1,0:T(8,128)(2,1)} %shard_map.161.refs_3_, ...), custom_call_target="tpu_custom_call" | custom-call | tf_op jit(solution)/shard_map/pallas_call | solution.py:239
  (41 shorter events, 1.0 us)
Async XLA Ops:
  0.6 10.2 %copy-start.3 = (f32[2,256]{1,0:T(2,128)S(1)}, f32[2,256]{1,0:T(2,128)}, u32[]{:S(2)}) copy-start(f32[2,256]{1,0:T(2,128)} %param.33) | copy-start | bytes 6148
  0.6 10.2 %copy-start.2 = (f32[2,64,16]{1,2,0:T(8,128)S(1)}, f32[2,64,16]{1,2,0:T(8,128)}, u32[]{:S(2)}) copy-start(f32[2,64,16]{1,2,0:T(8,128)} %param.30) | copy-start | bytes 24580
  0.7 10.3 %copy-start.1 = (f32[2,64,64]{2,1,0:T(8,128)S(1)}, f32[2,64,64]{2,1,0:T(8,128)}, u32[]{:S(2)}) copy-start(f32[2,64,64]{2,1,0:T(8,128)} %param.31) | copy-start | bytes 98308
  0.7 10.6 %copy-start = (f32[2,256,64]{1,2,0:T(8,128)S(1)}, f32[2,256,64]{1,2,0:T(8,128)}, u32[]{:S(2)}) copy-start(f32[2,256,64]{1,2,0:T(8,128)} %param.32) | copy-start | bytes 393220
  3.4 20.6 %all-to-all-start = ((bf16[16,7,16,128]{3,2,1,0:T(8,128)(2,1)}), bf16[16,7,16,128]{3,2,1,0:T(8,128)(2,1)S(1)}, u32[]{:S(2)}, u32[]{:S(2)}) async-start(bf16[16,7,16,128]{3,2,1,0:T(8,128)(2,1)} %shard_map.158), calls=%async_computation | async-start | bytes 917504 | tf_op jit(solution)/shard_map/all_to_all | solution.py:333
  16.8 3.2 %copy-start.4 = (f32[9]{0:T(128)S(1)}, f32[9]{0:T(128)}, u32[]{:S(2)}) copy-start(f32[9]{0:T(128)} %constant.125.clone.1) | copy-start | bytes 112
  44.3 16.8 %all-to-all-start.2 = ((bf16[16,7,16,128]{3,2,1,0:T(8,128)(2,1)}), bf16[16,7,16,128]{3,2,1,0:T(8,128)(2,1)S(1)}, u32[]{:S(2)}, u32[]{:S(2)}) async-start(bf16[16,7,16,128]{3,2,1,0:T(8,128)(2,1)} %get-tuple-element.53), calls=%async_computation.2 | async-start | bytes 917504 | tf_op jit(solution)/shard_map/all_to_all | solution.py:333

commit v13 on v12

--- a/solution.py
+++ b/solution.py
@@ -76,10 +76,11 @@
     lead_fwd, _, tw_c, tw_s, lane_fwd, _ = tables
     shards, planes, chans, local = field.shape
     flat = field.reshape(shards, -1).astype(jnp.bfloat16)
-    stage = jnp.dot(lead_fwd, flat, preferred_element_type=jnp.float32)
     half = lead_fwd.shape[0] // 2
-    stage = stage.reshape(2 * half, planes, chans, local)
-    st_r, st_i = stage[:half], stage[half:]
+    st_r = jnp.dot(lead_fwd[:half], flat, preferred_element_type=jnp.float32)
+    st_i = jnp.dot(lead_fwd[half:], flat, preferred_element_type=jnp.float32)
+    st_r = st_r.reshape(half, planes, chans, local)
+    st_i = st_i.reshape(half, planes, chans, local)
     tw_r = st_r * tw_c + st_i * tw_s
     tw_i = st_i * tw_c - st_r * tw_s
     joined = jnp.concatenate([tw_r, tw_i], axis=-1).reshape(-1, 2 * local).astype(jnp.bfloat16)
@@ -98,8 +99,10 @@
     bk_r, bk_i = back[..., :local], back[..., local:]
     un_r = bk_r * tw_c - bk_i * tw_s
     un_i = bk_r * tw_s + bk_i * tw_c
-    stacked = jnp.concatenate([un_r, un_i], axis=0).reshape(2 * half, -1).astype(jnp.bfloat16)
-    whole = jnp.dot(lead_inv, stacked, preferred_element_type=jnp.float32)
+    un_r = un_r.reshape(half, -1).astype(jnp.bfloat16)
+    un_i = un_i.reshape(half, -1).astype(jnp.bfloat16)
+    whole = jnp.dot(lead_inv[:, :half], un_r, preferred_element_type=jnp.float32)
+    whole = whole + jnp.dot(lead_inv[:, half:], un_i, preferred_element_type=jnp.float32)
     return whole.reshape(shards, planes, chans, local)
 
 

time: 81.2 us -> 82.7 us (1.018)
  matrix products: 13.5 us -> 15.1 us
    dot_general x6 -> x12, matrix products: 1.74 us -> 3.38 us  [the longest x4 1.35 us: forward_dft(): st_i = jnp.dot(lead_fwd[half:], flat, preferred_element_type=jnp.float32)]
where the time goes in v13:
time: 82.7 us; the launch traced here: 82.1 us
  blocking collectives  27.6 us (33%)
  matrix products  15.1 us (18%)
  Pallas kernels  14.9 us (18%)
  starting transfers between devices  11.3 us (14%)
  waiting for transfers between devices  8.55 us (10%)
  other arithmetic  2.04 us (2%)
  local copies, waits for them, and re-layouts  1.55 us (2%)
  between operations  1.11 us (1%)
    all_to_all x2, blocking collectives, per_device(): returned = lax.all_to_all(convolved, 'seq', 0, 0, tiled=True)  27.6 us
    all_to_all x2, starting transfers between devices, per_device(): regrouped = lax.all_to_all(outgoing, 'seq', 0, 0, tiled=True)  11.3 us
    pallas_call x3, Pallas kernels, token_step(): pl.pallas_call(kernel, grid=(1,), in_specs=specs, out_specs=[full(shape)...  10 us
    all_to_all x2, waiting for transfers between devices, per_device(): regrouped = lax.all_to_all(outgoing, 'seq', 0, 0, tiled=True)  8.55 us
    dot_general x2, matrix products, filter_values(): hid_two = jnp.sin(jnp.dot(second, hid_one, precision=HIGH))  4.87 us
    pallas_call x2, Pallas kernels, query_step(): pl.pallas_call(kernel, grid=(1,), in_specs=[full(state_s.shape), full(sta...  4.84 us
    dot_general x2, matrix products, filter_values(): hid_one = jnp.sin(jnp.dot(first, feats, precision=HIGH))  4.53 us
  transfers between devices with their start and end apart: 2, of which 2 were waited for; matrix products, arithmetic and copies ran while one was open for 15% of the time, Pallas kernels for 6%

profile of v13, /device:TPU:0, one launch (start us, length us, event | category | flops | bytes accessed | tf_op | source)
XLA Modules:
  0.0 82.1 jit_solution(9031168277216593709)
XLA Ops:
  0.6 2.7 %shard_map.158 = bf16[16,7,16,128]{3,2,1,0:T(8,128)(2,1)} custom-call(bf16[256,128]{1,0:T(8,128)(2,1)} %refs_0_.3, bf16[3,256,128]{2,1,0:T(8,128)(2,1)} %refs_1_.3, bf16[2,768,256]{2,1,0:T(8,128)(2,1)} %ws_ref.3, bf16[2,768,256]{2,1,0:T(8,128)(2,1)} %ws_ref.3, bf16[2,768,256]{2,1,0:T(8,128)(2,1)} %wv_ref.3, bf16[2,768,256]{2,1,0:T(8,128)(2,1)} %wv_ref.3, ...), custom_call_target="tpu_custom_call" | custom-call | tf_op jit(solution)/shard_map/pallas_call | solution.py:242
  3.3 7.5 %all-to-all-start = ((bf16[16,7,16,128]{3,2,1,0:T(8,128)(2,1)}), bf16[16,7,16,128]{3,2,1,0:T(8,128)(2,1)S(1)}, u32[]{:S(2)}, u32[]{:S(2)}) async-start(bf16[16,7,16,128]{3,2,1,0:T(8,128)(2,1)} %shard_map.158), calls=%async_computation | async-start | bytes 917504 | tf_op jit(solution)/shard_map/all_to_all | solution.py:336
  10.9 0.3 fusion.100
  11.1 0.3 negate_convert_fusion
  11.5 0.3 fusion.97
  11.9 2.3 %convolution_sine_fusion.3 = f32[64,2048]{1,0:T(8,128)S(1)} fusion(f32[64,16]{0,1:T(8,128)S(1)} %get-tuple-element.48, f32[8,2048]{1,0:T(8,128)S(1)} %get-tuple-element.97, f32[8,2048]{1,0:T(8,128)S(1)} %get-tuple-element.96), kind=kOutput, calls=%fused_computation.7 | convolution fusion | flops 25198592 | bytes 659456 | tf_op jit(solution)/shard_map/dot_general | solution.py:20
  14.2 2.4 %convolution_sine_fusion.2 = f32[64,2048]{1,0:T(8,128)S(1)} fusion(f32[64,64]{1,0:T(8,128)S(1)} %get-tuple-element.47, f32[64,2048]{1,0:T(8,128)S(1)} %convolution_sine_fusion.3), kind=kOutput, calls=%fused_computation.6 | convolution fusion | flops 100663296 | bytes 1064960 | tf_op jit(solution)/shard_map/dot_general | solution.py:21
  16.7 0.5 fusion.9
  17.2 2.4 %shard_map.159.refs_3_ = bf16[4,256,128]{2,1,0:T(8,128)(2,1)} custom-call(bf16[256,128]{1,0:T(8,128)(2,1)} %refs_0_.3, bf16[3,256,128]{2,1,0:T(8,128)(2,1)} %refs_1_.3, bf16[2,768,256]{2,1,0:T(8,128)(2,1)} %ws_ref.3, bf16[2,768,256]{2,1,0:T(8,128)(2,1)} %wv_ref.3, f32[2,4,256]{2,1,0:T(4,128)} %refs_10_.3), custom_call_target="tpu_custom_call" | custom-call | tf_op jit(solution)/shard_map/pallas_call | solution.py:271
  19.6 0.2 fusion.79
  19.8 0.2 add_convert_fusion.5
  20.1 0.2 fusion.61
  20.2 3.9 %all-to-all-done = bf16[16,7,16,128]{3,2,1,0:T(8,128)(2,1)S(1)} async-done(((bf16[16,7,16,128]{3,2,1,0:T(8,128)(2,1)}), bf16[16,7,16,128]{3,2,1,0:T(8,128)(2,1)S(1)}, u32[]{:S(2)}, u32[]{:S(2)}) %all-to-all-start) | async-done | bytes 458784 | tf_op jit(solution)/shard_map/all_to_all | solution.py:336
  24.1 0.1 copy.126
  24.3 0.3 fusion.20
  24.6 0.5 add_convert_fusion.1
  25.1 0.1 pad_maximum_fusion
  25.2 0.3 fusion.12
  25.8 0.2 fusion.22
  26.0 0.1 add_convert_fusion.3
  26.2 0.2 copy.62
  26.4 0.2 copy.63
  26.6 0.2 copy-done.3
  26.8 0.2 fusion.130
  27.0 0.3 fusion.7
  27.3 13.8 %all_to_all.20.refs_2_ = bf16[16,4,16,128]{3,2,1,0:T(8,128)(2,1)} all-to-all(bf16[16,4,16,128]{3,2,1,0:T(8,128)(2,1)S(1)} %bitcast.250), channel_id=1, replica_groups=mesh['grp'=2,'seq'=16] {'seq'}, dimensions={0} | all-to-all | bytes 524288 | tf_op jit(solution)/shard_map/all_to_all | solution.py:339
  41.2 4.0 %shard_map.160 = (bf16[16,7,16,128]{3,2,1,0:T(8,128)(2,1)}, f32[256,128]{1,0:T(8,128)}, f32[3,256,128]{2,1,0:T(8,128)}) custom-call(bf16[256,128]{1,0:T(8,128)(2,1)} %refs_0_.3, bf16[3,256,128]{2,1,0:T(8,128)(2,1)} %refs_1_.3, bf16[16,4,16,128]{3,2,1,0:T(8,128)(2,1)} %all_to_all.20.refs_2_, bf16[4,256,128]{2,1,0:T(8,128)(2,1)} %shard_map.159.refs_3_, ...), custom_call_target="tpu_custom_call" | custom-call | tf_op jit(solution)/shard_map/pallas_call | solution.py:242
  45.2 3.7 %all-to-all-start.2 = ((bf16[16,7,16,128]{3,2,1,0:T(8,128)(2,1)}), bf16[16,7,16,128]{3,2,1,0:T(8,128)(2,1)S(1)}, u32[]{:S(2)}, u32[]{:S(2)}) async-start(bf16[16,7,16,128]{3,2,1,0:T(8,128)(2,1)} %get-tuple-element.53), calls=%async_computation.2 | async-start | bytes 917504 | tf_op jit(solution)/shard_map/all_to_all | solution.py:336
  49.1 2.3 %convolution_sine_fusion.1 = f32[64,2048]{1,0:T(8,128)S(1)} fusion(f32[64,16]{0,1:T(8,128)S(1)} %get-tuple-element.57, f32[8,2048]{1,0:T(8,128)S(1)} %get-tuple-element.97, f32[8,2048]{1,0:T(8,128)S(1)} %get-tuple-element.96), kind=kOutput, calls=%fused_computation.5 | convolution fusion | flops 25198592 | bytes 659456 | tf_op jit(solution)/shard_map/dot_general | solution.py:20
  51.3 2.4 %convolution_sine_fusion = f32[64,2048]{1,0:T(8,128)S(1)} fusion(f32[64,64]{1,0:T(8,128)S(1)} %get-tuple-element.56, f32[64,2048]{1,0:T(8,128)S(1)} %convolution_sine_fusion.1), kind=kOutput, calls=%fused_computation.4 | convolution fusion | flops 100663296 | bytes 1064960 | tf_op jit(solution)/shard_map/dot_general | solution.py:21
  53.8 0.5 fusion.8
  54.3 2.4 %shard_map.161.refs_3_ = bf16[4,256,128]{2,1,0:T(8,128)(2,1)} custom-call(f32[256,128]{1,0:T(8,128)} %get-tuple-element.51.ss_ref.refs_0_, f32[3,256,128]{2,1,0:T(8,128)} %get-tuple-element.52.sv_ref.refs_1_, bf16[2,768,256]{2,1,0:T(8,128)(2,1)} %ws_ref.3, bf16[2,768,256]{2,1,0:T(8,128)(2,1)} %wv_ref.3, f32[2,4,256]{2,1,0:T(4,128)} %refs_10_.3), custom_call_target="tpu_custom_call" | custom-call | tf_op jit(solution)/shard_map/pallas_call | solution.py:271
  56.7 0.2 fusion.75
  56.9 0.2 add_convert_fusion.4
  57.1 0.2 fusion.59
  57.3 4.7 %all-to-all-done.2 = bf16[16,7,16,128]{3,2,1,0:T(8,128)(2,1)S(1)} async-done(((bf16[16,7,16,128]{3,2,1,0:T(8,128)(2,1)}), bf16[16,7,16,128]{3,2,1,0:T(8,128)(2,1)S(1)}, u32[]{:S(2)}, u32[]{:S(2)}) %all-to-all-start.2) | async-done | bytes 458784 | tf_op jit(solution)/shard_map/all_to_all | solution.py:336
  62.0 0.1 copy.125
  62.2 0.3 fusion.16
  62.5 0.5 add_convert_fusion
  63.0 0.1 pad_maximum_fusion.1
  63.1 0.3 fusion.10
  63.7 0.2 fusion.38
  64.1 0.2 copy.68
  64.3 0.2 copy.69
  64.5 0.2 fusion.129
  64.7 0.3 fusion.6
  65.0 13.8 %all_to_all.21.refs_2_ = bf16[16,4,16,128]{3,2,1,0:T(8,128)(2,1)} all-to-all(bf16[16,4,16,128]{3,2,1,0:T(8,128)(2,1)S(1)} %bitcast.251), channel_id=1, replica_groups=mesh['grp'=2,'seq'=16] {'seq'}, dimensions={0} | all-to-all | bytes 524288 | tf_op jit(solution)/shard_map/all_to_all | solution.py:339
  78.8 3.4 %shard_map.162 = (bf16[256,128]{1,0:T(8,128)(2,1)}, bf16[3,256,128]{2,1,0:T(8,128)(2,1)}) custom-call(f32[256,128]{1,0:T(8,128)} %get-tuple-element.51.ss_ref.refs_0_, f32[3,256,128]{2,1,0:T(8,128)} %get-tuple-element.52.sv_ref.refs_1_, bf16[16,4,16,128]{3,2,1,0:T(8,128)(2,1)} %all_to_all.21.refs_2_, bf16[4,256,128]{2,1,0:T(8,128)(2,1)} %shard_map.161.refs_3_, ...), custom_call_target="tpu_custom_call" | custom-call | tf_op jit(solution)/shard_map/pallas_call | solution.py:242
  (39 shorter events, 1.2 us)
Async XLA Ops:
  0.6 10.8 %copy-start.4 = (f32[2,256]{1,0:T(2,128)S(1)}, f32[2,256]{1,0:T(2,128)}, u32[]{:S(2)}) copy-start(f32[2,256]{1,0:T(2,128)} %param.33) | copy-start | bytes 6148
  3.3 8.1 %copy-start.2 = (f32[2,64,16]{1,2,0:T(8,128)S(1)}, f32[2,64,16]{1,2,0:T(8,128)}, u32[]{:S(2)}) copy-start(f32[2,64,16]{1,2,0:T(8,128)} %param.30) | copy-start | bytes 24580
  3.3 8.2 %copy-start.1 = (f32[2,64,64]{2,1,0:T(8,128)S(1)}, f32[2,64,64]{2,1,0:T(8,128)}, u32[]{:S(2)}) copy-start(f32[2,64,64]{2,1,0:T(8,128)} %param.31) | copy-start | bytes 98308
  3.3 8.5 %copy-start = (f32[2,256,64]{1,2,0:T(8,128)S(1)}, f32[2,256,64]{1,2,0:T(8,128)}, u32[]{:S(2)}) copy-start(f32[2,256,64]{1,2,0:T(8,128)} %param.32) | copy-start | bytes 393220
  3.3 20.8 %all-to-all-start = ((bf16[16,7,16,128]{3,2,1,0:T(8,128)(2,1)}), bf16[16,7,16,128]{3,2,1,0:T(8,128)(2,1)S(1)}, u32[]{:S(2)}, u32[]{:S(2)}) async-start(bf16[16,7,16,128]{3,2,1,0:T(8,128)(2,1)} %shard_map.158), calls=%async_computation | async-start | bytes 917504 | tf_op jit(solution)/shard_map/all_to_all | solution.py:336
  26.1 0.7 copy-start.3
  45.2 16.8 %all-to-all-start.2 = ((bf16[16,7,16,128]{3,2,1,0:T(8,128)(2,1)}), bf16[16,7,16,128]{3,2,1,0:T(8,128)(2,1)S(1)}, u32[]{:S(2)}, u32[]{:S(2)}) async-start(bf16[16,7,16,128]{3,2,1,0:T(8,128)(2,1)} %get-tuple-element.53), calls=%async_computation.2 | async-start | bytes 917504 | tf_op jit(solution)/shard_map/all_to_all | solution.py:336

commit v14 on v12

--- a/solution.py
+++ b/solution.py
@@ -201,11 +201,16 @@
             out_s = (qs * ys + mix).astype(bf16)
             ss = ss + mm(wos[...], out_s)
             sv = [sv[j] + mm(wov[...], (qs * yv[j]).astype(bf16)) for j in range(3)]
-            mlp_s = snorm(ss, g[:, 2:3]).astype(bf16)
+            mlp_f = snorm(ss, g[:, 2:3])
+            mlp_s = mlp_f.astype(bf16)
             mlp_v = [v.astype(bf16) for v in vnorm(sv, g[:, 3:4])]
-            hidden = gelu_tanh(mm(wup[...], mlp_s)).astype(bf16)
+            nt = (((1,), (1,)), ((), ()))
+            mlp_t = mlp_f.T.astype(bf16)
+            hidden_t = lax.dot_general(mlp_t, wup[...], nt, preferred_element_type=f32)
+            hidden_t = gelu_tanh(hidden_t).astype(bf16)
             gate = 1.0 / (1.0 + jnp.exp(-mm(wgt[...], mlp_s)))
-            ss = ss + mm(wdn[...], hidden)
+            down_t = lax.dot_general(hidden_t, wdn[...], nt, preferred_element_type=f32)
+            ss = ss + down_t.T
             sv = [sv[j] + mm(wmx[...], mlp_v[j]) * gate for j in range(3)]
         if pre is not None:
             wqs_k, wqs_w, wqv_k, wqv_w, gq = [refs.pop(0) for _ in range(5)]

time: 81.2 us -> 81.2 us (level)
  no operation moved by 1% of the time
where the time goes in v14:
time: 81.2 us; the launch traced here: 80.6 us
  blocking collectives  27.6 us (34%)
  Pallas kernels  14.9 us (18%)
  matrix products  13.4 us (17%)
  starting transfers between devices  11.1 us (14%)
  waiting for transfers between devices  8.72 us (11%)
  other arithmetic  2.24 us (3%)
  local copies, waits for them, and re-layouts  1.48 us (2%)
  between operations  1.13 us (1%)
    all_to_all x2, blocking collectives, per_device(): returned = lax.all_to_all(convolved, 'seq', 0, 0, tiled=True)  27.6 us
    all_to_all x2, starting transfers between devices, per_device(): regrouped = lax.all_to_all(outgoing, 'seq', 0, 0, tiled=True)  11.1 us
    pallas_call x3, Pallas kernels, token_step(): pl.pallas_call(kernel, grid=(1,), in_specs=specs, out_specs=[full(shape)...  10 us
    all_to_all x2, waiting for transfers between devices, per_device(): regrouped = lax.all_to_all(outgoing, 'seq', 0, 0, tiled=True)  8.72 us
    dot_general x2, matrix products, filter_values(): hid_two = jnp.sin(jnp.dot(second, hid_one, precision=HIGH))  4.86 us
    pallas_call x2, Pallas kernels, query_step(): pl.pallas_call(kernel, grid=(1,), in_specs=[full(state_s.shape), full(sta...  4.83 us
    dot_general x2, matrix products, filter_values(): hid_one = jnp.sin(jnp.dot(first, feats, precision=HIGH))  4.53 us
  transfers between devices with their start and end apart: 2, of which 2 were waited for; matrix products, arithmetic and copies ran while one was open for 15% of the time, Pallas kernels for 6%

profile of v14, /device:TPU:0, one launch (start us, length us, event | category | flops | bytes accessed | tf_op | source)
XLA Modules:
  0.0 80.6 jit_solution(6845216124558285705)
XLA Ops:
  0.7 2.7 %shard_map.158 = bf16[16,7,16,128]{3,2,1,0:T(8,128)(2,1)} custom-call(bf16[256,128]{1,0:T(8,128)(2,1)} %refs_0_.3, bf16[3,256,128]{2,1,0:T(8,128)(2,1)} %refs_1_.3, bf16[2,768,256]{2,1,0:T(8,128)(2,1)} %ws_ref.3, bf16[2,768,256]{2,1,0:T(8,128)(2,1)} %ws_ref.3, bf16[2,768,256]{2,1,0:T(8,128)(2,1)} %wv_ref.3, bf16[2,768,256]{2,1,0:T(8,128)(2,1)} %wv_ref.3, ...), custom_call_target="tpu_custom_call" | custom-call | tf_op jit(solution)/shard_map/pallas_call | solution.py:244
  3.4 7.4 %all-to-all-start = ((bf16[16,7,16,128]{3,2,1,0:T(8,128)(2,1)}), bf16[16,7,16,128]{3,2,1,0:T(8,128)(2,1)S(1)}, u32[]{:S(2)}, u32[]{:S(2)}) async-start(bf16[16,7,16,128]{3,2,1,0:T(8,128)(2,1)} %shard_map.158), calls=%async_computation | async-start | bytes 917504 | tf_op jit(solution)/shard_map/all_to_all | solution.py:338
  10.8 0.1 negate_convert_fusion.1
  10.9 0.3 fusion.97
  11.3 0.1 dynamic-slice_negate_fusion.1
  11.4 2.3 %convolution_sine_fusion.3 = f32[64,2048]{1,0:T(8,128)S(1)} fusion(f32[64,16]{0,1:T(8,128)S(1)} %get-tuple-element.48, f32[8,2048]{1,0:T(8,128)S(1)} %get-tuple-element.107, f32[8,2048]{1,0:T(8,128)S(1)} %get-tuple-element.106), kind=kOutput, calls=%fused_computation.3 | convolution fusion | flops 25198592 | bytes 659456 | tf_op jit(solution)/shard_map/dot_general | solution.py:20
  13.7 2.4 %convolution_sine_fusion.2 = f32[64,2048]{1,0:T(8,128)S(1)} fusion(f32[64,64]{1,0:T(8,128)S(1)} %get-tuple-element.47, f32[64,2048]{1,0:T(8,128)S(1)} %convolution_sine_fusion.3), kind=kOutput, calls=%fused_computation.2 | convolution fusion | flops 100663296 | bytes 1064960 | tf_op jit(solution)/shard_map/dot_general | solution.py:21
  16.1 0.5 fusion.5
  16.6 0.2 fusion.82
  16.9 2.4 %shard_map.159.refs_3_ = bf16[4,256,128]{2,1,0:T(8,128)(2,1)} custom-call(bf16[256,128]{1,0:T(8,128)(2,1)} %refs_0_.3, bf16[3,256,128]{2,1,0:T(8,128)(2,1)} %refs_1_.3, bf16[2,768,256]{2,1,0:T(8,128)(2,1)} %ws_ref.3, bf16[2,768,256]{2,1,0:T(8,128)(2,1)} %wv_ref.3, f32[2,4,256]{2,1,0:T(4,128)} %refs_10_.3), custom_call_target="tpu_custom_call" | custom-call | tf_op jit(solution)/shard_map/pallas_call | solution.py:273
  19.3 0.3 fusion.100
  19.6 0.3 negate_convert_fusion
  19.9 0.2 fusion.63
  20.1 0.1 multiply_convert_fusion.13
  20.2 3.9 %all-to-all-done = bf16[16,7,16,128]{3,2,1,0:T(8,128)(2,1)S(1)} async-done(((bf16[16,7,16,128]{3,2,1,0:T(8,128)(2,1)}), bf16[16,7,16,128]{3,2,1,0:T(8,128)(2,1)S(1)}, u32[]{:S(2)}, u32[]{:S(2)}) %all-to-all-start) | async-done | bytes 458784 | tf_op jit(solution)/shard_map/all_to_all | solution.py:338
  24.0 0.4 fusion.17
  24.4 0.1 fusion.138
  24.5 0.2 copy.48
  24.7 0.2 copy.47
  25.0 0.2 add_convert_fusion.1
  25.1 0.3 fusion.6
  25.7 0.2 fusion.24
  25.9 0.1 subtract_convert_fusion.3
  26.0 0.4 fusion.22
  26.4 0.1 copy.87
  26.5 13.8 %all_to_all.20.refs_2_ = bf16[16,4,16,128]{3,2,1,0:T(8,128)(2,1)} all-to-all(bf16[16,4,16,128]{3,2,1,0:T(8,128)(2,1)S(1)} %copy.87), channel_id=1, replica_groups=mesh['grp'=2,'seq'=16] {'seq'}, dimensions={0} | all-to-all | bytes 524288 | tf_op jit(solution)/shard_map/all_to_all | solution.py:341
  40.3 4.0 %shard_map.160 = (bf16[16,7,16,128]{3,2,1,0:T(8,128)(2,1)}, f32[256,128]{1,0:T(8,128)}, f32[3,256,128]{2,1,0:T(8,128)}) custom-call(bf16[256,128]{1,0:T(8,128)(2,1)} %refs_0_.3, bf16[3,256,128]{2,1,0:T(8,128)(2,1)} %refs_1_.3, bf16[16,4,16,128]{3,2,1,0:T(8,128)(2,1)} %all_to_all.20.refs_2_, bf16[4,256,128]{2,1,0:T(8,128)(2,1)} %shard_map.159.refs_3_, ...), custom_call_target="tpu_custom_call" | custom-call | tf_op jit(solution)/shard_map/pallas_call | solution.py:244
  44.3 3.7 %all-to-all-start.2 = ((bf16[16,7,16,128]{3,2,1,0:T(8,128)(2,1)}), bf16[16,7,16,128]{3,2,1,0:T(8,128)(2,1)S(1)}, u32[]{:S(2)}, u32[]{:S(2)}) async-start(bf16[16,7,16,128]{3,2,1,0:T(8,128)(2,1)} %get-tuple-element.53), calls=%async_computation.2 | async-start | bytes 917504 | tf_op jit(solution)/shard_map/all_to_all | solution.py:338
  48.1 0.1 dynamic-slice_negate_fusion
  48.2 2.3 %convolution_sine_fusion.1 = f32[64,2048]{1,0:T(8,128)S(1)} fusion(f32[64,16]{0,1:T(8,128)S(1)} %get-tuple-element.57, f32[8,2048]{1,0:T(8,128)S(1)} %get-tuple-element.107, f32[8,2048]{1,0:T(8,128)S(1)} %get-tuple-element.106), kind=kOutput, calls=%fused_computation.1 | convolution fusion | flops 25198592 | bytes 659456 | tf_op jit(solution)/shard_map/dot_general | solution.py:20
  50.5 2.4 %convolution_sine_fusion = f32[64,2048]{1,0:T(8,128)S(1)} fusion(f32[64,64]{1,0:T(8,128)S(1)} %get-tuple-element.56, f32[64,2048]{1,0:T(8,128)S(1)} %convolution_sine_fusion.1), kind=kOutput, calls=%fused_computation | convolution fusion | flops 100663296 | bytes 1064960 | tf_op jit(solution)/shard_map/dot_general | solution.py:21
  52.9 0.5 fusion.4
  53.4 0.2 fusion.79
  53.6 2.4 %shard_map.161.refs_3_ = bf16[4,256,128]{2,1,0:T(8,128)(2,1)} custom-call(f32[256,128]{1,0:T(8,128)} %get-tuple-element.51.ss_ref.refs_0_, f32[3,256,128]{2,1,0:T(8,128)} %get-tuple-element.52.sv_ref.refs_1_, bf16[2,768,256]{2,1,0:T(8,128)(2,1)} %ws_ref.3, bf16[2,768,256]{2,1,0:T(8,128)(2,1)} %wv_ref.3, f32[2,4,256]{2,1,0:T(4,128)} %refs_10_.3), custom_call_target="tpu_custom_call" | custom-call | tf_op jit(solution)/shard_map/pallas_call | solution.py:273
  56.1 0.2 fusion.61
  56.3 4.9 %all-to-all-done.2 = bf16[16,7,16,128]{3,2,1,0:T(8,128)(2,1)S(1)} async-done(((bf16[16,7,16,128]{3,2,1,0:T(8,128)(2,1)}), bf16[16,7,16,128]{3,2,1,0:T(8,128)(2,1)S(1)}, u32[]{:S(2)}, u32[]{:S(2)}) %all-to-all-start.2) | async-done | bytes 458784 | tf_op jit(solution)/shard_map/all_to_all | solution.py:338
  61.1 0.4 fusion.14
  61.5 0.1 fusion.137
  61.6 0.2 copy.56
  61.9 0.2 copy.55
  62.1 0.2 add_convert_fusion
  62.2 0.3 fusion.10
  62.8 0.2 fusion.40
  63.0 0.1 subtract_convert_fusion.2
  63.1 0.4 fusion.20
  63.5 0.1 copy.86
  63.6 13.8 %all_to_all.21.refs_2_ = bf16[16,4,16,128]{3,2,1,0:T(8,128)(2,1)} all-to-all(bf16[16,4,16,128]{3,2,1,0:T(8,128)(2,1)S(1)} %copy.86), channel_id=1, replica_groups=mesh['grp'=2,'seq'=16] {'seq'}, dimensions={0} | all-to-all | bytes 524288 | tf_op jit(solution)/shard_map/all_to_all | solution.py:341
  77.3 3.3 %shard_map.162 = (bf16[256,128]{1,0:T(8,128)(2,1)}, bf16[3,256,128]{2,1,0:T(8,128)(2,1)}) custom-call(f32[256,128]{1,0:T(8,128)} %get-tuple-element.51.ss_ref.refs_0_, f32[3,256,128]{2,1,0:T(8,128)} %get-tuple-element.52.sv_ref.refs_1_, bf16[16,4,16,128]{3,2,1,0:T(8,128)(2,1)} %all_to_all.21.refs_2_, bf16[4,256,128]{2,1,0:T(8,128)(2,1)} %shard_map.161.refs_3_, ...), custom_call_target="tpu_custom_call" | custom-call | tf_op jit(solution)/shard_map/pallas_call | solution.py:244
  (41 shorter events, 1.0 us)
Async XLA Ops:
  0.6 10.2 %copy-start.3 = (f32[2,256]{1,0:T(2,128)S(1)}, f32[2,256]{1,0:T(2,128)}, u32[]{:S(2)}) copy-start(f32[2,256]{1,0:T(2,128)} %param.33) | copy-start | bytes 6148
  0.6 10.2 %copy-start.2 = (f32[2,64,16]{1,2,0:T(8,128)S(1)}, f32[2,64,16]{1,2,0:T(8,128)}, u32[]{:S(2)}) copy-start(f32[2,64,16]{1,2,0:T(8,128)} %param.30) | copy-start | bytes 24580
  0.7 10.3 %copy-start.1 = (f32[2,64,64]{2,1,0:T(8,128)S(1)}, f32[2,64,64]{2,1,0:T(8,128)}, u32[]{:S(2)}) copy-start(f32[2,64,64]{2,1,0:T(8,128)} %param.31) | copy-start | bytes 98308
  0.7 10.6 %copy-start = (f32[2,256,64]{1,2,0:T(8,128)S(1)}, f32[2,256,64]{1,2,0:T(8,128)}, u32[]{:S(2)}) copy-start(f32[2,256,64]{1,2,0:T(8,128)} %param.32) | copy-start | bytes 393220
  3.4 20.6 %all-to-all-start = ((bf16[16,7,16,128]{3,2,1,0:T(8,128)(2,1)}), bf16[16,7,16,128]{3,2,1,0:T(8,128)(2,1)S(1)}, u32[]{:S(2)}, u32[]{:S(2)}) async-start(bf16[16,7,16,128]{3,2,1,0:T(8,128)(2,1)} %shard_map.158), calls=%async_computation | async-start | bytes 917504 | tf_op jit(solution)/shard_map/all_to_all | solution.py:338
  16.8 3.2 %copy-start.4 = (f32[9]{0:T(128)S(1)}, f32[9]{0:T(128)}, u32[]{:S(2)}) copy-start(f32[9]{0:T(128)} %constant.125.clone.1) | copy-start | bytes 112
  44.3 16.8 %all-to-all-start.2 = ((bf16[16,7,16,128]{3,2,1,0:T(8,128)(2,1)}), bf16[16,7,16,128]{3,2,1,0:T(8,128)(2,1)S(1)}, u32[]{:S(2)}, u32[]{:S(2)}) async-start(bf16[16,7,16,128]{3,2,1,0:T(8,128)(2,1)} %get-tuple-element.53), calls=%async_computation.2 | async-start | bytes 917504 | tf_op jit(solution)/shard_map/all_to_all | solution.py:338

commit v15 on v12

--- a/solution.py
+++ b/solution.py
@@ -5,6 +5,7 @@
 import numpy as np
 from jax import lax
 from jax.experimental import pallas as pl
+from jax.experimental.pallas import tpu as pltpu
 from jax.sharding import PartitionSpec as P
 
 HIGH = lax.Precision.HIGHEST
@@ -144,21 +145,22 @@
     def row_spec(w, layer, rows, block):
         return pl.BlockSpec((pl.Squeezed(), rows, w.shape[2]), lambda i: (layer, block, 0))
 
+    resident = pl.BlockSpec(memory_space=pltpu.MemorySpace.VMEM)
     ins, specs = [state_s, state_v], [full(state_s.shape), full(state_v.shape)]
     post_names = ("w_out_s", "w_out_v", "w_up", "w_down", "w_mix", "w_gate")
     if post is not None:
         ins += [arrays["conv"], arrays["query"]]
         specs += [full(arrays["conv"].shape), full(arrays["query"].shape)]
         for name in post_names + ("gains_t",):
-            ins.append(weights[name])
-            specs.append(layer_spec(weights[name], post))
+            ins.append(weights[name][post])
+            specs.append(resident)
     if pre is not None:
         for name in ("w_qkw_s", "w_qkw_v"):
             for block in (1, 2):
-                ins.append(weights[name])
-                specs.append(row_spec(weights[name], pre, chans, block))
-        ins.append(weights["gains_t"])
-        specs.append(layer_spec(weights["gains_t"], pre))
+                ins.append(weights[name][pre, block * chans : (block + 1) * chans])
+                specs.append(resident)
+        ins.append(weights["gains_t"][pre])
+        specs.append(resident)
     outs = []
     if pre is not None:
         plane_shape = (shards, 7, own, tok) if packed else (7, chans, tok)

time: 81.2 us -> 86.7 us (1.068)
  blocking collectives: 27.6 us -> 13.8 us
  local copies, waits for them, and re-layouts: 1.48 us -> 10.2 us
  waiting for transfers between devices: 8.73 us -> 14.8 us
  starting transfers between devices: 11.1 us -> 15.3 us
    all_to_all x2 -> x1, blocking collectives: 27.6 us -> 13.8 us  [per_device(): returned = lax.all_to_all(convolved, 'seq', 0, 0, tiled=True)]
    all_to_all x0 -> x1, waiting for transfers between devices: none -> 8.15 us  [per_device(): returned = lax.all_to_all(convolved, 'seq', 0, 0, tiled=True)]
    squeeze x0 -> x6, local copies, waits for them, and re-layouts: none -> 7.3 us  [the longest x4 3.75 us: token_step(): ins.append(weights[name][post])]
    all_to_all x0 -> x1, starting transfers between devices: none -> 4.15 us  [per_device(): returned = lax.all_to_all(convolved, 'seq', 0, 0, tiled=True)]
    all_to_all x2, waiting for transfers between devices: 8.73 us -> 6.7 us  [per_device(): regrouped = lax.all_to_all(outgoing, 'seq', 0, 0, tiled=True)]
  transfers between devices with their start and end apart: 2 -> 3, of which waited for: 2 -> 3; matrix products, arithmetic and copies ran while one was open for 15% -> 19% of each run, Pallas kernels for 6% -> 6%
where the time goes in v15:
time: 86.7 us; the launch traced here: 86.1 us
  starting transfers between devices  15.3 us (18%)
  Pallas kernels  15.1 us (17%)
  waiting for transfers between devices  14.8 us (17%)
  blocking collectives  13.8 us (16%)
  matrix products  13.5 us (16%)
  local copies, waits for them, and re-layouts  10.2 us (12%)
  other arithmetic  2.24 us (3%)
  between operations  1.2 us (1%)
    all_to_all x1, blocking collectives, per_device(): returned = lax.all_to_all(convolved, 'seq', 0, 0, tiled=True)  13.8 us
    all_to_all x2, starting transfers between devices, per_device(): regrouped = lax.all_to_all(outgoing, 'seq', 0, 0, tiled=True)  11.1 us
    pallas_call x3, Pallas kernels, token_step(): pl.pallas_call(kernel, grid=(1,), in_specs=specs, out_specs=[full(shape)...  10.2 us
    all_to_all x1, waiting for transfers between devices, per_device(): returned = lax.all_to_all(convolved, 'seq', 0, 0, tiled=True)  8.15 us
    all_to_all x2, waiting for transfers between devices, per_device(): regrouped = lax.all_to_all(outgoing, 'seq', 0, 0, tiled=True)  6.7 us
    pallas_call x2, Pallas kernels, query_step(): pl.pallas_call(kernel, grid=(1,), in_specs=[full(state_s.shape), full(sta...  4.91 us
    dot_general x2, matrix products, filter_values(): hid_two = jnp.sin(jnp.dot(second, hid_one, precision=HIGH))  4.86 us
    dot_general x2, matrix products, filter_values(): hid_one = jnp.sin(jnp.dot(first, feats, precision=HIGH))  4.53 us
  transfers between devices with their start and end apart: 3, of which 3 were waited for; matrix products, arithmetic and copies ran while one was open for 19% of the time, Pallas kernels for 6%

profile of v15, /device:TPU:0, one launch (start us, length us, event | category | flops | bytes accessed | tf_op | source)
XLA Modules:
  0.0 86.1 jit_solution(2161068939777292878)
XLA Ops:
  0.6 1.3 %slice_bitcast_fusion.30 = (f32[4,256]{1,0:T(4,128)}, f32[4,256]{1,0:T(4,128)}) fusion(f32[2,4,256]{2,1,0:T(4,128)} %g_ref.3), kind=kLoop, calls=%fused_computation.216 | loop fusion | bytes 16384 | tf_op jit(solution)/shard_map/squeeze | solution.py:162
  1.9 2.2 %slice_bitcast_fusion.8 = (bf16[256,256]{1,0:T(8,128)(2,1)}, bf16[256,256]{1,0:T(8,128)(2,1)}, bf16[256,256]{1,0:T(8,128)(2,1)}, bf16[256,256]{1,0:T(8,128)(2,1)...) fusion(bf16[2,768,256]{2,1,0:T(8,128)(2,1)} %wv_ref.3, ...), kind=kLoop, calls=%fused_computation.96 | loop fusion | bytes 2097152 | tf_op jit(solution)/shard_map/squeeze | solution.py:160
  4.2 2.7 %shard_map.158 = bf16[16,7,16,128]{3,2,1,0:T(8,128)(2,1)} custom-call(bf16[256,128]{1,0:T(8,128)(2,1)} %refs_0_.3, bf16[3,256,128]{2,1,0:T(8,128)(2,1)} %refs_1_.3, bf16[256,256]{1,0:T(8,128)(2,1)} %get-tuple-element.130.refs_2_, bf16[256,256]{1,0:T(8,128)(2,1)} %get-tuple-element.131.refs_3_, bf16[256,256]{1,0:T(8,128)(2,1)} %get-tuple-element.91.refs_4_, ...), custom_call_target="tpu_custom_call" | custom-call | tf_op jit(solution)/shard_map/pallas_call | solution.py:241
  6.9 7.4 %all-to-all-start = ((bf16[16,7,16,128]{3,2,1,0:T(8,128)(2,1)}), bf16[16,7,16,128]{3,2,1,0:T(8,128)(2,1)S(1)}, u32[]{:S(2)}, u32[]{:S(2)}) async-start(bf16[16,7,16,128]{3,2,1,0:T(8,128)(2,1)} %shard_map.158), calls=%async_computation | async-start | bytes 917504 | tf_op jit(solution)/shard_map/all_to_all | solution.py:335
  14.5 0.3 negate_convert_fusion
  14.9 0.3 fusion.97
  15.3 2.3 %convolution_sine_fusion.3 = f32[64,2048]{1,0:T(8,128)S(1)} fusion(f32[64,16]{0,1:T(8,128)S(1)} %get-tuple-element.48, f32[8,2048]{1,0:T(8,128)S(1)} %get-tuple-element.129, f32[8,2048]{1,0:T(8,128)S(1)} %get-tuple-element.128), kind=kOutput, calls=%fused_computation.3 | convolution fusion | flops 25198592 | bytes 659456 | tf_op jit(solution)/shard_map/dot_general | solution.py:21
  17.6 2.4 %convolution_sine_fusion.2 = f32[64,2048]{1,0:T(8,128)S(1)} fusion(f32[64,64]{1,0:T(8,128)S(1)} %get-tuple-element.47, f32[64,2048]{1,0:T(8,128)S(1)} %convolution_sine_fusion.3), kind=kOutput, calls=%fused_computation.2 | convolution fusion | flops 100663296 | bytes 1064960 | tf_op jit(solution)/shard_map/dot_general | solution.py:22
  20.0 0.5 fusion.5
  20.5 0.2 fusion.82
  20.8 0.3 fusion.100
  21.1 2.5 %shard_map.159.refs_3_ = bf16[4,256,128]{2,1,0:T(8,128)(2,1)} custom-call(bf16[256,128]{1,0:T(8,128)(2,1)} %refs_0_.3, bf16[3,256,128]{2,1,0:T(8,128)(2,1)} %refs_1_.3, bf16[2,768,256]{2,1,0:T(8,128)(2,1)} %ws_ref.3, bf16[2,768,256]{2,1,0:T(8,128)(2,1)} %wv_ref.3, f32[2,4,256]{2,1,0:T(4,128)} %g_ref.3), custom_call_target="tpu_custom_call" | custom-call | tf_op jit(solution)/shard_map/pallas_call | solution.py:270
  23.6 0.2 fusion.63
  23.9 0.8 slice_bitcast_fusion.6
  24.7 1.1 %slice_bitcast_fusion.1 = (bf16[1024,256]{1,0:T(8,128)(2,1)}, bf16[1024,256]{1,0:T(8,128)(2,1)}) fusion(bf16[2,1024,256]{2,1,0:T(8,128)(2,1)S(1)} %copy-done), kind=kLoop, calls=%fused_computation.15 | loop fusion | bytes 2097152 | tf_op jit(solution)/shard_map/squeeze | solution.py:155
  25.7 1.8 %all-to-all-done = bf16[16,7,16,128]{3,2,1,0:T(8,128)(2,1)S(1)} async-done(((bf16[16,7,16,128]{3,2,1,0:T(8,128)(2,1)}), bf16[16,7,16,128]{3,2,1,0:T(8,128)(2,1)S(1)}, u32[]{:S(2)}, u32[]{:S(2)}) %all-to-all-start) | async-done | bytes 458784 | tf_op jit(solution)/shard_map/all_to_all | solution.py:335
  27.6 0.4 fusion.17
  28.0 0.1 fusion.138
  28.1 0.2 copy.48
  28.3 0.2 copy.47
  28.5 0.2 add_convert_fusion.1
  28.7 0.3 fusion.6
  29.2 0.2 fusion.24
  29.6 0.4 fusion.22
  30.0 0.8 copy.87
  30.8 4.2 %all-to-all-start.1 = ((bf16[16,4,16,128]{3,2,1,0:T(8,128)(2,1)}), bf16[16,4,16,128]{3,2,1,0:T(8,128)(2,1)S(1)}, u32[]{:S(2)}, u32[]{:S(2)}) async-start(bf16[16,4,16,128]{3,2,1,0:T(8,128)(2,1)} %copy.87), calls=%async_computation.1 | async-start | bytes 524288 | tf_op jit(solution)/shard_map/all_to_all | solution.py:338
  35.0 0.8 slice_bitcast_fusion.4
  35.8 1.0 %slice_bitcast_fusion = (bf16[256,1024]{1,0:T(8,128)(2,1)}, bf16[256,1024]{1,0:T(8,128)(2,1)}) fusion(bf16[2,256,1024]{2,1,0:T(8,128)(2,1)S(1)} %copy-done.1), kind=kLoop, calls=%fused_computation.14 | loop fusion | bytes 2097152 | tf_op jit(solution)/shard_map/squeeze | solution.py:155
  36.9 8.1 %all-to-all-done.1.refs_2_ = bf16[16,4,16,128]{3,2,1,0:T(8,128)(2,1)S(1)} async-done(((bf16[16,4,16,128]{3,2,1,0:T(8,128)(2,1)}), bf16[16,4,16,128]{3,2,1,0:T(8,128)(2,1)S(1)}, u32[]{:S(2)}, u32[]{:S(2)}) %all-to-all-start.1) | async-done | bytes 262176 | tf_op jit(solution)/shard_map/all_to_all | solution.py:338
  45.0 0.7 copy-done.2
  45.7 4.1 %shard_map.160 = (bf16[16,7,16,128]{3,2,1,0:T(8,128)(2,1)}, f32[256,128]{1,0:T(8,128)}, f32[3,256,128]{2,1,0:T(8,128)}) custom-call(bf16[256,128]{1,0:T(8,128)(2,1)} %refs_0_.3, bf16[3,256,128]{2,1,0:T(8,128)(2,1)} %refs_1_.3, bf16[16,4,16,128]{3,2,1,0:T(8,128)(2,1)} %copy-done.2, bf16[4,256,128]{2,1,0:T(8,128)(2,1)} %shard_map.159.refs_3_, ...), custom_call_target="tpu_custom_call" | custom-call | tf_op jit(solution)/shard_map/pallas_call | solution.py:241
  49.7 3.7 %all-to-all-start.2 = ((bf16[16,7,16,128]{3,2,1,0:T(8,128)(2,1)}), bf16[16,7,16,128]{3,2,1,0:T(8,128)(2,1)S(1)}, u32[]{:S(2)}, u32[]{:S(2)}) async-start(bf16[16,7,16,128]{3,2,1,0:T(8,128)(2,1)} %get-tuple-element.53), calls=%async_computation.2 | async-start | bytes 917504 | tf_op jit(solution)/shard_map/all_to_all | solution.py:335
  53.6 2.3 %convolution_sine_fusion.1 = f32[64,2048]{1,0:T(8,128)S(1)} fusion(f32[64,16]{0,1:T(8,128)S(1)} %get-tuple-element.57, f32[8,2048]{1,0:T(8,128)S(1)} %get-tuple-element.129, f32[8,2048]{1,0:T(8,128)S(1)} %get-tuple-element.128), kind=kOutput, calls=%fused_computation.1 | convolution fusion | flops 25198592 | bytes 659456 | tf_op jit(solution)/shard_map/dot_general | solution.py:21
  55.8 2.4 %convolution_sine_fusion = f32[64,2048]{1,0:T(8,128)S(1)} fusion(f32[64,64]{1,0:T(8,128)S(1)} %get-tuple-element.56, f32[64,2048]{1,0:T(8,128)S(1)} %convolution_sine_fusion.1), kind=kOutput, calls=%fused_computation | convolution fusion | flops 100663296 | bytes 1064960 | tf_op jit(solution)/shard_map/dot_general | solution.py:22
  58.3 0.5 fusion.4
  58.8 0.2 fusion.79
  59.0 2.4 %shard_map.161.refs_3_ = bf16[4,256,128]{2,1,0:T(8,128)(2,1)} custom-call(f32[256,128]{1,0:T(8,128)} %get-tuple-element.51.ss_ref.refs_0_, f32[3,256,128]{2,1,0:T(8,128)} %get-tuple-element.52.sv_ref.refs_1_, bf16[2,768,256]{2,1,0:T(8,128)(2,1)} %ws_ref.3, bf16[2,768,256]{2,1,0:T(8,128)(2,1)} %wv_ref.3, f32[2,4,256]{2,1,0:T(4,128)} %g_ref.3), custom_call_target="tpu_custom_call" | custom-call | tf_op jit(solution)/shard_map/pallas_call | solution.py:270
  61.5 0.2 fusion.61
  61.7 4.9 %all-to-all-done.2 = bf16[16,7,16,128]{3,2,1,0:T(8,128)(2,1)S(1)} async-done(((bf16[16,7,16,128]{3,2,1,0:T(8,128)(2,1)}), bf16[16,7,16,128]{3,2,1,0:T(8,128)(2,1)S(1)}, u32[]{:S(2)}, u32[]{:S(2)}) %all-to-all-start.2) | async-done | bytes 458784 | tf_op jit(solution)/shard_map/all_to_all | solution.py:335
  66.5 0.4 fusion.14
  67.0 0.2 copy.56
  67.2 0.2 copy.55
  67.5 0.2 add_convert_fusion
  67.6 0.3 fusion.10
  68.2 0.2 fusion.40
  68.5 0.4 fusion.20
  69.0 13.8 %all_to_all.20.refs_2_ = bf16[16,4,16,128]{3,2,1,0:T(8,128)(2,1)} all-to-all(bf16[16,4,16,128]{3,2,1,0:T(8,128)(2,1)S(1)} %copy.86), channel_id=1, replica_groups=mesh['grp'=2,'seq'=16] {'seq'}, dimensions={0} | all-to-all | bytes 524288 | tf_op jit(solution)/shard_map/all_to_all | solution.py:338
  82.7 3.4 %shard_map.162 = (bf16[256,128]{1,0:T(8,128)(2,1)}, bf16[3,256,128]{2,1,0:T(8,128)(2,1)}) custom-call(f32[256,128]{1,0:T(8,128)} %get-tuple-element.51.ss_ref.refs_0_, f32[3,256,128]{2,1,0:T(8,128)} %get-tuple-element.52.sv_ref.refs_1_, bf16[16,4,16,128]{3,2,1,0:T(8,128)(2,1)} %all_to_all.20.refs_2_, bf16[4,256,128]{2,1,0:T(8,128)(2,1)} %shard_map.161.refs_3_, ...), custom_call_target="tpu_custom_call" | custom-call | tf_op jit(solution)/shard_map/pallas_call | solution.py:241
  (62 shorter events, 1.7 us)
Async XLA Ops:
  4.2 10.6 %copy-start.10 = (f32[2,256]{1,0:T(2,128)S(1)}, f32[2,256]{1,0:T(2,128)}, u32[]{:S(2)}) copy-start(f32[2,256]{1,0:T(2,128)} %param.33) | copy-start | bytes 6148
  4.2 10.6 %copy-start.9 = (f32[2,64,16]{1,2,0:T(8,128)S(1)}, f32[2,64,16]{1,2,0:T(8,128)}, u32[]{:S(2)}) copy-start(f32[2,64,16]{1,2,0:T(8,128)} %param.30) | copy-start | bytes 24580
  4.2 10.6 %copy-start.8 = (f32[2,64,64]{2,1,0:T(8,128)S(1)}, f32[2,64,64]{2,1,0:T(8,128)}, u32[]{:S(2)}) copy-start(f32[2,64,64]{2,1,0:T(8,128)} %param.31) | copy-start | bytes 98308
  4.2 11.0 %copy-start.7 = (f32[2,256,64]{1,2,0:T(8,128)S(1)}, f32[2,256,64]{1,2,0:T(8,128)}, u32[]{:S(2)}) copy-start(f32[2,256,64]{1,2,0:T(8,128)} %param.32) | copy-start | bytes 393220
  6.9 20.6 %all-to-all-start = ((bf16[16,7,16,128]{3,2,1,0:T(8,128)(2,1)}), bf16[16,7,16,128]{3,2,1,0:T(8,128)(2,1)S(1)}, u32[]{:S(2)}, u32[]{:S(2)}) async-start(bf16[16,7,16,128]{3,2,1,0:T(8,128)(2,1)} %shard_map.158), calls=%async_computation | async-start | bytes 917504 | tf_op jit(solution)/shard_map/all_to_all | solution.py:335
  20.8 3.0 %copy-start.11 = (f32[9]{0:T(128)S(1)}, f32[9]{0:T(128)}, u32[]{:S(2)}) copy-start(f32[9]{0:T(128)} %constant.125.clone.1) | copy-start | bytes 112
  20.8 3.0 %copy-start.3 = (bf16[2,256,256]{2,1,0:T(8,128)(2,1)S(1)}, bf16[2,256,256]{2,1,0:T(8,128)(2,1)}, u32[]{:S(2)}) copy-start(bf16[2,256,256]{2,1,0:T(8,128)(2,1)} %param.24) | copy-start | bytes 786436
  20.8 3.0 %copy-start.4 = (bf16[2,256,256]{2,1,0:T(8,128)(2,1)S(1)}, bf16[2,256,256]{2,1,0:T(8,128)(2,1)}, u32[]{:S(2)}) copy-start(bf16[2,256,256]{2,1,0:T(8,128)(2,1)} %param.23) | copy-start | bytes 786436
  21.1 3.6 %copy-start = (bf16[2,1024,256]{2,1,0:T(8,128)(2,1)S(1)}, bf16[2,1024,256]{2,1,0:T(8,128)(2,1)}, u32[]{:S(2)}) copy-start(bf16[2,1024,256]{2,1,0:T(8,128)(2,1)} %param.25) | copy-start | bytes 3145732
  29.6 5.4 %copy-start.5 = (bf16[2,256,256]{2,1,0:T(8,128)(2,1)S(1)}, bf16[2,256,256]{2,1,0:T(8,128)(2,1)}, u32[]{:S(2)}) copy-start(bf16[2,256,256]{2,1,0:T(8,128)(2,1)} %param.28) | copy-start | bytes 786436
  29.6 5.4 %copy-start.6 = (bf16[2,256,256]{2,1,0:T(8,128)(2,1)S(1)}, bf16[2,256,256]{2,1,0:T(8,128)(2,1)}, u32[]{:S(2)}) copy-start(bf16[2,256,256]{2,1,0:T(8,128)(2,1)} %param.27) | copy-start | bytes 786436
  29.6 6.2 %copy-start.1 = (bf16[2,256,1024]{2,1,0:T(8,128)(2,1)S(1)}, bf16[2,256,1024]{2,1,0:T(8,128)(2,1)}, u32[]{:S(2)}) copy-start(bf16[2,256,1024]{2,1,0:T(8,128)(2,1)} %param.26) | copy-start | bytes 3145732
  30.8 14.2 %all-to-all-start.1 = ((bf16[16,4,16,128]{3,2,1,0:T(8,128)(2,1)}), bf16[16,4,16,128]{3,2,1,0:T(8,128)(2,1)S(1)}, u32[]{:S(2)}, u32[]{:S(2)}) async-start(bf16[16,4,16,128]{3,2,1,0:T(8,128)(2,1)} %copy.87), calls=%async_computation.1 | async-start | bytes 524288 | tf_op jit(solution)/shard_map/all_to_all | solution.py:338
  45.0 0.7 copy-start.2
  49.7 16.8 %all-to-all-start.2 = ((bf16[16,7,16,128]{3,2,1,0:T(8,128)(2,1)}), bf16[16,7,16,128]{3,2,1,0:T(8,128)(2,1)S(1)}, u32[]{:S(2)}, u32[]{:S(2)}) async-start(bf16[16,7,16,128]{3,2,1,0:T(8,128)(2,1)} %get-tuple-element.53), calls=%async_computation.2 | async-start | bytes 917504 | tf_op jit(solution)/shard_map/all_to_all | solution.py:335
